TPU v7x, 256 devices: a whole 4x4x8 slice. The times are simulated.
256 devices in a mesh: tile: 64 (over y, z, core), sub: 4 (over x).
Axes of the slice: x: 4, y: 4, z: 8, core: 2. Of those that a mesh axis runs over, the one named last changes fastest.
Arguments:
- atm_fields: float32 [6, 2048, 128], P(None, ('tile', 'sub')), may hold values from -6 to 6
- pair_atm: int32 [5120], P(('tile', 'sub')), may hold values from 0 to 7
- pair_land: int32 [5120], P(('tile', 'sub')), may hold values from 0 to 4095, as said below
- pair_weight: bfloat16 [5120, 3, 128, 512], P(('tile', 'sub')), may hold values from -0.3125 to 0.3125
- land_mask: int32 [2097152], P(('tile', 'sub')), may hold values 0 or 1
- conductance: float32 [20, 2097152], P(None, ('tile', 'sub')), may hold values from 0.1 to 3
- soil_moisture: float32 [20, 2097152], P(None, ('tile', 'sub')), may hold values from 0.1 to 0.5
- river_owner: int32 [16384], P(('tile', 'sub')), may hold values from 0 to 63, as said below
Outputs:
- land_forcing: bfloat16 [6, 2097152], P(None, ('tile', 'sub'))
- soil_state: float32 [20, 2097152], P(None, ('tile', 'sub'))
- river_runoff: float32 [64, 4, 64, 2, 128], P('tile', 'sub')
- river_blocks: int32 [64, 4, 64, 2], P('tile', 'sub')
Inputs may be any that keep to these rules, and one draw needn't show every extreme that they name: `pair_land`: the land block of a pair lies in the tile of the pair's atmosphere device or in one of the two tiles beside it, cyclically over the 64 tiles (device d = t * 4 + s owns land blocks d * 16 onward). At most 4 pairs of one device name land blocks of one device, and in every tile some land device receives exactly 4 pairs from each of the tile's 4 devices. `river_owner`: A block goes to the river owner device on the given tile with the same sub index. At most 2 blocks of one device go to one owner, and for every sub index some owner receives exactly 2 blocks from each device of that sub index.
All inputs are finite; a program needn't handle non-finite values. No bound on the sum of `land_mask` on one device may be relied on, other than what follows from the above.
Results may differ from a plain program's by a relative error of at most 0.0049.
Values sent between devices are 32-bit elements; how exact they have to be, the bound alone decides.
No kernel may reach another device: no remote copies, remote signals or barrier semaphores. Data moves between devices by JAX's collectives and lax.ppermute only.
A program may use at most 64 MiB of HBM per device.

v0:
```python
import jax
import jax.numpy as jnp
from jax import lax
from jax.sharding import PartitionSpec as P

SOIL_STEPS = 4
LBLK = 512
RBLK = 128
LB_DEV = 16


def passed_along(block, axis, distance):
    devices = range(lax.axis_size(axis))
    route = [((i - distance) % len(devices), i) for i in devices]
    return lax.ppermute(block, axis, route)


def padded(array, sides, width):
    for axis, dim in sides:
        devices, length = (lax.axis_size(axis), array.shape[dim])
        up = [(i, (i + 1) % devices) for i in range(devices)]
        down = [(j, i) for i, j in up]
        last = lax.slice_in_dim(array, length - width, length, axis=dim)
        initial = lax.slice_in_dim(array, 0, width, axis=dim)
        before = lax.ppermute(last, axis, up)
        after = lax.ppermute(initial, axis, down)
        array = jnp.concatenate([before, array, after], axis=dim)
    return array


def x_gradient(fields):
    inner = (fields[:, :, 2:] - fields[:, :, :-2]) * 0.5
    first = fields[:, :, 1:2] - fields[:, :, 0:1]
    last = fields[:, :, -1:] - fields[:, :, -2:-1]
    return jnp.concatenate([first, inner, last], axis=2)


def column_factors(conductance):
    layers = conductance.shape[0]
    inverse = []
    ratios = []
    for k in range(layers):
        diagonal = 1.0 + conductance[k]
        if k > 0:
            diagonal = (
                diagonal
                + conductance[k - 1]
                - conductance[k - 1] * conductance[k - 1] * inverse[k - 1]
            )
        pivot_inv = 1.0 / diagonal
        inverse.append(pivot_inv)
        ratios.append(-conductance[k] * pivot_inv)
    return (inverse, ratios)


def column_solve(moisture, source, conductance, inverse, ratios):
    layers = len(inverse)
    forward = []
    for k in range(layers):
        if k == 0:
            column_value = moisture[0] + source
        else:
            column_value = moisture[k] + conductance[k - 1] * forward[k - 1]
        forward.append(column_value * inverse[k])
    solved = [forward[layers - 1]]
    for k in range(layers - 2, -1, -1):
        solved.insert(0, forward[k] - ratios[k] * solved[0])
    return jnp.stack(solved)


def soil_update(forcing, land_mask, conductance, soil_moisture):
    wetness = land_mask.astype(jnp.float32)
    source = wetness * (
        jax.nn.softplus(forcing[0]) * jax.nn.sigmoid(forcing[1])
        - 0.5 * jax.nn.sigmoid(forcing[2]) * jax.nn.softplus(forcing[3])
    )
    surface = wetness * jax.nn.softplus(forcing[0]) * (1.0 - jax.nn.sigmoid(forcing[1]))
    inverse, ratios = column_factors(conductance)
    bottom = conductance.shape[0] - 1
    moisture = soil_moisture
    drainage = jnp.zeros_like(surface)
    for substep in range(SOIL_STEPS):
        moisture = column_solve(moisture, source, conductance, inverse, ratios)
        drainage = drainage + conductance[bottom] * moisture[bottom]
    runoff = wetness * (SOIL_STEPS * surface + drainage)
    return (moisture, runoff)


def beside_tiles(lower_piece, upper_piece):
    from_below = passed_along(upper_piece, "tile", 1)
    from_above = passed_along(lower_piece, "tile", -1)
    return from_below + from_above


def onehot_sum(group_id, count, flat_terms):
    selector = (group_id[None, :] == jnp.arange(count, dtype=jnp.int32)[:, None]).astype(
        jnp.float32
    )
    return jnp.dot(selector, flat_terms, precision=lax.Precision.HIGHEST)


def on_device(
    atm_fields, pair_atm, pair_land, pair_weight, land_mask, conductance, soil_moisture, river_owner
):
    tile_count = lax.axis_size("tile")
    sub_count = lax.axis_size("sub")
    tile_index = lax.axis_index("tile")
    sub_index = lax.axis_index("sub")
    field_count, row_count, row_width = atm_fields.shape
    extended = padded(atm_fields, ((("tile", "sub"), 1),), 1)
    grad_x = x_gradient(atm_fields)
    grad_y = (extended[:, 2:, :] - extended[:, :-2, :]) * 0.5
    stacked = jnp.concatenate([atm_fields, grad_x, grad_y], axis=2).astype(jnp.bfloat16)
    pair_count = pair_atm.shape[0]
    picked = stacked[:, pair_atm, :]
    weights = pair_weight.reshape(pair_count, 3 * row_width, LBLK)
    partial_value = jnp.einsum("fpk,pkl->pfl", picked, weights, preferred_element_type=jnp.float32)
    flat_terms = partial_value.reshape(pair_count, field_count * LBLK)
    owner_device = pair_land // LB_DEV
    dest_tile = owner_device // sub_count
    dest_sub = owner_device % sub_count
    local_block = pair_land % LB_DEV
    offset = (dest_tile - tile_index + 1 + tile_count) % tile_count
    tile_blocks = sub_count * LB_DEV
    group_id = offset * tile_blocks + dest_sub * LB_DEV + local_block
    dense_sums = onehot_sum(group_id, 3 * tile_blocks, flat_terms).reshape(
        3, tile_blocks, field_count, LBLK
    )
    total_sums = dense_sums[1] + beside_tiles(dense_sums[0], dense_sums[2])
    owned_sums = lax.psum_scatter(total_sums, "sub", scatter_dimension=0, tiled=True)
    forcing = owned_sums.transpose(1, 0, 2).reshape(field_count, LB_DEV * LBLK)
    land_forcing = forcing.astype(jnp.bfloat16)
    moisture, runoff = soil_update(forcing, land_mask, conductance, soil_moisture)
    block_count = runoff.shape[0] // RBLK
    capacity = max(2, 2 * block_count // tile_count)
    runoff_blocks = runoff.reshape(block_count, RBLK)
    hits = (river_owner[:, None] == jnp.arange(tile_count, dtype=jnp.int32)[None, :]).astype(
        jnp.int32
    )
    ranks = jnp.sum((jnp.cumsum(hits, axis=0) - hits) * hits, axis=1)
    slot_id = river_owner * capacity + ranks
    placing = slot_id[None, :] == jnp.arange(tile_count * capacity, dtype=jnp.int32)[:, None]
    values = jnp.dot(placing.astype(jnp.float32), runoff_blocks, precision=lax.Precision.HIGHEST)
    values = values.reshape(tile_count, capacity, RBLK)
    block_ids = (tile_index * sub_count + sub_index) * block_count + jnp.arange(
        block_count, dtype=jnp.int32
    )
    numbers = jnp.sum(jnp.where(placing, block_ids[None, :] + 1, 0), axis=1) - 1
    numbers = numbers.astype(jnp.float32).reshape(tile_count, capacity)
    got_values, got_numbers = (
        lax.all_to_all(values, "tile", split_axis=0, concat_axis=0, tiled=True),
        lax.all_to_all(numbers, "tile", split_axis=0, concat_axis=0, tiled=True),
    )
    river_runoff = got_values[None, None]
    river_blocks = got_numbers.astype(jnp.int32)[None, None]
    return (land_forcing, moisture, river_runoff, river_blocks)


def solution(mesh):
    return jax.shard_map(
        on_device,
        mesh=mesh,
        in_specs=(
            P(None, ("tile", "sub"), None),
            P(("tile", "sub")),
            P(("tile", "sub")),
            P(("tile", "sub"), None, None, None),
            P(("tile", "sub")),
            P(None, ("tile", "sub")),
            P(None, ("tile", "sub")),
            P(("tile", "sub")),
        ),
        out_specs=(
            P(None, ("tile", "sub")),
            P(None, ("tile", "sub")),
            P("tile", "sub", None, None, None),
            P("tile", "sub", None, None),
        ),
        check_vma=False,
    )
```

profile of v0, /device:TPU:1, one launch (start us, length us, event | category | flops | bytes accessed | tf_op | source)
XLA Modules:
  0.0 113.2 jit_solution(18173431361019818082)
XLA Ops:
  7.2 0.8 fusion.53
  8.0 3.9 %collective-permute-start = (f32[6,1,128]{2,1,0:T(1,128)S(1)}, f32[6,1,128]{2,1,0:T(1,128)S(1)}, u32[]{:S(2)}, u32[]{:S(2)}) collective-permute-start(f32[6,1,128]{2,1,0:T(1,128)S(1)} %get-tuple-element.114), channel_id=1, source_target_pairs={{1,0},{2,1},{3,2},{4,3},{5,4},{6,5},{7,6},{8,7},{9,8},{10,9},{11,1... | collective-permute-start | bytes 9224 | tf_op jit(solution)/shard_map/ppermute | solution.py:26
  11.9 0.7 fusion.30
  12.6 0.1 reduce_window_sum.11
  12.7 0.8 select_reduce_fusion.1
  13.5 0.7 add_add_fusion
  14.2 0.1 select_reduce_fusion
  14.3 0.8 convert_element_type.47
  15.1 11.8 %all-to-all-start.1 = ((f32[64,1,2]{2,1,0:T(1,128)}), f32[64,1,2]{2,1,0:T(1,128)S(1)}, u32[]{:S(2)}, u32[]{:S(2)}) async-start(f32[64,1,2]{2,1,0:T(1,128)} %bitcast.66), calls=%async_computation.2 | async-start | bytes 65536 | tf_op jit(solution)/shard_map/all_to_all | solution.py:152
  26.8 0.0 reduce-scatter.2.cloned.1.call-start
  26.9 1.0 subtract_convert_fusion
  27.9 0.9 multiply_convert_fusion
  28.7 0.7 compare_select_fusion.3
  29.4 0.7 fusion.41
  30.1 0.9 fusion.37
  31.0 0.1 concatenate.13
  31.1 0.6 gather_fusion
  31.7 4.3 %fusion = f32[20,6,512]{2,1,0:T(8,128)S(1)} fusion(bf16[20,384,512]{2,1,0:T(8,128)(2,1)} %bitcast.106, bf16[20,6,384]{2,1,0:T(8,128)(2,1)S(1)} %gather_fusion), kind=kOutput, calls=%fused_computation.4 | convolution fusion | flops 47185920 | bytes 8202240 | tf_op jit(solution)/shard_map/fpk,pkl->pfl/dot_general | solution.py:117
  36.1 0.2 copy.74
  36.3 0.0 copy-start.1
  36.3 1.1 fusion.2
  37.4 0.2 fusion.50
  37.6 0.1 copy.84
  37.7 1.7 %collective-permute-start.2 = (f32[64,6,512]{2,0,1:T(8,128)S(1)}, f32[64,6,512]{2,0,1:T(8,128)S(1)}, u32[]{:S(2)}, u32[]{:S(2)}) collective-permute-start(f32[64,6,512]{2,0,1:T(8,128)S(1)} %bitcast.304), channel_id=1, source_target_pairs={{252,0},{0,4},{4,8},{8,12},{12,16},{16,20},{20,24},{24,28},{28,32}... | collective-permute-start | bytes 2359304 | tf_op jit(solution)/shard_map/ppermute | solution.py:15
  39.4 0.1 copy.83
  39.5 0.1 collective-permute-start.3
  39.6 0.5 fusion.51
  40.1 8.2 %collective-permute-done.2 = f32[64,6,512]{2,0,1:T(8,128)S(1)} collective-permute-done((f32[64,6,512]{2,0,1:T(8,128)S(1)}, f32[64,6,512]{2,0,1:T(8,128)S(1)}, u32[]{:S(2)}, u32[]{:S(2)}) %collective-permute-start.2) | collective-permute-done | bytes 786464 | tf_op jit(solution)/shard_map/ppermute | solution.py:15
  48.3 2.9 %collective-permute-done.3 = f32[64,6,512]{2,0,1:T(8,128)S(1)} collective-permute-done((f32[64,6,512]{2,0,1:T(8,128)S(1)}, f32[64,6,512]{2,0,1:T(8,128)S(1)}, u32[]{:S(2)}, u32[]{:S(2)}) %collective-permute-start.3) | collective-permute-done | bytes 786464 | tf_op jit(solution)/shard_map/ppermute | solution.py:15
  51.3 1.1 bitcast_add_fusion
  52.4 0.0 reduce-scatter.2.cloned.1.call-update
  52.4 0.5 fusion.52
  53.1 0.1 copy.70
  53.1 0.6 convert_bitcast_fusion.1
  53.7 25.7 %reduce-scatter.2.cloned.1.call-done = f32[16,6,512]{2,0,1:T(8,128)} async-done(((f32[64,6,512]{2,0,1:T(8,128)}), f32[16,6,512]{2,0,1:T(8,128)}) %reduce-scatter.2.cloned.1.call-update) | async-done | bytes 196624 | tf_op jit(solution)/shard_map/reduce_scatter | solution.py:130
  79.4 0.9 slice_bitcast_fusion.1
  80.3 0.3 add_multiply_fusion.63
  80.7 0.7 multiply_subtract_fusion.34
  81.4 0.8 add_multiply_fusion.1
  82.1 0.6 multiply_subtract_fusion.2
  82.8 0.7 fusion.3
  83.5 0.7 copy.68
  84.1 11.7 %all-to-all-start = ((f32[64,2,128]{2,1,0:T(2,128)}), f32[64,2,128]{2,1,0:T(2,128)S(1)}, u32[]{:S(2)}, u32[]{:S(2)}) async-start(f32[64,2,128]{2,1,0:T(2,128)} %copy.68), calls=%async_computation.1 | async-start | bytes 131072 | tf_op jit(solution)/shard_map/all_to_all | solution.py:151
  95.9 0.7 copy.75
  96.6 0.1 multiply_subtract_fusion
  96.7 3.0 %stack.83 = f32[20,8192]{1,0:T(8,128)} concatenate(f32[1,8192]{1,0:T(1,128)S(1)} %bitcast.334, f32[1,8192]{1,0:T(1,128)S(1)} %bitcast.335, f32[1,8192]{1,0:T(1,128)S(1)} %bitcast.317, f32[1,8192]{1,0:T(1,128)S(1)} %bitcast.315, f32[1,8192]{1,0:T(1,128)S(1)} %bitcast.318, f32[1,8192]{1,0:T(1,128)S(1)} %bitcast.319, f32[1,8192]{1,0:T(1,128)S(1)} %bitcast.320, ...), dimensions={0} | concatenate | bytes 1310720 | tf_op jit(solution)/shard_map/stack | solution.py:68
  99.7 6.0 %all-to-all-done = f32[64,2,128]{2,1,0:T(2,128)S(1)} async-done(((f32[64,2,128]{2,1,0:T(2,128)}), f32[64,2,128]{2,1,0:T(2,128)S(1)}, u32[]{:S(2)}, u32[]{:S(2)}) %all-to-all-start) | async-done | bytes 65568 | tf_op jit(solution)/shard_map/all_to_all | solution.py:151
  105.7 0.6 copy.86
  (23 shorter events, 0.2 us)
Async XLA Ops:
  8.0 22.1 %collective-permute-start = (f32[6,1,128]{2,1,0:T(1,128)S(1)}, f32[6,1,128]{2,1,0:T(1,128)S(1)}, u32[]{:S(2)}, u32[]{:S(2)}) collective-permute-start(f32[6,1,128]{2,1,0:T(1,128)S(1)} %get-tuple-element.114), channel_id=1, source_target_pairs={{1,0},{2,1},{3,2},{4,3},{5,4},{6,5},{7,6},{8,7},{9,8},{10,9},{11,1... | collective-permute-start | bytes 9224 | tf_op jit(solution)/shard_map/ppermute | solution.py:26
  11.9 18.3 %collective-permute-start.1 = (f32[6,1,128]{2,1,0:T(1,128)S(1)}, f32[6,1,128]{2,1,0:T(1,128)S(1)}, u32[]{:S(2)}, u32[]{:S(2)}) collective-permute-start(f32[6,1,128]{2,1,0:T(1,128)S(1)} %get-tuple-element.115), channel_id=1, source_target_pairs={{0,1},{1,2},{2,3},{3,4},{4,5},{5,6},{6,7},{7,8},{8,9},{9,10},{10,1... | collective-permute-start | bytes 9224 | tf_op jit(solution)/shard_map/ppermute | solution.py:25
  15.1 38.0 %all-to-all-start.1 = ((f32[64,1,2]{2,1,0:T(1,128)}), f32[64,1,2]{2,1,0:T(1,128)S(1)}, u32[]{:S(2)}, u32[]{:S(2)}) async-start(f32[64,1,2]{2,1,0:T(1,128)} %bitcast.66), calls=%async_computation.2 | async-start | bytes 65536 | tf_op jit(solution)/shard_map/all_to_all | solution.py:152
  26.8 52.6 %reduce-scatter.2.cloned.1.call-start = ((), (), s32[]{:S(2)}) async-start(), calls=%async_computation.3 | async-start | bytes 983040 | tf_op jit(solution)/shard_map/reduce_scatter | solution.py:130
  36.0 3.5 %copy-start = (f32[20,8192]{1,0:T(8,128)S(1)}, f32[20,8192]{1,0:T(8,128)}, u32[]{:S(2)}) copy-start(f32[20,8192]{1,0:T(8,128)} %param.13) | copy-start | bytes 1966084
  36.3 16.1 %copy-start.1 = (f32[20,8192]{1,0:T(8,128)S(1)}, f32[20,8192]{1,0:T(8,128)}, u32[]{:S(2)}) copy-start(f32[20,8192]{1,0:T(8,128)} %param.14) | copy-start | bytes 1966084
  37.4 43.0 %copy-start.3 = (s32[8192]{0:T(1024)S(1)}, s32[8192]{0:T(1024)}, u32[]{:S(2)}) copy-start(s32[8192]{0:T(1024)} %param.12) | copy-start | bytes 98308
  37.7 10.6 %collective-permute-start.2 = (f32[64,6,512]{2,0,1:T(8,128)S(1)}, f32[64,6,512]{2,0,1:T(8,128)S(1)}, u32[]{:S(2)}, u32[]{:S(2)}) collective-permute-start(f32[64,6,512]{2,0,1:T(8,128)S(1)} %bitcast.304), channel_id=1, source_target_pairs={{252,0},{0,4},{4,8},{8,12},{12,16},{16,20},{20,24},{24,28},{28,32}... | collective-permute-start | bytes 2359304 | tf_op jit(solution)/shard_map/ppermute | solution.py:15
  39.5 11.8 %collective-permute-start.3 = (f32[64,6,512]{2,0,1:T(8,128)S(1)}, f32[64,6,512]{2,0,1:T(8,128)S(1)}, u32[]{:S(2)}, u32[]{:S(2)}) collective-permute-start(f32[64,6,512]{2,0,1:T(8,128)S(1)} %bitcast.305), channel_id=1, source_target_pairs={{4,0},{8,4},{12,8},{16,12},{20,16},{24,20},{28,24},{32,28},{36,32}... | collective-permute-start | bytes 2359304 | tf_op jit(solution)/shard_map/ppermute | solution.py:15
  79.4 16.5 %copy-start.2 = (f32[16,6,512]{2,0,1:T(8,128)S(1)}, f32[16,6,512]{2,0,1:T(8,128)}, u32[]{:S(2)}) copy-start(f32[16,6,512]{2,0,1:T(8,128)} %reduce-scatter.2.cloned.1.call-done) | copy-start | bytes 589828
  84.1 21.5 %all-to-all-start = ((f32[64,2,128]{2,1,0:T(2,128)}), f32[64,2,128]{2,1,0:T(2,128)S(1)}, u32[]{:S(2)}, u32[]{:S(2)}) async-start(f32[64,2,128]{2,1,0:T(2,128)} %copy.68), calls=%async_computation.1 | async-start | bytes 131072 | tf_op jit(solution)/shard_map/all_to_all | solution.py:151
Sparse Core Ops, SparseCore 0:
  52.5 26.8 reduce-scatter.1
where the time goes:
time: 114 us; the launch traced here: 113 us
  waiting for transfers between devices  42.8 us (38%)
  starting transfers between devices  29.2 us (26%)
  between operations  14.3 us (13%)
  other arithmetic  11.6 us (10%)
  local copies, waits for them, and re-layouts  9.17 us (8%)
  matrix products  6.09 us (5%)
    reduce_scatter x1, waiting for transfers between devices, on_device(): lax.psum_scatter(total_sums, 'sub', scatter_dimension=0, tiled=True)  25.7 us
    all_to_all x1, starting transfers between devices, on_device(): lax.all_to_all(numbers, 'tile', split_axis=0, concat_axis=0, tiled=True)  11.8 us
    all_to_all x1, starting transfers between devices, on_device(): lax.all_to_all(values, 'tile', split_axis=0, concat_axis=0, tiled=True)  11.7 us
    ppermute x2, waiting for transfers between devices, passed_along(): return lax.ppermute(block, axis, route)  11.1 us
    all_to_all x1, waiting for transfers between devices, on_device(): lax.all_to_all(values, 'tile', split_axis=0, concat_axis=0, tiled=True)  5.96 us
    dot_general x1, matrix products, on_device(): jnp.einsum('fpk,pkl->pfl', picked, weights, preferred_element_type=jnp.fl...  4.35 us
    ppermute x1, starting transfers between devices, padded(): after = lax.ppermute(initial, axis, down)  3.87 us
    another operation x1, local copies, waits for them, and re-layouts, column_solve(): return jnp.stack(solved)  3.03 us
  transfers between devices with their start and end apart: 7, of which 4 were waited for; matrix products, arithmetic and copies ran while one was open for 18% of the time, Pallas kernels for 0%

commit v1 on v0

--- a/solution.py
+++ b/solution.py
@@ -86,17 +86,48 @@
     return (moisture, runoff)
 
 
-def beside_tiles(lower_piece, upper_piece):
-    from_below = passed_along(upper_piece, "tile", 1)
-    from_above = passed_along(lower_piece, "tile", -1)
-    return from_below + from_above
-
-
-def onehot_sum(group_id, count, flat_terms):
-    selector = (group_id[None, :] == jnp.arange(count, dtype=jnp.int32)[:, None]).astype(
-        jnp.float32
-    )
-    return jnp.dot(selector, flat_terms, precision=lax.Precision.HIGHEST)
+CAP_P = 4
+CAP_R = 2
+
+
+def route_partials(flat_terms, pair_land, tile_count, sub_count, tile_index, sub_index):
+    pair_count, width = flat_terms.shape
+    owner_device = pair_land // LB_DEV
+    tile_step = (owner_device // sub_count - tile_index + 1 + tile_count) % tile_count
+    sub_step = (owner_device % sub_count - sub_index + sub_count) % sub_count
+    group_count = 3 * sub_count
+    group_id = tile_step * sub_count + sub_step
+    hits = (group_id[:, None] == jnp.arange(group_count, dtype=jnp.int32)[None, :]).astype(jnp.int32)
+    ranks = jnp.sum((jnp.cumsum(hits, axis=0) - hits) * hits, axis=1)
+    slot_id = group_id * CAP_P + ranks
+    slot_count = group_count * CAP_P
+    placing = slot_id[None, :] == jnp.arange(slot_count, dtype=jnp.int32)[:, None]
+    source = jnp.sum(jnp.where(placing, jnp.arange(pair_count, dtype=jnp.int32)[None, :] + 1, 0), axis=1) - 1
+    filled = source >= 0
+    picked = jnp.maximum(source, 0)
+    rows = jnp.where(filled[:, None], flat_terms[picked], 0.0)
+    ids = jnp.where(filled, pair_land[picked] % LB_DEV, -1).astype(jnp.float32)
+    ids = jnp.pad(ids.reshape(group_count, CAP_P), ((0, 0), (0, 128 - CAP_P)))
+    messages = jnp.concatenate([rows.reshape(group_count, CAP_P * width), ids], axis=1)
+    devices = tile_count * sub_count
+    received = []
+    for tile_offset in range(3):
+        for sub_offset in range(sub_count):
+            message = messages[tile_offset * sub_count + sub_offset]
+            if tile_offset == 1 and sub_offset == 0:
+                received.append(message)
+                continue
+            route = []
+            for d in range(devices):
+                t, s = divmod(d, sub_count)
+                target = ((t + tile_offset - 1) % tile_count) * sub_count + (s + sub_offset) % sub_count
+                route.append((d, target))
+            received.append(lax.ppermute(message, ("tile", "sub"), route))
+    got = jnp.stack(received)
+    data = got[:, : CAP_P * width].reshape(slot_count, width)
+    got_ids = got[:, CAP_P * width : CAP_P * width + CAP_P].reshape(slot_count)
+    selector = (got_ids[None, :] == jnp.arange(LB_DEV, dtype=jnp.float32)[:, None]).astype(jnp.float32)
+    return jnp.dot(selector, data, precision=lax.Precision.HIGHEST)
 
 
 def on_device(
@@ -116,23 +147,14 @@
     weights = pair_weight.reshape(pair_count, 3 * row_width, LBLK)
     partial_value = jnp.einsum("fpk,pkl->pfl", picked, weights, preferred_element_type=jnp.float32)
     flat_terms = partial_value.reshape(pair_count, field_count * LBLK)
-    owner_device = pair_land // LB_DEV
-    dest_tile = owner_device // sub_count
-    dest_sub = owner_device % sub_count
-    local_block = pair_land % LB_DEV
-    offset = (dest_tile - tile_index + 1 + tile_count) % tile_count
-    tile_blocks = sub_count * LB_DEV
-    group_id = offset * tile_blocks + dest_sub * LB_DEV + local_block
-    dense_sums = onehot_sum(group_id, 3 * tile_blocks, flat_terms).reshape(
-        3, tile_blocks, field_count, LBLK
-    )
-    total_sums = dense_sums[1] + beside_tiles(dense_sums[0], dense_sums[2])
-    owned_sums = lax.psum_scatter(total_sums, "sub", scatter_dimension=0, tiled=True)
-    forcing = owned_sums.transpose(1, 0, 2).reshape(field_count, LB_DEV * LBLK)
+    owned_sums = route_partials(flat_terms, pair_land, tile_count, sub_count, tile_index, sub_index)
+    forcing = owned_sums.reshape(LB_DEV, field_count, LBLK).transpose(1, 0, 2).reshape(
+        field_count, LB_DEV * LBLK
+    )
     land_forcing = forcing.astype(jnp.bfloat16)
     moisture, runoff = soil_update(forcing, land_mask, conductance, soil_moisture)
     block_count = runoff.shape[0] // RBLK
-    capacity = max(2, 2 * block_count // tile_count)
+    capacity = CAP_R
     runoff_blocks = runoff.reshape(block_count, RBLK)
     hits = (river_owner[:, None] == jnp.arange(tile_count, dtype=jnp.int32)[None, :]).astype(
         jnp.int32
@@ -141,18 +163,17 @@
     slot_id = river_owner * capacity + ranks
     placing = slot_id[None, :] == jnp.arange(tile_count * capacity, dtype=jnp.int32)[:, None]
     values = jnp.dot(placing.astype(jnp.float32), runoff_blocks, precision=lax.Precision.HIGHEST)
-    values = values.reshape(tile_count, capacity, RBLK)
+    values = values.reshape(tile_count, capacity * RBLK)
     block_ids = (tile_index * sub_count + sub_index) * block_count + jnp.arange(
         block_count, dtype=jnp.int32
     )
     numbers = jnp.sum(jnp.where(placing, block_ids[None, :] + 1, 0), axis=1) - 1
     numbers = numbers.astype(jnp.float32).reshape(tile_count, capacity)
-    got_values, got_numbers = (
-        lax.all_to_all(values, "tile", split_axis=0, concat_axis=0, tiled=True),
-        lax.all_to_all(numbers, "tile", split_axis=0, concat_axis=0, tiled=True),
-    )
-    river_runoff = got_values[None, None]
-    river_blocks = got_numbers.astype(jnp.int32)[None, None]
+    numbers = jnp.pad(numbers, ((0, 0), (0, RBLK - capacity)))
+    packed = jnp.concatenate([values, numbers], axis=1)
+    got = lax.all_to_all(packed, "tile", split_axis=0, concat_axis=0, tiled=True)
+    river_runoff = got[:, : capacity * RBLK].reshape(tile_count, capacity, RBLK)[None, None]
+    river_blocks = got[:, capacity * RBLK : capacity * RBLK + capacity].astype(jnp.int32)[None, None]
     return (land_forcing, moisture, river_runoff, river_blocks)
 
 

time: 114 us -> 87.9 us (0.77)
  waiting for transfers between devices: 42.8 us -> 8.48 us
  local copies, waits for them, and re-layouts: 9.17 us -> 26.1 us
  between operations: 14.3 us -> 1.09 us
  starting transfers between devices: 29.2 us -> 36.1 us
  other arithmetic: 11.6 us -> 10.2 us
    reduce_scatter x1 -> x0, waiting for transfers between devices: 25.7 us -> none  [on_device(): lax.psum_scatter(total_sums, 'sub', scatter_dimension=0, tiled=True)]
    ppermute x2 -> x11, starting transfers between devices: 1.79 us -> 24.9 us  [route_partials(): received.append(lax.ppermute(message, ('tile', 'sub'), route))]
    all_to_all x2 -> x1, starting transfers between devices: 23.5 us -> 7.28 us  [on_device(): lax.all_to_all(packed, 'tile', split_axis=0, concat_axis=0, tiled=True)]
    ppermute x2 -> x11, waiting for transfers between devices: 11.1 us -> 1.38 us  [route_partials(): received.append(lax.ppermute(message, ('tile', 'sub'), route))]
    slice x2, local copies, waits for them, and re-layouts: 0.58 us -> 5.38 us  [column_factors(): diagonal = 1.0 + conductance[k]]
    slice x2, local copies, waits for them, and re-layouts: 0.58 us -> 4.99 us  [column_solve(): column_value = moisture[k] + conductance[k - 1] * forward[k - 1]]
    another operation x0 -> x12, local copies, waits for them, and re-layouts: none -> 3.74 us  [route_partials(): got = jnp.stack(received)]
    gather x0 -> x4, local copies, waits for them, and re-layouts: none -> 2.54 us  [the longest x2 1.51 us: route_partials(): ids = jnp.where(filled, pair_land[picked] % LB_DEV, -1).astype(jnp.float32)]
  transfers between devices with their start and end apart: 7 -> 14, of which waited for: 4 -> 2; matrix products, arithmetic and copies ran while one was open for 18% -> 25% of each run, Pallas kernels for 0% -> 0%
where the time goes in v1:
time: 87.9 us; the launch traced here: 87.3 us
  starting transfers between devices  36.1 us (41%)
  local copies, waits for them, and re-layouts  26.1 us (30%)
  other arithmetic  10.2 us (12%)
  waiting for transfers between devices  8.48 us (10%)
  matrix products  5.34 us (6%)
  between operations  1.09 us (1%)
    ppermute x11, starting transfers between devices, route_partials(): received.append(lax.ppermute(message, ('tile', 'sub'), route))  24.9 us
    all_to_all x1, starting transfers between devices, on_device(): lax.all_to_all(packed, 'tile', split_axis=0, concat_axis=0, tiled=True)  7.28 us
    all_to_all x1, waiting for transfers between devices, on_device(): lax.all_to_all(packed, 'tile', split_axis=0, concat_axis=0, tiled=True)  7.1 us
    slice x2, local copies, waits for them, and re-layouts, column_factors(): diagonal = 1.0 + conductance[k]  5.38 us
    slice x2, local copies, waits for them, and re-layouts, column_solve(): column_value = moisture[k] + conductance[k - 1] * forward[k - 1]  4.99 us
    dot_general x1, matrix products, on_device(): jnp.einsum('fpk,pkl->pfl', picked, weights, preferred_element_type=jnp.fl...  4.35 us
    ppermute x1, starting transfers between devices, padded(): after = lax.ppermute(initial, axis, down)  3.87 us
    another operation x12, local copies, waits for them, and re-layouts, route_partials(): got = jnp.stack(received)  3.74 us
  transfers between devices with their start and end apart: 14, of which 2 were waited for; matrix products, arithmetic and copies ran while one was open for 25% of the time, Pallas kernels for 0%

profile of v1, /device:TPU:1, one launch (start us, length us, event | category | flops | bytes accessed | tf_op | source)
XLA Modules:
  0.0 87.3 jit_solution(9711312749482322049)
XLA Ops:
  0.6 0.8 fusion.59
  1.5 3.9 %collective-permute-start = (f32[6,1,128]{2,1,0:T(1,128)S(1)}, f32[6,1,128]{2,1,0:T(1,128)S(1)}, u32[]{:S(2)}, u32[]{:S(2)}) collective-permute-start(f32[6,1,128]{2,1,0:T(1,128)S(1)} %get-tuple-element.119), channel_id=1, source_target_pairs={{1,0},{2,1},{3,2},{4,3},{5,4},{6,5},{7,6},{8,7},{9,8},{10,9},{11,1... | collective-permute-start | bytes 9224 | tf_op jit(solution)/shard_map/ppermute | solution.py:26
  5.3 0.7 fusion.47
  6.1 0.2 select_reduce_fusion.3
  6.3 0.7 iota_add_fusion
  7.1 0.9 %multiply_convert_fusion = bf16[6,8,126]{2,1,0:T(8,128)(2,1)S(1)} fusion(f32[6,8,128]{2,1,0:T(8,128)} %param.8), kind=kLoop, calls=%fused_computation.260 | loop fusion | flops 18144 | bytes 60480 | tf_op jit(solution)/shard_map/convert.2
  8.0 1.0 %subtract_convert_fusion = (bf16[6,8,1]{2,1,0:T(8,128)(2,1)S(1)}, bf16[6,8,1]{2,1,0:T(8,128)(2,1)S(1)}) fusion(f32[6,8,128]{2,1,0:T(8,128)} %param.8), kind=kLoop, calls=%fused_computation.259 | loop fusion | flops 192 | bytes 960 | tf_op jit(solution)/shard_map/convert.3
  9.0 0.7 compare_select_fusion.3
  9.7 1.4 %gather_fusion.2 = s32[48]{0:T(128)S(1)} fusion(s32[20]{0:T(128)} %param.10, s32[1024]{0:T(1024)S(1)} %pad_clamp_fusion), kind=kCustom, calls=%fused_computation.2 | custom fusion | bytes 576 | tf_op jit(solution)/shard_map/gather | solution.py:109
  11.3 0.7 fusion.27
  12.1 0.8 select_reduce_fusion.1
  12.9 4.4 %fusion.57 = (f32[1,8192]{1,0:T(1,128)S(1)}, f32[1,8192]{1,0:T(1,128)S(1)}, f32[1,8192]{1,0:T(1,128)S(1)}, f32[1,8192]{1,0:T(1,128)S(1)}, f32[1,8192]{1,0:T(1,12...) fusion(f32[20,8192]{1,0:T(8,128)} %param.13), kind=kLoop, calls=%fused_computation.316 | loop fusion | bytes 1245184 | tf_op jit(solution)/shard_map/slice | solution.py:43
  17.3 4.0 %fusion.58 = (f32[1,8192]{1,0:T(1,128)S(1)}, f32[1,8192]{1,0:T(1,128)S(1)}, f32[1,8192]{1,0:T(1,128)S(1)}, f32[1,8192]{1,0:T(1,128)S(1)}, f32[1,8192]{1,0:T(1,12...) fusion(f32[20,8192]{1,0:T(8,128)} %param.14), kind=kLoop, calls=%fused_computation.317 | loop fusion | bytes 1245184 | tf_op jit(solution)/shard_map/slice | solution.py:63
  21.5 0.2 pad.27
  21.9 0.9 fusion.34
  22.9 0.6 gather_fusion
  23.4 4.3 %fusion.2 = f32[20,6,512]{2,1,0:T(8,128)S(1)} fusion(bf16[20,384,512]{2,1,0:T(8,128)(2,1)} %bitcast.104, bf16[20,6,384]{2,1,0:T(8,128)(2,1)S(1)} %gather_fusion), kind=kOutput, calls=%fused_computation.9 | convolution fusion | flops 47185920 | bytes 8202240 | tf_op jit(solution)/shard_map/fpk,pkl->pfl/dot_general | solution.py:148
  27.8 0.2 copy.63
  28.0 0.8 gather_fusion.1
  28.8 0.3 gather.15
  29.2 1.4 %slice_reduce_fusion = (f32[12416]{0:T(1024)S(1)}, f32[12416]{0:T(1024)S(1)}, f32[12416]{0:T(1024)S(1)}, f32[12416]{0:T(1024)S(1)}, f32[12416]{0:T(1024)S(1)}, /...) fusion(f32[12,12416]{1,0:T(8,128)S(1)} %select_maximum_fusion), kind=kLoop, calls=%fused_computation.16 | loop fusion | bytes 1191936 | tf_op jit(solution)/shard_map/slice | solution.py:116
  30.7 4.4 %collective-permute-start.12 = (f32[12416]{0:T(1024)S(1)}, f32[12416]{0:T(1024)S(1)}, u32[]{:S(2)}, u32[]{:S(2)}) collective-permute-start(f32[12416]{0:T(1024)S(1)} %get-tuple-element.8), channel_id=1, source_target_pairs={{0,7},{1,4},{2,5},{3,6},{4,11},{5,8},{6,9},{7,10},{8,15},{9,12},{1... | collective-permute-start | bytes 149000 | tf_op jit(solution)/shard_map/ppermute | solution.py:125
  35.1 1.8 %collective-permute-start.10 = (f32[12416]{0:T(1024)S(1)}, f32[12416]{0:T(1024)S(1)}, u32[]{:S(2)}, u32[]{:S(2)}) collective-permute-start(f32[12416]{0:T(1024)S(1)} %get-tuple-element.10), channel_id=1, source_target_pairs={{0,5},{1,6},{2,7},{3,4},{4,9},{5,10},{6,11},{7,8},{8,13},{9,14},{1... | collective-permute-start | bytes 149000 | tf_op jit(solution)/shard_map/ppermute | solution.py:125
  36.9 0.8 collective-permute-start.9
  37.7 2.1 %collective-permute-start.8 = (f32[12416]{0:T(1024)S(1)}, f32[12416]{0:T(1024)S(1)}, u32[]{:S(2)}, u32[]{:S(2)}) collective-permute-start(f32[12416]{0:T(1024)S(1)} %get-tuple-element.12), channel_id=1, source_target_pairs={{0,3},{1,0},{2,1},{3,2},{4,7},{5,4},{6,5},{7,6},{8,11},{9,8},{10,9... | collective-permute-start | bytes 149000 | tf_op jit(solution)/shard_map/ppermute | solution.py:125
  39.8 2.3 %collective-permute-start.7 = (f32[12416]{0:T(1024)S(1)}, f32[12416]{0:T(1024)S(1)}, u32[]{:S(2)}, u32[]{:S(2)}) collective-permute-start(f32[12416]{0:T(1024)S(1)} %get-tuple-element.13), channel_id=1, source_target_pairs={{0,2},{1,3},{2,0},{3,1},{4,6},{5,7},{6,4},{7,5},{8,10},{9,11},{10,... | collective-permute-start | bytes 149000 | tf_op jit(solution)/shard_map/ppermute | solution.py:125
  42.2 1.8 %collective-permute-start.6 = (f32[12416]{0:T(1024)S(1)}, f32[12416]{0:T(1024)S(1)}, u32[]{:S(2)}, u32[]{:S(2)}) collective-permute-start(f32[12416]{0:T(1024)S(1)} %get-tuple-element.14), channel_id=1, source_target_pairs={{0,1},{1,2},{2,3},{3,0},{4,5},{5,6},{6,7},{7,4},{8,9},{9,10},{10,1... | collective-permute-start | bytes 149000 | tf_op jit(solution)/shard_map/ppermute | solution.py:125
  43.9 8.2 %collective-permute-start.5 = (f32[12416]{0:T(1024)S(1)}, f32[12416]{0:T(1024)S(1)}, u32[]{:S(2)}, u32[]{:S(2)}) collective-permute-start(f32[12416]{0:T(1024)S(1)} %get-tuple-element.15), channel_id=1, source_target_pairs={{0,255},{1,252},{2,253},{3,254},{4,3},{5,0},{6,1},{7,2},{8,7},{9,4... | collective-permute-start | bytes 149000 | tf_op jit(solution)/shard_map/ppermute | solution.py:125
  52.2 1.8 %collective-permute-start.4 = (f32[12416]{0:T(1024)S(1)}, f32[12416]{0:T(1024)S(1)}, u32[]{:S(2)}, u32[]{:S(2)}) collective-permute-start(f32[12416]{0:T(1024)S(1)} %get-tuple-element.16), channel_id=1, source_target_pairs={{0,254},{1,255},{2,252},{3,253},{4,2},{5,3},{6,0},{7,1},{8,6},{9,7... | collective-permute-start | bytes 149000 | tf_op jit(solution)/shard_map/ppermute | solution.py:125
  54.0 1.8 %collective-permute-start.2 = (f32[12416]{0:T(1024)S(1)}, f32[12416]{0:T(1024)S(1)}, u32[]{:S(2)}, u32[]{:S(2)}) collective-permute-start(f32[12416]{0:T(1024)S(1)} %get-tuple-element.18), channel_id=1, source_target_pairs={{0,252},{1,253},{2,254},{3,255},{4,0},{5,1},{6,2},{7,3},{8,4},{9,5... | collective-permute-start | bytes 149000 | tf_op jit(solution)/shard_map/ppermute | solution.py:125
  55.8 1.0 %slice.211 = f32[1,8192]{1,0:T(1,128)S(1)} slice(f32[20,8192]{1,0:T(8,128)} %param.13), slice={[18:19], [0:8192]} | slice | bytes 65536 | tf_op jit(solution)/shard_map/slice | solution.py:43
  56.7 1.0 %slice.210 = f32[1,8192]{1,0:T(1,128)S(1)} slice(f32[20,8192]{1,0:T(8,128)} %param.14), slice={[18:19], [0:8192]} | slice | bytes 65536 | tf_op jit(solution)/shard_map/slice | solution.py:63
  58.3 1.3 %collective-permute-done.3 = f32[12416]{0:T(1024)S(1)} collective-permute-done((f32[12416]{0:T(1024)S(1)}, f32[12416]{0:T(1024)S(1)}, u32[]{:S(2)}, u32[]{:S(2)}) %collective-permute-start.3) | collective-permute-done | bytes 49696 | tf_op jit(solution)/shard_map/ppermute | solution.py:125
  59.7 3.3 %stack.110 = f32[12,12416]{1,0:T(8,128)S(1)} concatenate(f32[1,12416]{1,0:T(1,128)S(1)} %stack.99, f32[1,12416]{1,0:T(1,128)S(1)} %stack.100, f32[1,12416]{1,0:T(1,128)S(1)} %stack.101, f32[1,12416]{1,0:T(1,128)S(1)} %stack.102, f32[1,12416]{1,0:T(1,128)S(1)} %get-tuple-element.74, f32[1,12416]{1,0:T(1,128)S(1)} %stack.103, f32[1,12416]{1,0:T(1,128)S(1)} %stack.104, ...), dimensions={0} | concatenate | bytes 1191936 | tf_op jit(solution)/shard_map/stack | solution.py:126
  63.1 0.2 reshape.102
  63.4 0.3 convolution_bitcast_fusion
  63.9 0.7 copy.64
  64.6 0.3 add_multiply_fusion.63
  64.9 0.7 multiply_subtract_fusion.34
  65.6 0.8 add_multiply_fusion.1
  66.4 0.7 multiply_subtract_fusion.2
  67.0 0.7 fusion.16
  67.7 0.7 all_to_all.8
  68.4 7.3 %all-to-all-start = ((f32[64,1,384]{2,1,0:T(1,128)}), f32[64,1,384]{2,1,0:T(1,128)S(1)}, u32[]{:S(2)}, u32[]{:S(2)}) async-start(f32[64,1,384]{2,1,0:T(1,128)} %all_to_all.8), calls=%async_computation | async-start | bytes 196608 | tf_op jit(solution)/shard_map/all_to_all | solution.py:174
  75.8 3.0 %stack.131 = f32[20,8192]{1,0:T(8,128)} concatenate(f32[1,8192]{1,0:T(1,128)S(1)} %bitcast.330, f32[1,8192]{1,0:T(1,128)S(1)} %bitcast.331, f32[1,8192]{1,0:T(1,128)S(1)} %bitcast.313, f32[1,8192]{1,0:T(1,128)S(1)} %bitcast.312, f32[1,8192]{1,0:T(1,128)S(1)} %bitcast.314, f32[1,8192]{1,0:T(1,128)S(1)} %bitcast.315, f32[1,8192]{1,0:T(1,128)S(1)} %bitcast.316, ...), dimensions={0} | concatenate | bytes 1310720 | tf_op jit(solution)/shard_map/stack | solution.py:68
  78.8 7.1 %all-to-all-done = f32[64,1,384]{2,1,0:T(1,128)S(1)} async-done(((f32[64,1,384]{2,1,0:T(1,128)}), f32[64,1,384]{2,1,0:T(1,128)S(1)}, u32[]{:S(2)}, u32[]{:S(2)}) %all-to-all-start) | async-done | bytes 98336 | tf_op jit(solution)/shard_map/all_to_all | solution.py:174
  86.0 0.6 fusion.46
  86.6 0.7 copy.60
  (66 shorter events, 2.2 us)
Async XLA Ops:
  1.5 20.4 %collective-permute-start = (f32[6,1,128]{2,1,0:T(1,128)S(1)}, f32[6,1,128]{2,1,0:T(1,128)S(1)}, u32[]{:S(2)}, u32[]{:S(2)}) collective-permute-start(f32[6,1,128]{2,1,0:T(1,128)S(1)} %get-tuple-element.119), channel_id=1, source_target_pairs={{1,0},{2,1},{3,2},{4,3},{5,4},{6,5},{7,6},{8,7},{9,8},{10,9},{11,1... | collective-permute-start | bytes 9224 | tf_op jit(solution)/shard_map/ppermute | solution.py:26
  5.3 16.5 %collective-permute-start.1 = (f32[6,1,128]{2,1,0:T(1,128)S(1)}, f32[6,1,128]{2,1,0:T(1,128)S(1)}, u32[]{:S(2)}, u32[]{:S(2)}) collective-permute-start(f32[6,1,128]{2,1,0:T(1,128)S(1)} %get-tuple-element.120), channel_id=1, source_target_pairs={{0,1},{1,2},{2,3},{3,4},{4,5},{5,6},{6,7},{7,8},{8,9},{9,10},{10,1... | collective-permute-start | bytes 9224 | tf_op jit(solution)/shard_map/ppermute | solution.py:25
  27.8 7.3 %copy-start.1 = (s32[64]{0:T(128)S(1)}, s32[64]{0:T(128)}, u32[]{:S(2)}) copy-start(s32[64]{0:T(128)} %param.15) | copy-start | bytes 772
  28.8 35.8 %copy-start = (s32[8192]{0:T(1024)S(1)}, s32[8192]{0:T(1024)}, u32[]{:S(2)}) copy-start(s32[8192]{0:T(1024)} %param.12) | copy-start | bytes 98308
  30.7 9.1 %collective-permute-start.12 = (f32[12416]{0:T(1024)S(1)}, f32[12416]{0:T(1024)S(1)}, u32[]{:S(2)}, u32[]{:S(2)}) collective-permute-start(f32[12416]{0:T(1024)S(1)} %get-tuple-element.8), channel_id=1, source_target_pairs={{0,7},{1,4},{2,5},{3,6},{4,11},{5,8},{6,9},{7,10},{8,15},{9,12},{1... | collective-permute-start | bytes 149000 | tf_op jit(solution)/shard_map/ppermute | solution.py:125
  35.1 7.1 %collective-permute-start.11 = (f32[12416]{0:T(1024)S(1)}, f32[12416]{0:T(1024)S(1)}, u32[]{:S(2)}, u32[]{:S(2)}) collective-permute-start(f32[12416]{0:T(1024)S(1)} %get-tuple-element.9), channel_id=1, source_target_pairs={{0,6},{1,7},{2,4},{3,5},{4,10},{5,11},{6,8},{7,9},{8,14},{9,15},{1... | collective-permute-start | bytes 149000 | tf_op jit(solution)/shard_map/ppermute | solution.py:125
  35.1 8.9 %collective-permute-start.10 = (f32[12416]{0:T(1024)S(1)}, f32[12416]{0:T(1024)S(1)}, u32[]{:S(2)}, u32[]{:S(2)}) collective-permute-start(f32[12416]{0:T(1024)S(1)} %get-tuple-element.10), channel_id=1, source_target_pairs={{0,5},{1,6},{2,7},{3,4},{4,9},{5,10},{6,11},{7,8},{8,13},{9,14},{1... | collective-permute-start | bytes 149000 | tf_op jit(solution)/shard_map/ppermute | solution.py:125
  36.9 15.3 %collective-permute-start.9 = (f32[12416]{0:T(1024)S(1)}, f32[12416]{0:T(1024)S(1)}, u32[]{:S(2)}, u32[]{:S(2)}) collective-permute-start(f32[12416]{0:T(1024)S(1)} %get-tuple-element.11), channel_id=1, source_target_pairs={{0,4},{1,5},{2,6},{3,7},{4,8},{5,9},{6,10},{7,11},{8,12},{9,13},{1... | collective-permute-start | bytes 149000 | tf_op jit(solution)/shard_map/ppermute | solution.py:125
  37.7 16.3 %collective-permute-start.8 = (f32[12416]{0:T(1024)S(1)}, f32[12416]{0:T(1024)S(1)}, u32[]{:S(2)}, u32[]{:S(2)}) collective-permute-start(f32[12416]{0:T(1024)S(1)} %get-tuple-element.12), channel_id=1, source_target_pairs={{0,3},{1,0},{2,1},{3,2},{4,7},{5,4},{6,5},{7,6},{8,11},{9,8},{10,9... | collective-permute-start | bytes 149000 | tf_op jit(solution)/shard_map/ppermute | solution.py:125
  39.8 14.2 %collective-permute-start.7 = (f32[12416]{0:T(1024)S(1)}, f32[12416]{0:T(1024)S(1)}, u32[]{:S(2)}, u32[]{:S(2)}) collective-permute-start(f32[12416]{0:T(1024)S(1)} %get-tuple-element.13), channel_id=1, source_target_pairs={{0,2},{1,3},{2,0},{3,1},{4,6},{5,7},{6,4},{7,5},{8,10},{9,11},{10,... | collective-permute-start | bytes 149000 | tf_op jit(solution)/shard_map/ppermute | solution.py:125
  42.2 16.0 %collective-permute-start.6 = (f32[12416]{0:T(1024)S(1)}, f32[12416]{0:T(1024)S(1)}, u32[]{:S(2)}, u32[]{:S(2)}) collective-permute-start(f32[12416]{0:T(1024)S(1)} %get-tuple-element.14), channel_id=1, source_target_pairs={{0,1},{1,2},{2,3},{3,0},{4,5},{5,6},{6,7},{7,4},{8,9},{9,10},{10,1... | collective-permute-start | bytes 149000 | tf_op jit(solution)/shard_map/ppermute | solution.py:125
  43.9 14.2 %collective-permute-start.5 = (f32[12416]{0:T(1024)S(1)}, f32[12416]{0:T(1024)S(1)}, u32[]{:S(2)}, u32[]{:S(2)}) collective-permute-start(f32[12416]{0:T(1024)S(1)} %get-tuple-element.15), channel_id=1, source_target_pairs={{0,255},{1,252},{2,253},{3,254},{4,3},{5,0},{6,1},{7,2},{8,7},{9,4... | collective-permute-start | bytes 149000 | tf_op jit(solution)/shard_map/ppermute | solution.py:125
  52.2 6.1 %collective-permute-start.4 = (f32[12416]{0:T(1024)S(1)}, f32[12416]{0:T(1024)S(1)}, u32[]{:S(2)}, u32[]{:S(2)}) collective-permute-start(f32[12416]{0:T(1024)S(1)} %get-tuple-element.16), channel_id=1, source_target_pairs={{0,254},{1,255},{2,252},{3,253},{4,2},{5,3},{6,0},{7,1},{8,6},{9,7... | collective-permute-start | bytes 149000 | tf_op jit(solution)/shard_map/ppermute | solution.py:125
  53.9 5.7 %collective-permute-start.3 = (f32[12416]{0:T(1024)S(1)}, f32[12416]{0:T(1024)S(1)}, u32[]{:S(2)}, u32[]{:S(2)}) collective-permute-start(f32[12416]{0:T(1024)S(1)} %get-tuple-element.17), channel_id=1, source_target_pairs={{0,253},{1,254},{2,255},{3,252},{4,1},{5,2},{6,3},{7,0},{8,5},{9,6... | collective-permute-start | bytes 149000 | tf_op jit(solution)/shard_map/ppermute | solution.py:125
  54.0 5.7 %collective-permute-start.2 = (f32[12416]{0:T(1024)S(1)}, f32[12416]{0:T(1024)S(1)}, u32[]{:S(2)}, u32[]{:S(2)}) collective-permute-start(f32[12416]{0:T(1024)S(1)} %get-tuple-element.18), channel_id=1, source_target_pairs={{0,252},{1,253},{2,254},{3,255},{4,0},{5,1},{6,2},{7,3},{8,4},{9,5... | collective-permute-start | bytes 149000 | tf_op jit(solution)/shard_map/ppermute | solution.py:125
  68.4 17.5 %all-to-all-start = ((f32[64,1,384]{2,1,0:T(1,128)}), f32[64,1,384]{2,1,0:T(1,128)S(1)}, u32[]{:S(2)}, u32[]{:S(2)}) async-start(f32[64,1,384]{2,1,0:T(1,128)} %all_to_all.8), calls=%async_computation | async-start | bytes 196608 | tf_op jit(solution)/shard_map/all_to_all | solution.py:174

commit v2 on v1

--- a/solution.py
+++ b/solution.py
@@ -2,6 +2,8 @@
 import jax.numpy as jnp
 from jax import lax
 from jax.sharding import PartitionSpec as P
+from jax.experimental import pallas as pl
+from jax.experimental.pallas import tpu as pltpu
 
 SOIL_STEPS = 4
 LBLK = 512
@@ -68,6 +70,46 @@
     return jnp.stack(solved)
 
 
+def soil_kernel(source_ref, surface_ref, wet_ref, cond_ref, moist_ref, out_ref, runoff_ref):
+    layers = cond_ref.shape[0]
+    groups = cond_ref.shape[1] // 8
+
+    def one_group(g, carry):
+        rows = pl.ds(pl.multiple_of(g * 8, 8), 8)
+        cond = [cond_ref[k, rows, :] for k in range(layers)]
+        inverse = []
+        ratios = []
+        for k in range(layers):
+            diagonal = 1.0 + cond[k]
+            if k > 0:
+                diagonal = diagonal + cond[k - 1] - cond[k - 1] * cond[k - 1] * inverse[k - 1]
+            pivot_inv = 1.0 / diagonal
+            inverse.append(pivot_inv)
+            ratios.append(-cond[k] * pivot_inv)
+        source = source_ref[rows, :]
+        moisture = [moist_ref[k, rows, :] for k in range(layers)]
+        drainage = jnp.zeros_like(source)
+        for substep in range(SOIL_STEPS):
+            forward = []
+            for k in range(layers):
+                if k == 0:
+                    column_value = moisture[0] + source
+                else:
+                    column_value = moisture[k] + cond[k - 1] * forward[k - 1]
+                forward.append(column_value * inverse[k])
+            solved = [forward[layers - 1]]
+            for k in range(layers - 2, -1, -1):
+                solved.insert(0, forward[k] - ratios[k] * solved[0])
+            moisture = solved
+            drainage = drainage + cond[layers - 1] * moisture[layers - 1]
+        for k in range(layers):
+            out_ref[k, rows, :] = moisture[k]
+        runoff_ref[rows, :] = wet_ref[rows, :] * (SOIL_STEPS * surface_ref[rows, :] + drainage)
+        return carry
+
+    lax.fori_loop(0, groups, one_group, 0)
+
+
 def soil_update(forcing, land_mask, conductance, soil_moisture):
     wetness = land_mask.astype(jnp.float32)
     source = wetness * (
@@ -75,15 +117,29 @@
         - 0.5 * jax.nn.sigmoid(forcing[2]) * jax.nn.softplus(forcing[3])
     )
     surface = wetness * jax.nn.softplus(forcing[0]) * (1.0 - jax.nn.sigmoid(forcing[1]))
-    inverse, ratios = column_factors(conductance)
-    bottom = conductance.shape[0] - 1
-    moisture = soil_moisture
-    drainage = jnp.zeros_like(surface)
-    for substep in range(SOIL_STEPS):
-        moisture = column_solve(moisture, source, conductance, inverse, ratios)
-        drainage = drainage + conductance[bottom] * moisture[bottom]
-    runoff = wetness * (SOIL_STEPS * surface + drainage)
-    return (moisture, runoff)
+    layers, cells = conductance.shape
+    rows = cells // 128
+    grid = 2
+    block = rows // grid
+    plane = pl.BlockSpec((block, 128), lambda i: (i, 0))
+    stack = pl.BlockSpec((layers, block, 128), lambda i: (0, i, 0))
+    moisture, runoff = pl.pallas_call(
+        soil_kernel,
+        grid=(grid,),
+        in_specs=[plane, plane, plane, stack, stack],
+        out_specs=[stack, plane],
+        out_shape=[
+            jax.ShapeDtypeStruct((layers, rows, 128), jnp.float32),
+            jax.ShapeDtypeStruct((rows, 128), jnp.float32),
+        ],
+    )(
+        source.reshape(rows, 128),
+        surface.reshape(rows, 128),
+        wetness.reshape(rows, 128),
+        conductance.reshape(layers, rows, 128),
+        soil_moisture.reshape(layers, rows, 128),
+    )
+    return (moisture.reshape(layers, cells), runoff.reshape(cells))
 
 
 CAP_P = 4

time: 87.9 us -> 82.5 us (0.939)
  local copies, waits for them, and re-layouts: 26.1 us -> 17.3 us
  Pallas kernels: 0 us -> 5.96 us
  starting transfers between devices: 36.1 us -> 33.3 us
    slice x4 -> x0, local copies, waits for them, and re-layouts: 10.4 us -> none  [the longest x2 5.38 us: column_factors(): diagonal = 1.0 + conductance[k]]
    pallas_call x0 -> x1, Pallas kernels: none -> 5.96 us  [soil_update(): pl.pallas_call(soil_kernel, grid=(grid,), in_specs=[plane, plane, plane,...]
    another operation x1 -> x0, local copies, waits for them, and re-layouts: 3.03 us -> none  [column_solve(): return jnp.stack(solved)]
    ppermute x11, starting transfers between devices: 24.9 us -> 22.1 us  [route_partials(): received.append(lax.ppermute(message, ('tile', 'sub'), route))]
    unnamed x14 -> x22, local copies, waits for them, and re-layouts: 1.98 us -> 4.76 us
    reshape x0 -> x2, other arithmetic: none -> 2.04 us  [the longest x1 1.36 us: soil_update(): wetness.reshape(rows, 128)]
    ppermute x1, starting transfers between devices: 0.01 us -> 2.04 us  [padded(): before = lax.ppermute(last, axis, up)]
    ppermute x1, starting transfers between devices: 3.87 us -> 1.92 us  [padded(): after = lax.ppermute(initial, axis, down)]
  transfers between devices with their start and end apart: 14 -> 14, of which waited for: 2 -> 3; matrix products, arithmetic and copies ran while one was open for 25% -> 19% of each run, Pallas kernels for 0% -> 0%
where the time goes in v2:
time: 82.5 us; the launch traced here: 81.8 us
  starting transfers between devices  33.3 us (40%)
  local copies, waits for them, and re-layouts  17.3 us (21%)
  other arithmetic  9.77 us (12%)
  waiting for transfers between devices  8.59 us (10%)
  Pallas kernels  5.96 us (7%)
  matrix products  5.74 us (7%)
  between operations  1.08 us (1%)
    ppermute x11, starting transfers between devices, route_partials(): received.append(lax.ppermute(message, ('tile', 'sub'), route))  22.1 us
    all_to_all x1, starting transfers between devices, on_device(): lax.all_to_all(packed, 'tile', split_axis=0, concat_axis=0, tiled=True)  7.2 us
    all_to_all x1, waiting for transfers between devices, on_device(): lax.all_to_all(packed, 'tile', split_axis=0, concat_axis=0, tiled=True)  7.05 us
    pallas_call x1, Pallas kernels, soil_update(): pl.pallas_call(soil_kernel, grid=(grid,), in_specs=[plane, plane, plane,...  5.96 us
    unnamed x22, local copies, waits for them, and re-layouts  4.76 us
    dot_general x1, matrix products, on_device(): jnp.einsum('fpk,pkl->pfl', picked, weights, preferred_element_type=jnp.fl...  4.35 us
    another operation x12, local copies, waits for them, and re-layouts, route_partials(): got = jnp.stack(received)  3.74 us
    another operation x3, other arithmetic  2.73 us
  transfers between devices with their start and end apart: 14, of which 3 were waited for; matrix products, arithmetic and copies ran while one was open for 19% of the time, Pallas kernels for 0%

profile of v2, /device:TPU:1, one launch (start us, length us, event | category | flops | bytes accessed | tf_op | source)
XLA Modules:
  0.0 81.8 jit_solution(10869671764332370958)
XLA Ops:
  0.6 0.8 %fusion.37 = (f32[6,1,128]{2,1,0:T(1,128)S(1)}, f32[6,1,128]{2,1,0:T(1,128)S(1)}) fusion(f32[6,8,128]{2,1,0:T(8,128)} %param.8), kind=kLoop, calls=%fused_computation.108 | loop fusion | bytes 12288 | tf_op jit(solution)/shard_map/slice | solution.py:26
  1.5 2.0 %collective-permute-start.1 = (f32[6,1,128]{2,1,0:T(1,128)S(1)}, f32[6,1,128]{2,1,0:T(1,128)S(1)}, u32[]{:S(2)}, u32[]{:S(2)}) collective-permute-start(f32[6,1,128]{2,1,0:T(1,128)S(1)} %get-tuple-element.33), channel_id=1, source_target_pairs={{0,1},{1,2},{2,3},{3,4},{4,5},{5,6},{6,7},{7,8},{8,9},{9,10},{10,1... | collective-permute-start | bytes 9224 | tf_op jit(solution)/shard_map/ppermute | solution.py:27
  3.5 1.9 %collective-permute-start = (f32[6,1,128]{2,1,0:T(1,128)S(1)}, f32[6,1,128]{2,1,0:T(1,128)S(1)}, u32[]{:S(2)}, u32[]{:S(2)}) collective-permute-start(f32[6,1,128]{2,1,0:T(1,128)S(1)} %get-tuple-element.32), channel_id=1, source_target_pairs={{1,0},{2,1},{3,2},{4,3},{5,4},{6,5},{7,6},{8,7},{9,8},{10,9},{11,1... | collective-permute-start | bytes 9224 | tf_op jit(solution)/shard_map/ppermute | solution.py:28
  5.4 0.7 fusion.31
  6.2 0.2 select_reduce_fusion.3
  6.4 0.7 iota_add_fusion
  7.2 1.0 %subtract_convert_fusion = (bf16[6,8,1]{2,1,0:T(8,128)(2,1)S(1)}, bf16[6,8,1]{2,1,0:T(8,128)(2,1)S(1)}) fusion(f32[6,8,128]{2,1,0:T(8,128)} %param.8), kind=kLoop, calls=%fused_computation.57 | loop fusion | flops 192 | bytes 960 | tf_op jit(solution)/shard_map/convert.3
  8.2 0.9 %multiply_convert_fusion = bf16[6,8,126]{2,1,0:T(8,128)(2,1)S(1)} fusion(f32[6,8,128]{2,1,0:T(8,128)} %param.8), kind=kLoop, calls=%fused_computation.58 | loop fusion | flops 18144 | bytes 60480 | tf_op jit(solution)/shard_map/convert.2
  9.2 1.4 %gather_fusion.2 = s32[48]{0:T(128)S(1)} fusion(s32[20]{0:T(128)} %param.10, s32[1024]{0:T(1024)S(1)} %pad_clamp_fusion), kind=kCustom, calls=%fused_computation.2 | custom fusion | bytes 576 | tf_op jit(solution)/shard_map/gather | solution.py:165
  10.7 0.7 compare_select_fusion.2
  11.4 1.4 %convert_bitcast_fusion.1.wet_ref = f32[64,128]{1,0:T(8,128)} fusion(s32[8192]{0:T(1024)} %param.12), kind=kLoop, calls=%fused_computation.51 | loop fusion | flops 8192 | bytes 65536 | tf_op jit(solution)/shard_map/reshape | solution.py:138
  12.7 0.7 fusion.18
  13.5 0.8 %select_reduce_fusion.1 = s32[64]{0:T(128)S(1)} fusion(s32[64,64]{1,0:T(8,128)S(1)} %reduce_window_sum.23, s32[64]{0:T(128)} %param.15), kind=kLoop, calls=%fused_computation.47 | loop fusion | flops 20416 | bytes 16896 | tf_op jit(solution)/shard_map/reduce_sum | solution.py:218
  14.6 0.2 pad.27
  14.9 0.9 %fusion.21 = (bf16[6,8,128]{2,1,0:T(8,128)(2,1)S(1)}, bf16[6,8,128]{2,1,0:T(8,128)(2,1)S(1)}) fusion(f32[6,8,128]{2,1,0:T(8,128)} %param.8, f32[6,1,128]{2,1,0:T(1,128)S(1)} %collective-permute-done.1, f32[6,1,128]{2,1,0:T(1,128)S(1)} %collective-permute-done), kind=kLoop, calls=%fused_computation.55 | loop fusion | flops 36864 | bytes 55296 | tf_op jit(solution)/shard_map/convert.4
  15.9 0.6 gather_fusion
  16.5 4.3 %fusion.2 = f32[20,6,512]{2,1,0:T(8,128)S(1)} fusion(bf16[20,384,512]{2,1,0:T(8,128)(2,1)} %bitcast.57, bf16[20,6,384]{2,1,0:T(8,128)(2,1)S(1)} %gather_fusion), kind=kOutput, calls=%fused_computation.9 | convolution fusion | flops 47185920 | bytes 8202240 | tf_op jit(solution)/shard_map/fpk,pkl->pfl/dot_general | solution.py:204
  21.1 0.8 gather_fusion.1
  21.8 0.3 gather.15
  22.3 1.4 %slice_reduce_fusion = (f32[12416]{0:T(1024)S(1)}, f32[12416]{0:T(1024)S(1)}, f32[12416]{0:T(1024)S(1)}, f32[12416]{0:T(1024)S(1)}, f32[12416]{0:T(1024)S(1)}, /...) fusion(f32[12,12416]{1,0:T(8,128)S(1)} %select_maximum_fusion), kind=kLoop, calls=%fused_computation.16 | loop fusion | bytes 1191936 | tf_op jit(solution)/shard_map/slice | solution.py:172
  23.7 7.7 %collective-permute-start.2 = (f32[12416]{0:T(1024)S(1)}, f32[12416]{0:T(1024)S(1)}, u32[]{:S(2)}, u32[]{:S(2)}) collective-permute-start(f32[12416]{0:T(1024)S(1)} %get-tuple-element.22), channel_id=1, source_target_pairs={{0,252},{1,253},{2,254},{3,255},{4,0},{5,1},{6,2},{7,3},{8,4},{9,5... | collective-permute-start | bytes 149000 | tf_op jit(solution)/shard_map/ppermute | solution.py:181
  31.4 0.3 collective-permute-start.3
  31.6 3.4 %collective-permute-start.4 = (f32[12416]{0:T(1024)S(1)}, f32[12416]{0:T(1024)S(1)}, u32[]{:S(2)}, u32[]{:S(2)}) collective-permute-start(f32[12416]{0:T(1024)S(1)} %get-tuple-element.20), channel_id=1, source_target_pairs={{0,254},{1,255},{2,252},{3,253},{4,2},{5,3},{6,0},{7,1},{8,6},{9,7... | collective-permute-start | bytes 149000 | tf_op jit(solution)/shard_map/ppermute | solution.py:181
  35.0 1.1 %collective-permute-start.5 = (f32[12416]{0:T(1024)S(1)}, f32[12416]{0:T(1024)S(1)}, u32[]{:S(2)}, u32[]{:S(2)}) collective-permute-start(f32[12416]{0:T(1024)S(1)} %get-tuple-element.19), channel_id=1, source_target_pairs={{0,255},{1,252},{2,253},{3,254},{4,3},{5,0},{6,1},{7,2},{8,7},{9,4... | collective-permute-start | bytes 149000 | tf_op jit(solution)/shard_map/ppermute | solution.py:181
  36.2 0.3 collective-permute-start.6
  36.5 1.7 %collective-permute-start.7 = (f32[12416]{0:T(1024)S(1)}, f32[12416]{0:T(1024)S(1)}, u32[]{:S(2)}, u32[]{:S(2)}) collective-permute-start(f32[12416]{0:T(1024)S(1)} %get-tuple-element.17), channel_id=1, source_target_pairs={{0,2},{1,3},{2,0},{3,1},{4,6},{5,7},{6,4},{7,5},{8,10},{9,11},{10,... | collective-permute-start | bytes 149000 | tf_op jit(solution)/shard_map/ppermute | solution.py:181
  38.4 2.1 %collective-permute-start.8 = (f32[12416]{0:T(1024)S(1)}, f32[12416]{0:T(1024)S(1)}, u32[]{:S(2)}, u32[]{:S(2)}) collective-permute-start(f32[12416]{0:T(1024)S(1)} %get-tuple-element.16), channel_id=1, source_target_pairs={{0,3},{1,0},{2,1},{3,2},{4,7},{5,4},{6,5},{7,6},{8,11},{9,8},{10,9... | collective-permute-start | bytes 149000 | tf_op jit(solution)/shard_map/ppermute | solution.py:181
  40.5 2.3 %collective-permute-start.9 = (f32[12416]{0:T(1024)S(1)}, f32[12416]{0:T(1024)S(1)}, u32[]{:S(2)}, u32[]{:S(2)}) collective-permute-start(f32[12416]{0:T(1024)S(1)} %get-tuple-element.15), channel_id=1, source_target_pairs={{0,4},{1,5},{2,6},{3,7},{4,8},{5,9},{6,10},{7,11},{8,12},{9,13},{1... | collective-permute-start | bytes 149000 | tf_op jit(solution)/shard_map/ppermute | solution.py:181
  42.8 1.2 %collective-permute-start.11 = (f32[12416]{0:T(1024)S(1)}, f32[12416]{0:T(1024)S(1)}, u32[]{:S(2)}, u32[]{:S(2)}) collective-permute-start(f32[12416]{0:T(1024)S(1)} %get-tuple-element.13), channel_id=1, source_target_pairs={{0,6},{1,7},{2,4},{3,5},{4,10},{5,11},{6,8},{7,9},{8,14},{9,15},{1... | collective-permute-start | bytes 149000 | tf_op jit(solution)/shard_map/ppermute | solution.py:181
  44.1 1.9 %collective-permute-start.12 = (f32[12416]{0:T(1024)S(1)}, f32[12416]{0:T(1024)S(1)}, u32[]{:S(2)}, u32[]{:S(2)}) collective-permute-start(f32[12416]{0:T(1024)S(1)} %get-tuple-element.12), channel_id=1, source_target_pairs={{0,7},{1,4},{2,5},{3,6},{4,11},{5,8},{6,9},{7,10},{8,15},{9,12},{1... | collective-permute-start | bytes 149000 | tf_op jit(solution)/shard_map/ppermute | solution.py:181
  46.1 0.9 %slice.154.cond_ref = f32[20,64,128]{2,1,0:T(8,128)} slice(f32[24,64,128]{2,1,0:T(8,128)S(1)} %bitcast.59), slice={[0:20], [0:64], [0:128]} | slice | bytes 1310720 | tf_op jit(solution)/shard_map/reshape | solution.py:139
  47.2 0.9 %slice.155.moist_ref = f32[20,64,128]{2,1,0:T(8,128)} slice(f32[24,64,128]{2,1,0:T(8,128)S(1)} %bitcast.60), slice={[0:20], [0:64], [0:128]} | slice | bytes 1310720 | tf_op jit(solution)/shard_map/reshape | solution.py:140
  48.6 0.6 collective-permute-done.10
  49.2 1.0 %collective-permute-done.12 = f32[12416]{0:T(1024)S(1)} collective-permute-done((f32[12416]{0:T(1024)S(1)}, f32[12416]{0:T(1024)S(1)}, u32[]{:S(2)}, u32[]{:S(2)}) %collective-permute-start.12) | collective-permute-done | bytes 49696 | tf_op jit(solution)/shard_map/ppermute | solution.py:181
  50.2 3.3 %stack.47 = f32[12,12416]{1,0:T(8,128)S(1)} concatenate(f32[1,12416]{1,0:T(1,128)S(1)} %stack.36, f32[1,12416]{1,0:T(1,128)S(1)} %stack.37, f32[1,12416]{1,0:T(1,128)S(1)} %stack.38, f32[1,12416]{1,0:T(1,128)S(1)} %stack.39, f32[1,12416]{1,0:T(1,128)S(1)} %get-tuple-element.23, f32[1,12416]{1,0:T(1,128)S(1)} %stack.40, f32[1,12416]{1,0:T(1,128)S(1)} %stack.41, ...), dimensions={0} | concatenate | bytes 1191936 | tf_op jit(solution)/shard_map/stack | solution.py:182
  53.6 0.2 reshape.117
  53.9 0.3 convolution_bitcast_fusion
  54.3 0.7 multiply_bitcast_fusion
  55.0 6.0 %shard_map.111 = (f32[20,64,128]{2,1,0:T(8,128)}, f32[64,128]{1,0:T(8,128)}) custom-call(f32[64,128]{1,0:T(8,128)} %get-tuple-element.29.source_ref, f32[64,128]{1,0:T(8,128)} %get-tuple-element.28.surface_ref, f32[64,128]{1,0:T(8,128)} %convert_bitcast_fusion.1.wet_ref, f32[20,64,128]{2,1,0:T(8,128)} %slice.154.cond_ref, f32[20,64,128]{2,1,0:T(8,128)} %slice.155.moist_ref), custom_call_target="tpu_custom_call" | custom-call | tf_op jit(solution)/shard_map/pallas_call | solution.py:126
  61.0 1.1 %fusion.17 = f32[128,128]{1,0:T(8,128)S(1)} fusion(f32[64,128]{1,0:T(8,128)} %get-tuple-element.7, s32[64]{0:T(128)S(1)} %get-tuple-element.39), kind=kOutput, calls=%fused_computation.46 | convolution fusion | flops 12591104 | bytes 98560 | tf_op jit(solution)/shard_map/dot_general | solution.py:221
  62.1 0.7 all_to_all.8
  62.8 7.2 %all-to-all-start = ((f32[64,1,384]{2,1,0:T(1,128)}), f32[64,1,384]{2,1,0:T(1,128)S(1)}, u32[]{:S(2)}, u32[]{:S(2)}) async-start(f32[64,1,384]{2,1,0:T(1,128)} %all_to_all.8), calls=%async_computation | async-start | bytes 196608 | tf_op jit(solution)/shard_map/all_to_all | solution.py:230
  70.0 0.7 copy.64
  70.8 1.2 %pad.29 = f32[24,64,128]{2,1,0:T(8,128)S(1)} pad(f32[20,64,128]{2,1,0:T(8,128)} %get-tuple-element.6, f32[]{:T(128)} %constant.113.clone.1), padding=0_4x0_0x0_0 | pad | bytes 1441796
  71.9 1.3 %copy.71 = f32[3,8,64,128]{3,1,2,0:T(8,128)} copy(f32[3,8,64,128]{3,2,1,0:T(8,128)S(1)} %bitcast.58) | data formatting | bytes 1572864
  73.3 7.0 %all-to-all-done = f32[64,1,384]{2,1,0:T(1,128)S(1)} async-done(((f32[64,1,384]{2,1,0:T(1,128)}), f32[64,1,384]{2,1,0:T(1,128)S(1)}, u32[]{:S(2)}, u32[]{:S(2)}) %all-to-all-start) | async-done | bytes 98336 | tf_op jit(solution)/shard_map/all_to_all | solution.py:230
  80.5 0.6 fusion.30
  81.1 0.7 copy.60
  (69 shorter events, 2.6 us)
Async XLA Ops:
  1.5 13.4 %collective-permute-start.1 = (f32[6,1,128]{2,1,0:T(1,128)S(1)}, f32[6,1,128]{2,1,0:T(1,128)S(1)}, u32[]{:S(2)}, u32[]{:S(2)}) collective-permute-start(f32[6,1,128]{2,1,0:T(1,128)S(1)} %get-tuple-element.33), channel_id=1, source_target_pairs={{0,1},{1,2},{2,3},{3,4},{4,5},{5,6},{6,7},{7,8},{8,9},{9,10},{10,1... | collective-permute-start | bytes 9224 | tf_op jit(solution)/shard_map/ppermute | solution.py:27
  3.5 11.4 %collective-permute-start = (f32[6,1,128]{2,1,0:T(1,128)S(1)}, f32[6,1,128]{2,1,0:T(1,128)S(1)}, u32[]{:S(2)}, u32[]{:S(2)}) collective-permute-start(f32[6,1,128]{2,1,0:T(1,128)S(1)} %get-tuple-element.32), channel_id=1, source_target_pairs={{1,0},{2,1},{3,2},{4,3},{5,4},{6,5},{7,6},{8,7},{9,8},{10,9},{11,1... | collective-permute-start | bytes 9224 | tf_op jit(solution)/shard_map/ppermute | solution.py:28
  20.8 10.5 %copy-start.3 = (s32[64]{0:T(128)S(1)}, s32[64]{0:T(128)}, u32[]{:S(2)}) copy-start(s32[64]{0:T(128)} %param.15) | copy-start | bytes 772
  20.8 25.2 %copy-start = (f32[20,8192]{1,0:T(8,128)S(1)}, f32[20,8192]{1,0:T(8,128)}, u32[]{:S(2)}) copy-start(f32[20,8192]{1,0:T(8,128)} %param.13) | copy-start | bytes 1966084
  20.8 26.2 %copy-start.1 = (f32[20,8192]{1,0:T(8,128)S(1)}, f32[20,8192]{1,0:T(8,128)}, u32[]{:S(2)}) copy-start(f32[20,8192]{1,0:T(8,128)} %param.14) | copy-start | bytes 1966084
  22.2 32.2 %copy-start.2 = (s32[8192]{0:T(1024)S(1)}, s32[8192]{0:T(1024)}, u32[]{:S(2)}) copy-start(s32[8192]{0:T(1024)} %param.12) | copy-start | bytes 98308
  23.7 12.8 %collective-permute-start.2 = (f32[12416]{0:T(1024)S(1)}, f32[12416]{0:T(1024)S(1)}, u32[]{:S(2)}, u32[]{:S(2)}) collective-permute-start(f32[12416]{0:T(1024)S(1)} %get-tuple-element.22), channel_id=1, source_target_pairs={{0,252},{1,253},{2,254},{3,255},{4,0},{5,1},{6,2},{7,3},{8,4},{9,5... | collective-permute-start | bytes 149000 | tf_op jit(solution)/shard_map/ppermute | solution.py:181
  31.4 7.0 %collective-permute-start.3 = (f32[12416]{0:T(1024)S(1)}, f32[12416]{0:T(1024)S(1)}, u32[]{:S(2)}, u32[]{:S(2)}) collective-permute-start(f32[12416]{0:T(1024)S(1)} %get-tuple-element.21), channel_id=1, source_target_pairs={{0,253},{1,254},{2,255},{3,252},{4,1},{5,2},{6,3},{7,0},{8,5},{9,6... | collective-permute-start | bytes 149000 | tf_op jit(solution)/shard_map/ppermute | solution.py:181
  31.6 8.9 %collective-permute-start.4 = (f32[12416]{0:T(1024)S(1)}, f32[12416]{0:T(1024)S(1)}, u32[]{:S(2)}, u32[]{:S(2)}) collective-permute-start(f32[12416]{0:T(1024)S(1)} %get-tuple-element.20), channel_id=1, source_target_pairs={{0,254},{1,255},{2,252},{3,253},{4,2},{5,3},{6,0},{7,1},{8,6},{9,7... | collective-permute-start | bytes 149000 | tf_op jit(solution)/shard_map/ppermute | solution.py:181
  35.0 7.8 %collective-permute-start.5 = (f32[12416]{0:T(1024)S(1)}, f32[12416]{0:T(1024)S(1)}, u32[]{:S(2)}, u32[]{:S(2)}) collective-permute-start(f32[12416]{0:T(1024)S(1)} %get-tuple-element.19), channel_id=1, source_target_pairs={{0,255},{1,252},{2,253},{3,254},{4,3},{5,0},{6,1},{7,2},{8,7},{9,4... | collective-permute-start | bytes 149000 | tf_op jit(solution)/shard_map/ppermute | solution.py:181
  36.2 6.6 %collective-permute-start.6 = (f32[12416]{0:T(1024)S(1)}, f32[12416]{0:T(1024)S(1)}, u32[]{:S(2)}, u32[]{:S(2)}) collective-permute-start(f32[12416]{0:T(1024)S(1)} %get-tuple-element.18), channel_id=1, source_target_pairs={{0,1},{1,2},{2,3},{3,0},{4,5},{5,6},{6,7},{7,4},{8,9},{9,10},{10,1... | collective-permute-start | bytes 149000 | tf_op jit(solution)/shard_map/ppermute | solution.py:181
  36.5 7.5 %collective-permute-start.7 = (f32[12416]{0:T(1024)S(1)}, f32[12416]{0:T(1024)S(1)}, u32[]{:S(2)}, u32[]{:S(2)}) collective-permute-start(f32[12416]{0:T(1024)S(1)} %get-tuple-element.17), channel_id=1, source_target_pairs={{0,2},{1,3},{2,0},{3,1},{4,6},{5,7},{6,4},{7,5},{8,10},{9,11},{10,... | collective-permute-start | bytes 149000 | tf_op jit(solution)/shard_map/ppermute | solution.py:181
  38.4 10.1 %collective-permute-start.8 = (f32[12416]{0:T(1024)S(1)}, f32[12416]{0:T(1024)S(1)}, u32[]{:S(2)}, u32[]{:S(2)}) collective-permute-start(f32[12416]{0:T(1024)S(1)} %get-tuple-element.16), channel_id=1, source_target_pairs={{0,3},{1,0},{2,1},{3,2},{4,7},{5,4},{6,5},{7,6},{8,11},{9,8},{10,9... | collective-permute-start | bytes 149000 | tf_op jit(solution)/shard_map/ppermute | solution.py:181
  40.5 8.0 %collective-permute-start.9 = (f32[12416]{0:T(1024)S(1)}, f32[12416]{0:T(1024)S(1)}, u32[]{:S(2)}, u32[]{:S(2)}) collective-permute-start(f32[12416]{0:T(1024)S(1)} %get-tuple-element.15), channel_id=1, source_target_pairs={{0,4},{1,5},{2,6},{3,7},{4,8},{5,9},{6,10},{7,11},{8,12},{9,13},{1... | collective-permute-start | bytes 149000 | tf_op jit(solution)/shard_map/ppermute | solution.py:181
  42.8 6.3 %collective-permute-start.10 = (f32[12416]{0:T(1024)S(1)}, f32[12416]{0:T(1024)S(1)}, u32[]{:S(2)}, u32[]{:S(2)}) collective-permute-start(f32[12416]{0:T(1024)S(1)} %get-tuple-element.14), channel_id=1, source_target_pairs={{0,5},{1,6},{2,7},{3,4},{4,9},{5,10},{6,11},{7,8},{8,13},{9,14},{1... | collective-permute-start | bytes 149000 | tf_op jit(solution)/shard_map/ppermute | solution.py:181
  42.8 6.3 %collective-permute-start.11 = (f32[12416]{0:T(1024)S(1)}, f32[12416]{0:T(1024)S(1)}, u32[]{:S(2)}, u32[]{:S(2)}) collective-permute-start(f32[12416]{0:T(1024)S(1)} %get-tuple-element.13), channel_id=1, source_target_pairs={{0,6},{1,7},{2,4},{3,5},{4,10},{5,11},{6,8},{7,9},{8,14},{9,15},{1... | collective-permute-start | bytes 149000 | tf_op jit(solution)/shard_map/ppermute | solution.py:181
  44.1 6.1 %collective-permute-start.12 = (f32[12416]{0:T(1024)S(1)}, f32[12416]{0:T(1024)S(1)}, u32[]{:S(2)}, u32[]{:S(2)}) collective-permute-start(f32[12416]{0:T(1024)S(1)} %get-tuple-element.12), channel_id=1, source_target_pairs={{0,7},{1,4},{2,5},{3,6},{4,11},{5,8},{6,9},{7,10},{8,15},{9,12},{1... | collective-permute-start | bytes 149000 | tf_op jit(solution)/shard_map/ppermute | solution.py:181
  62.8 17.5 %all-to-all-start = ((f32[64,1,384]{2,1,0:T(1,128)}), f32[64,1,384]{2,1,0:T(1,128)S(1)}, u32[]{:S(2)}, u32[]{:S(2)}) async-start(f32[64,1,384]{2,1,0:T(1,128)} %all_to_all.8), calls=%async_computation | async-start | bytes 196608 | tf_op jit(solution)/shard_map/all_to_all | solution.py:230

commit v3 on v2

--- a/solution.py
+++ b/solution.py
@@ -146,13 +146,18 @@
 CAP_R = 2
 
 
-def route_partials(flat_terms, pair_land, tile_count, sub_count, tile_index, sub_index):
-    pair_count, width = flat_terms.shape
+def id_rows(ids, width):
+    flat = ids.reshape(-1)
+    return jnp.pad(flat, (0, 8 * width - flat.shape[0])).reshape(8, width)
+
+
+def route_partials(partial_value, pair_land, tile_count, sub_count, tile_index):
+    pair_count, field_count, width = partial_value.shape
     owner_device = pair_land // LB_DEV
     tile_step = (owner_device // sub_count - tile_index + 1 + tile_count) % tile_count
-    sub_step = (owner_device % sub_count - sub_index + sub_count) % sub_count
+    dest_sub = owner_device % sub_count
     group_count = 3 * sub_count
-    group_id = tile_step * sub_count + sub_step
+    group_id = dest_sub * 3 + tile_step
     hits = (group_id[:, None] == jnp.arange(group_count, dtype=jnp.int32)[None, :]).astype(jnp.int32)
     ranks = jnp.sum((jnp.cumsum(hits, axis=0) - hits) * hits, axis=1)
     slot_id = group_id * CAP_P + ranks
@@ -161,29 +166,38 @@
     source = jnp.sum(jnp.where(placing, jnp.arange(pair_count, dtype=jnp.int32)[None, :] + 1, 0), axis=1) - 1
     filled = source >= 0
     picked = jnp.maximum(source, 0)
-    rows = jnp.where(filled[:, None], flat_terms[picked], 0.0)
+    rows = jnp.where(filled[:, None, None], partial_value[picked], 0.0)
     ids = jnp.where(filled, pair_land[picked] % LB_DEV, -1).astype(jnp.float32)
-    ids = jnp.pad(ids.reshape(group_count, CAP_P), ((0, 0), (0, 128 - CAP_P)))
-    messages = jnp.concatenate([rows.reshape(group_count, CAP_P * width), ids], axis=1)
-    devices = tile_count * sub_count
-    received = []
-    for tile_offset in range(3):
-        for sub_offset in range(sub_count):
-            message = messages[tile_offset * sub_count + sub_offset]
-            if tile_offset == 1 and sub_offset == 0:
-                received.append(message)
-                continue
-            route = []
-            for d in range(devices):
-                t, s = divmod(d, sub_count)
-                target = ((t + tile_offset - 1) % tile_count) * sub_count + (s + sub_offset) % sub_count
-                route.append((d, target))
-            received.append(lax.ppermute(message, ("tile", "sub"), route))
-    got = jnp.stack(received)
-    data = got[:, : CAP_P * width].reshape(slot_count, width)
-    got_ids = got[:, CAP_P * width : CAP_P * width + CAP_P].reshape(slot_count)
-    selector = (got_ids[None, :] == jnp.arange(LB_DEV, dtype=jnp.float32)[:, None]).astype(jnp.float32)
-    return jnp.dot(selector, data, precision=lax.Precision.HIGHEST)
+    chunk_rows = 3 * CAP_P * field_count
+    ids = ids.reshape(sub_count, 3 * CAP_P)
+    chunks = jnp.concatenate(
+        [
+            rows.reshape(sub_count, chunk_rows, width),
+            jnp.stack([id_rows(ids[j], width) for j in range(sub_count)]),
+        ],
+        axis=1,
+    )
+    by_sub = lax.all_to_all(chunks, "sub", split_axis=0, concat_axis=0, tiled=True)
+    part_rows = CAP_P * field_count
+    got_ids = by_sub[:, chunk_rows, : 3 * CAP_P]
+    messages = []
+    for tile_step in range(3):
+        data = by_sub[:, tile_step * part_rows : (tile_step + 1) * part_rows, :]
+        data = data.reshape(sub_count * part_rows, width)
+        step_ids = got_ids[:, tile_step * CAP_P : (tile_step + 1) * CAP_P]
+        messages.append(jnp.concatenate([data, id_rows(step_ids, width)], axis=0))
+    devices = range(tile_count)
+    received = [
+        lax.ppermute(messages[0], "tile", [(i, (i - 1) % tile_count) for i in devices]),
+        messages[1],
+        lax.ppermute(messages[2], "tile", [(i, (i + 1) % tile_count) for i in devices]),
+    ]
+    message_rows = sub_count * part_rows
+    data = jnp.concatenate([m[:message_rows] for m in received], axis=0)
+    slot_ids = jnp.concatenate([m[message_rows, : sub_count * CAP_P] for m in received])
+    selector = (slot_ids[None, :] == jnp.arange(LB_DEV, dtype=jnp.float32)[:, None]).astype(jnp.float32)
+    data = data.reshape(slot_ids.shape[0], field_count, width)
+    return jnp.einsum("bs,sfl->fbl", selector, data, precision=lax.Precision.HIGHEST)
 
 
 def on_device(
@@ -202,11 +216,8 @@
     picked = stacked[:, pair_atm, :]
     weights = pair_weight.reshape(pair_count, 3 * row_width, LBLK)
     partial_value = jnp.einsum("fpk,pkl->pfl", picked, weights, preferred_element_type=jnp.float32)
-    flat_terms = partial_value.reshape(pair_count, field_count * LBLK)
-    owned_sums = route_partials(flat_terms, pair_land, tile_count, sub_count, tile_index, sub_index)
-    forcing = owned_sums.reshape(LB_DEV, field_count, LBLK).transpose(1, 0, 2).reshape(
-        field_count, LB_DEV * LBLK
-    )
+    owned_sums = route_partials(partial_value, pair_land, tile_count, sub_count, tile_index)
+    forcing = owned_sums.reshape(field_count, LB_DEV * LBLK)
     land_forcing = forcing.astype(jnp.bfloat16)
     moisture, runoff = soil_update(forcing, land_mask, conductance, soil_moisture)
     block_count = runoff.shape[0] // RBLK

time: 82.5 us -> 79.3 us (0.961)
  local copies, waits for them, and re-layouts: 17.3 us -> 11.6 us
  waiting for transfers between devices: 8.59 us -> 13.7 us
  starting transfers between devices: 33.3 us -> 29.6 us
  other arithmetic: 9.77 us -> 10.7 us
    ppermute x11 -> x2, starting transfers between devices: 22.1 us -> 8.89 us  [the longest x1 5.8 us: route_partials(): lax.ppermute(messages[2], 'tile', [(i, (i + 1) % tile_count) for i in dev...]
    all_to_all x1, starting transfers between devices: 7.2 us -> 13.2 us  [on_device(): lax.all_to_all(packed, 'tile', split_axis=0, concat_axis=0, tiled=True)]
    all_to_all x0 -> x1, waiting for transfers between devices: none -> 4.66 us  [route_partials(): lax.all_to_all(chunks, 'sub', split_axis=0, concat_axis=0, tiled=True)]
    another operation x12 -> x4, local copies, waits for them, and re-layouts: 3.74 us -> 0.02 us  [route_partials(): jnp.stack([id_rows(ids[j], width) for j in range(sub_count)])]
    all_to_all x0 -> x1, starting transfers between devices: none -> 3.48 us  [route_partials(): lax.all_to_all(chunks, 'sub', split_axis=0, concat_axis=0, tiled=True)]
    slice x3 -> x6, local copies, waits for them, and re-layouts: 1.5 us -> 0.22 us  [the longest x1 0.08 us: route_partials(): step_ids = got_ids[:, tile_step * CAP_P:(tile_step + 1) * CAP_P]]
    concatenate x1 -> x5, other arithmetic: 0.06 us -> 1.04 us  [the longest x1 0.89 us: route_partials(): jnp.concatenate([rows.reshape(sub_count, chunk_rows, width), jnp.stack([i...]
    ppermute x11 -> x2, waiting for transfers between devices: 1.54 us -> 2.13 us  [the longest x1 1.49 us: route_partials(): lax.ppermute(messages[0], 'tile', [(i, (i - 1) % tile_count) for i in dev...]
  transfers between devices with their start and end apart: 14 -> 6, of which waited for: 3 -> 4; matrix products, arithmetic and copies ran while one was open for 19% -> 19% of each run, Pallas kernels for 0% -> 0%
where the time goes in v3:
time: 79.3 us; the launch traced here: 78.7 us
  starting transfers between devices  29.6 us (37%)
  waiting for transfers between devices  13.7 us (17%)
  local copies, waits for them, and re-layouts  11.6 us (15%)
  other arithmetic  10.7 us (13%)
  matrix products  6.14 us (8%)
  Pallas kernels  5.93 us (7%)
  between operations  1.02 us (1%)
    all_to_all x1, starting transfers between devices, on_device(): lax.all_to_all(packed, 'tile', split_axis=0, concat_axis=0, tiled=True)  13.2 us
    all_to_all x1, waiting for transfers between devices, on_device(): lax.all_to_all(packed, 'tile', split_axis=0, concat_axis=0, tiled=True)  6.94 us
    pallas_call x1, Pallas kernels, soil_update(): pl.pallas_call(soil_kernel, grid=(grid,), in_specs=[plane, plane, plane,...  5.93 us
    ppermute x1, starting transfers between devices, route_partials(): lax.ppermute(messages[2], 'tile', [(i, (i + 1) % tile_count) for i in dev...  5.8 us
    all_to_all x1, waiting for transfers between devices, route_partials(): lax.all_to_all(chunks, 'sub', split_axis=0, concat_axis=0, tiled=True)  4.66 us
    dot_general x1, matrix products, on_device(): jnp.einsum('fpk,pkl->pfl', picked, weights, preferred_element_type=jnp.fl...  4.42 us
    unnamed x16, local copies, waits for them, and re-layouts  4.26 us
    all_to_all x1, starting transfers between devices, route_partials(): lax.all_to_all(chunks, 'sub', split_axis=0, concat_axis=0, tiled=True)  3.48 us
  transfers between devices with their start and end apart: 6, of which 4 were waited for; matrix products, arithmetic and copies ran while one was open for 19% of the time, Pallas kernels for 0%

profile of v3, /device:TPU:1, one launch (start us, length us, event | category | flops | bytes accessed | tf_op | source)
XLA Modules:
  0.0 78.7 jit_solution(16968128685050221845)
XLA Ops:
  0.6 0.8 %fusion.34 = (f32[6,1,128]{2,1,0:T(1,128)S(1)}, f32[6,1,128]{2,1,0:T(1,128)S(1)}) fusion(f32[6,8,128]{2,1,0:T(8,128)} %param.8), kind=kLoop, calls=%fused_computation.97 | loop fusion | bytes 12288 | tf_op jit(solution)/shard_map/slice | solution.py:26
  1.5 2.0 %collective-permute-start.1 = (f32[6,1,128]{2,1,0:T(1,128)S(1)}, f32[6,1,128]{2,1,0:T(1,128)S(1)}, u32[]{:S(2)}, u32[]{:S(2)}) collective-permute-start(f32[6,1,128]{2,1,0:T(1,128)S(1)} %get-tuple-element.24), channel_id=1, source_target_pairs={{0,1},{1,2},{2,3},{3,4},{4,5},{5,6},{6,7},{7,8},{8,9},{9,10},{10,1... | collective-permute-start | bytes 9224 | tf_op jit(solution)/shard_map/ppermute | solution.py:27
  3.5 1.9 %collective-permute-start = (f32[6,1,128]{2,1,0:T(1,128)S(1)}, f32[6,1,128]{2,1,0:T(1,128)S(1)}, u32[]{:S(2)}, u32[]{:S(2)}) collective-permute-start(f32[6,1,128]{2,1,0:T(1,128)S(1)} %get-tuple-element.23), channel_id=1, source_target_pairs={{1,0},{2,1},{3,2},{4,3},{5,4},{6,5},{7,6},{8,7},{9,8},{10,9},{11,1... | collective-permute-start | bytes 9224 | tf_op jit(solution)/shard_map/ppermute | solution.py:28
  5.4 1.0 %subtract_convert_fusion = (bf16[6,8,1]{2,1,0:T(8,128)(2,1)S(1)}, bf16[6,8,1]{2,1,0:T(8,128)(2,1)S(1)}) fusion(f32[6,8,128]{2,1,0:T(8,128)} %param.8), kind=kLoop, calls=%fused_computation.47 | loop fusion | flops 192 | bytes 960 | tf_op jit(solution)/shard_map/convert.3
  6.4 0.9 %multiply_convert_fusion = bf16[6,8,126]{2,1,0:T(8,128)(2,1)S(1)} fusion(f32[6,8,128]{2,1,0:T(8,128)} %param.8), kind=kLoop, calls=%fused_computation.48 | loop fusion | flops 18144 | bytes 60480 | tf_op jit(solution)/shard_map/convert.2
  7.3 0.7 fusion.27
  8.1 0.2 select_reduce_fusion.3
  8.3 0.7 iota_add_fusion
  9.1 1.4 %gather_fusion.2 = s32[48]{0:T(128)S(1)} fusion(s32[20]{0:T(128)} %param.10, s32[1024]{0:T(1024)S(1)} %pad_clamp_fusion), kind=kCustom, calls=%fused_computation.2 | custom fusion | bytes 576 | tf_op jit(solution)/shard_map/gather | solution.py:170
  10.6 0.7 compare_select_fusion.2
  11.3 0.7 fusion.17
  12.0 0.1 reduce_window_sum.23
  12.1 0.8 %select_reduce_fusion.1 = s32[64]{0:T(128)S(1)} fusion(s32[64,64]{1,0:T(8,128)S(1)} %reduce_window_sum.23, s32[64]{0:T(128)} %param.15), kind=kLoop, calls=%fused_computation.37 | loop fusion | flops 20416 | bytes 16896 | tf_op jit(solution)/shard_map/reduce_sum | solution.py:229
  12.9 0.7 add_add_fusion
  13.9 0.1 broadcast_in_dim.66
  14.0 0.9 %fusion.20 = (bf16[6,8,128]{2,1,0:T(8,128)(2,1)S(1)}, bf16[6,8,128]{2,1,0:T(8,128)(2,1)S(1)}) fusion(f32[6,8,128]{2,1,0:T(8,128)} %param.8, f32[6,1,128]{2,1,0:T(1,128)S(1)} %collective-permute-done.1, f32[6,1,128]{2,1,0:T(1,128)S(1)} %collective-permute-done), kind=kLoop, calls=%fused_computation.45 | loop fusion | flops 36864 | bytes 55296 | tf_op jit(solution)/shard_map/convert.4
  14.9 0.1 concatenate.31
  15.0 0.6 gather_fusion
  15.6 4.4 %fusion.1 = f32[20,6,512]{2,1,0:T(8,128)S(1)} fusion(bf16[20,384,512]{2,1,0:T(8,128)(2,1)} %bitcast.55, bf16[20,6,384]{2,1,0:T(8,128)(2,1)S(1)} %gather_fusion), kind=kOutput, calls=%fused_computation.10 | convolution fusion | flops 47185920 | bytes 8202240 | tf_op jit(solution)/shard_map/fpk,pkl->pfl/dot_general | solution.py:218
  20.0 0.6 gather_fusion.1
  20.7 0.1 broadcast_select_fusion
  20.8 0.9 %maximum_maximum_fusion = f32[4,80,512]{2,1,0:T(8,128)} fusion(f32[1,8,512]{2,1,0:T(8,128)S(1)} %stack_reshape.15, f32[1,8,512]{2,1,0:T(8,128)S(1)} %stack_reshape.14, f32[1,8,512]{2,1,0:T(8,128)S(1)} %stack_reshape.13, f32[1,8,512]{2,1,0:T(8,128)S(1)} %stack_reshape.12, f32[4,72,512]{2,1,0:T(8,128)S(1)} %broadcast_select_fusion), kind=kLoop, calls=%fused_computation.4 | loop fusion | flops 655360 | bytes 1310720 | tf_op jit(solution)/shard_map/concatenate | solution.py:173
  21.7 3.5 %all-to-all-start = ((f32[4,80,512]{2,1,0:T(8,128)}), f32[4,80,512]{2,1,0:T(8,128)S(1)}, u32[]{:S(2)}, u32[]{:S(2)}) async-start(f32[4,80,512]{2,1,0:T(8,128)} %maximum_maximum_fusion), calls=%async_computation | async-start | bytes 1310720 | tf_op jit(solution)/shard_map/all_to_all | solution.py:180
  25.2 0.1 select_reduce_fusion
  25.3 0.1 copy.71
  25.5 0.9 %slice.161.cond_ref = f32[20,64,128]{2,1,0:T(8,128)} slice(f32[24,64,128]{2,1,0:T(8,128)S(1)} %bitcast.57), slice={[0:20], [0:64], [0:128]} | slice | bytes 1310720 | tf_op jit(solution)/shard_map/reshape | solution.py:139
  26.4 0.1 copy.72
  26.5 0.9 %slice.162.moist_ref = f32[20,64,128]{2,1,0:T(8,128)} slice(f32[24,64,128]{2,1,0:T(8,128)S(1)} %bitcast.58), slice={[0:20], [0:64], [0:128]} | slice | bytes 1310720 | tf_op jit(solution)/shard_map/reshape | solution.py:140
  27.4 0.1 convert_element_type.49
  27.5 0.6 convert_bitcast_fusion.1.wet_ref
  28.2 4.7 %all-to-all-done = f32[4,80,512]{2,1,0:T(8,128)S(1)} async-done(((f32[4,80,512]{2,1,0:T(8,128)}), f32[4,80,512]{2,1,0:T(8,128)S(1)}, u32[]{:S(2)}, u32[]{:S(2)}) %all-to-all-start) | async-done | bytes 655392 | tf_op jit(solution)/shard_map/all_to_all | solution.py:180
  33.1 5.8 %collective-permute-start.3 = (f32[104,512]{1,0:T(8,128)S(1)}, f32[104,512]{1,0:T(8,128)S(1)}, u32[]{:S(2)}, u32[]{:S(2)}) collective-permute-start(f32[104,512]{1,0:T(8,128)S(1)} %pad_maximum_fusion.2), channel_id=1, source_target_pairs={{0,4},{4,8},{8,12},{12,16},{16,20},{20,24},{24,28},{28,32},{32,36}... | collective-permute-start | bytes 638984 | tf_op jit(solution)/shard_map/ppermute | solution.py:193
  39.0 3.1 %collective-permute-start.2 = (f32[104,512]{1,0:T(8,128)S(1)}, f32[104,512]{1,0:T(8,128)S(1)}, u32[]{:S(2)}, u32[]{:S(2)}) collective-permute-start(f32[104,512]{1,0:T(8,128)S(1)} %pad_maximum_fusion.1), channel_id=1, source_target_pairs={{0,252},{4,0},{8,4},{12,8},{16,12},{20,16},{24,20},{28,24},{32,28}... | collective-permute-start | bytes 638984 | tf_op jit(solution)/shard_map/ppermute | solution.py:191
  42.2 0.6 collective-permute-done.3
  42.9 1.5 %collective-permute-done.2 = f32[104,512]{1,0:T(8,128)S(1)} collective-permute-done((f32[104,512]{1,0:T(8,128)S(1)}, f32[104,512]{1,0:T(8,128)S(1)}, u32[]{:S(2)}, u32[]{:S(2)}) %collective-permute-start.2) | collective-permute-done | bytes 213024 | tf_op jit(solution)/shard_map/ppermute | solution.py:191
  44.6 0.6 convolution_bitcast_fusion
  45.4 0.7 multiply_bitcast_fusion
  46.0 5.9 %shard_map.111 = (f32[20,64,128]{2,1,0:T(8,128)}, f32[64,128]{1,0:T(8,128)}) custom-call(f32[64,128]{1,0:T(8,128)} %get-tuple-element.20.source_ref, f32[64,128]{1,0:T(8,128)} %get-tuple-element.19.surface_ref, f32[64,128]{1,0:T(8,128)} %convert_bitcast_fusion.1.wet_ref, f32[20,64,128]{2,1,0:T(8,128)} %slice.161.cond_ref, f32[20,64,128]{2,1,0:T(8,128)} %slice.162.moist_ref), custom_call_target="tpu_custom_call" | custom-call | tf_op jit(solution)/shard_map/pallas_call | solution.py:126
  52.0 1.1 %fusion.16 = f32[128,128]{1,0:T(8,128)S(1)} fusion(f32[64,128]{1,0:T(8,128)} %get-tuple-element.7, s32[64]{0:T(128)S(1)} %get-tuple-element.37), kind=kOutput, calls=%fused_computation.36 | convolution fusion | flops 12591104 | bytes 98560 | tf_op jit(solution)/shard_map/dot_general | solution.py:232
  53.1 0.7 all_to_all.12
  53.8 13.2 %all-to-all-start.1 = ((f32[64,1,384]{2,1,0:T(1,128)}), f32[64,1,384]{2,1,0:T(1,128)S(1)}, u32[]{:S(2)}, u32[]{:S(2)}) async-start(f32[64,1,384]{2,1,0:T(1,128)} %all_to_all.12), calls=%async_computation.1 | async-start | bytes 196608 | tf_op jit(solution)/shard_map/all_to_all | solution.py:241
  67.0 0.7 copy.66
  67.8 1.2 %pad.64 = f32[24,64,128]{2,1,0:T(8,128)S(1)} pad(f32[20,64,128]{2,1,0:T(8,128)} %get-tuple-element.6, f32[]{:T(128)} %constant.108.clone.1), padding=0_4x0_0x0_0 | pad | bytes 1441796
  68.9 1.3 %copy.73 = f32[3,8,64,128]{3,1,2,0:T(8,128)} copy(f32[3,8,64,128]{3,2,1,0:T(8,128)S(1)} %bitcast.56) | data formatting | bytes 1572864
  70.3 6.9 %all-to-all-done.1 = f32[64,1,384]{2,1,0:T(1,128)S(1)} async-done(((f32[64,1,384]{2,1,0:T(1,128)}), f32[64,1,384]{2,1,0:T(1,128)S(1)}, u32[]{:S(2)}, u32[]{:S(2)}) %all-to-all-start.1) | async-done | bytes 98336 | tf_op jit(solution)/shard_map/all_to_all | solution.py:241
  77.2 0.1 copy.64
  77.4 0.6 fusion.26
  77.9 0.7 copy.65
  (61 shorter events, 1.4 us)
Async XLA Ops:
  1.5 12.5 %collective-permute-start.1 = (f32[6,1,128]{2,1,0:T(1,128)S(1)}, f32[6,1,128]{2,1,0:T(1,128)S(1)}, u32[]{:S(2)}, u32[]{:S(2)}) collective-permute-start(f32[6,1,128]{2,1,0:T(1,128)S(1)} %get-tuple-element.24), channel_id=1, source_target_pairs={{0,1},{1,2},{2,3},{3,4},{4,5},{5,6},{6,7},{7,8},{8,9},{9,10},{10,1... | collective-permute-start | bytes 9224 | tf_op jit(solution)/shard_map/ppermute | solution.py:27
  3.5 10.5 %collective-permute-start = (f32[6,1,128]{2,1,0:T(1,128)S(1)}, f32[6,1,128]{2,1,0:T(1,128)S(1)}, u32[]{:S(2)}, u32[]{:S(2)}) collective-permute-start(f32[6,1,128]{2,1,0:T(1,128)S(1)} %get-tuple-element.23), channel_id=1, source_target_pairs={{1,0},{2,1},{3,2},{4,3},{5,4},{6,5},{7,6},{8,7},{9,8},{10,9},{11,1... | collective-permute-start | bytes 9224 | tf_op jit(solution)/shard_map/ppermute | solution.py:28
  15.6 9.8 %copy-start = (f32[20,8192]{1,0:T(8,128)S(1)}, f32[20,8192]{1,0:T(8,128)}, u32[]{:S(2)}) copy-start(f32[20,8192]{1,0:T(8,128)} %param.13) | copy-start | bytes 1966084
  20.0 6.4 %copy-start.1 = (f32[20,8192]{1,0:T(8,128)S(1)}, f32[20,8192]{1,0:T(8,128)}, u32[]{:S(2)}) copy-start(f32[20,8192]{1,0:T(8,128)} %param.14) | copy-start | bytes 1966084
  20.0 7.5 %copy-start.2 = (s32[8192]{0:T(1024)S(1)}, s32[8192]{0:T(1024)}, u32[]{:S(2)}) copy-start(s32[8192]{0:T(1024)} %param.12) | copy-start | bytes 98308
  21.7 11.1 %all-to-all-start = ((f32[4,80,512]{2,1,0:T(8,128)}), f32[4,80,512]{2,1,0:T(8,128)S(1)}, u32[]{:S(2)}, u32[]{:S(2)}) async-start(f32[4,80,512]{2,1,0:T(8,128)} %maximum_maximum_fusion), calls=%async_computation | async-start | bytes 1310720 | tf_op jit(solution)/shard_map/all_to_all | solution.py:180
  33.1 9.8 %collective-permute-start.3 = (f32[104,512]{1,0:T(8,128)S(1)}, f32[104,512]{1,0:T(8,128)S(1)}, u32[]{:S(2)}, u32[]{:S(2)}) collective-permute-start(f32[104,512]{1,0:T(8,128)S(1)} %pad_maximum_fusion.2), channel_id=1, source_target_pairs={{0,4},{4,8},{8,12},{12,16},{16,20},{20,24},{24,28},{28,32},{32,36}... | collective-permute-start | bytes 638984 | tf_op jit(solution)/shard_map/ppermute | solution.py:193
  39.0 5.3 %collective-permute-start.2 = (f32[104,512]{1,0:T(8,128)S(1)}, f32[104,512]{1,0:T(8,128)S(1)}, u32[]{:S(2)}, u32[]{:S(2)}) collective-permute-start(f32[104,512]{1,0:T(8,128)S(1)} %pad_maximum_fusion.1), channel_id=1, source_target_pairs={{0,252},{4,0},{8,4},{12,8},{16,12},{20,16},{24,20},{28,24},{32,28}... | collective-permute-start | bytes 638984 | tf_op jit(solution)/shard_map/ppermute | solution.py:191
  53.8 23.4 %all-to-all-start.1 = ((f32[64,1,384]{2,1,0:T(1,128)}), f32[64,1,384]{2,1,0:T(1,128)S(1)}, u32[]{:S(2)}, u32[]{:S(2)}) async-start(f32[64,1,384]{2,1,0:T(1,128)} %all_to_all.12), calls=%async_computation.1 | async-start | bytes 196608 | tf_op jit(solution)/shard_map/all_to_all | solution.py:241

commit v4 on v3

--- a/solution.py
+++ b/solution.py
@@ -110,36 +110,38 @@
     lax.fori_loop(0, groups, one_group, 0)
 
 
-def soil_update(forcing, land_mask, conductance, soil_moisture):
-    wetness = land_mask.astype(jnp.float32)
+def soil_inputs(forcing, wetness):
     source = wetness * (
         jax.nn.softplus(forcing[0]) * jax.nn.sigmoid(forcing[1])
         - 0.5 * jax.nn.sigmoid(forcing[2]) * jax.nn.softplus(forcing[3])
     )
     surface = wetness * jax.nn.softplus(forcing[0]) * (1.0 - jax.nn.sigmoid(forcing[1]))
-    layers, cells = conductance.shape
-    rows = cells // 128
+    return (source, surface)
+
+
+def soil_update(source, surface, wetness, conductance, soil_moisture):
+    layers, rows, lanes = conductance.shape
     grid = 2
     block = rows // grid
-    plane = pl.BlockSpec((block, 128), lambda i: (i, 0))
-    stack = pl.BlockSpec((layers, block, 128), lambda i: (0, i, 0))
+    plane = pl.BlockSpec((block, lanes), lambda i: (i, 0))
+    stack = pl.BlockSpec((layers, block, lanes), lambda i: (0, i, 0))
     moisture, runoff = pl.pallas_call(
         soil_kernel,
         grid=(grid,),
         in_specs=[plane, plane, plane, stack, stack],
         out_specs=[stack, plane],
         out_shape=[
-            jax.ShapeDtypeStruct((layers, rows, 128), jnp.float32),
-            jax.ShapeDtypeStruct((rows, 128), jnp.float32),
+            jax.ShapeDtypeStruct((layers, rows, lanes), jnp.float32),
+            jax.ShapeDtypeStruct((rows, lanes), jnp.float32),
         ],
     )(
-        source.reshape(rows, 128),
-        surface.reshape(rows, 128),
-        wetness.reshape(rows, 128),
-        conductance.reshape(layers, rows, 128),
-        soil_moisture.reshape(layers, rows, 128),
-    )
-    return (moisture.reshape(layers, cells), runoff.reshape(cells))
+        source.reshape(rows, lanes),
+        surface.reshape(rows, lanes),
+        wetness,
+        conductance,
+        soil_moisture,
+    )
+    return (moisture.reshape(layers, rows * lanes), runoff.reshape(rows * lanes))
 
 
 CAP_P = 4
@@ -151,8 +153,8 @@
     return jnp.pad(flat, (0, 8 * width - flat.shape[0])).reshape(8, width)
 
 
-def route_partials(partial_value, pair_land, tile_count, sub_count, tile_index):
-    pair_count, field_count, width = partial_value.shape
+def slot_plan(pair_land, tile_count, sub_count, tile_index):
+    pair_count = pair_land.shape[0]
     owner_device = pair_land // LB_DEV
     tile_step = (owner_device // sub_count - tile_index + 1 + tile_count) % tile_count
     dest_sub = owner_device % sub_count
@@ -166,8 +168,14 @@
     source = jnp.sum(jnp.where(placing, jnp.arange(pair_count, dtype=jnp.int32)[None, :] + 1, 0), axis=1) - 1
     filled = source >= 0
     picked = jnp.maximum(source, 0)
+    ids = jnp.where(filled, pair_land[picked] % LB_DEV, -1).astype(jnp.float32)
+    return (filled, picked, ids)
+
+
+def route_partials(partial_value, plan, sub_count, tile_count):
+    filled, picked, ids = plan
+    pair_count, field_count, width = partial_value.shape
     rows = jnp.where(filled[:, None, None], partial_value[picked], 0.0)
-    ids = jnp.where(filled, pair_land[picked] % LB_DEV, -1).astype(jnp.float32)
     chunk_rows = 3 * CAP_P * field_count
     ids = ids.reshape(sub_count, 3 * CAP_P)
     chunks = jnp.concatenate(
@@ -208,35 +216,61 @@
     tile_index = lax.axis_index("tile")
     sub_index = lax.axis_index("sub")
     field_count, row_count, row_width = atm_fields.shape
-    extended = padded(atm_fields, ((("tile", "sub"), 1),), 1)
-    grad_x = x_gradient(atm_fields)
-    grad_y = (extended[:, 2:, :] - extended[:, :-2, :]) * 0.5
-    stacked = jnp.concatenate([atm_fields, grad_x, grad_y], axis=2).astype(jnp.bfloat16)
     pair_count = pair_atm.shape[0]
-    picked = stacked[:, pair_atm, :]
+    layers, cell_count = conductance.shape
+    tiles = (cell_count // RBLK, RBLK)
+
+    plain = jnp.concatenate([atm_fields, x_gradient(atm_fields)], axis=2).astype(jnp.bfloat16)
     weights = pair_weight.reshape(pair_count, 3 * row_width, LBLK)
-    partial_value = jnp.einsum("fpk,pkl->pfl", picked, weights, preferred_element_type=jnp.float32)
-    owned_sums = route_partials(partial_value, pair_land, tile_count, sub_count, tile_index)
-    forcing = owned_sums.reshape(field_count, LB_DEV * LBLK)
-    land_forcing = forcing.astype(jnp.bfloat16)
-    moisture, runoff = soil_update(forcing, land_mask, conductance, soil_moisture)
-    block_count = runoff.shape[0] // RBLK
+    partial_plain = jnp.einsum(
+        "fpk,pkl->pfl",
+        plain[:, pair_atm, :],
+        weights[:, : 2 * row_width, :],
+        preferred_element_type=jnp.float32,
+    )
+    plan = slot_plan(pair_land, tile_count, sub_count, tile_index)
+    wetness = land_mask.astype(jnp.float32).reshape(tiles)
+    cond_tiles = conductance.reshape((layers,) + tiles)
+    moist_tiles = soil_moisture.reshape((layers,) + tiles)
+
+    block_count = cell_count // RBLK
     capacity = CAP_R
-    runoff_blocks = runoff.reshape(block_count, RBLK)
     hits = (river_owner[:, None] == jnp.arange(tile_count, dtype=jnp.int32)[None, :]).astype(
         jnp.int32
     )
     ranks = jnp.sum((jnp.cumsum(hits, axis=0) - hits) * hits, axis=1)
     slot_id = river_owner * capacity + ranks
     placing = slot_id[None, :] == jnp.arange(tile_count * capacity, dtype=jnp.int32)[:, None]
-    values = jnp.dot(placing.astype(jnp.float32), runoff_blocks, precision=lax.Precision.HIGHEST)
-    values = values.reshape(tile_count, capacity * RBLK)
+    placing_f = placing.astype(jnp.float32)
     block_ids = (tile_index * sub_count + sub_index) * block_count + jnp.arange(
         block_count, dtype=jnp.int32
     )
     numbers = jnp.sum(jnp.where(placing, block_ids[None, :] + 1, 0), axis=1) - 1
     numbers = numbers.astype(jnp.float32).reshape(tile_count, capacity)
     numbers = jnp.pad(numbers, ((0, 0), (0, RBLK - capacity)))
+
+    (atm_fields, partial_plain, plan, wetness, cond_tiles, moist_tiles, placing_f, numbers) = (
+        lax.optimization_barrier(
+            (atm_fields, partial_plain, plan, wetness, cond_tiles, moist_tiles, placing_f, numbers)
+        )
+    )
+
+    extended = padded(atm_fields, ((("tile", "sub"), 1),), 1)
+    grad_y = ((extended[:, 2:, :] - extended[:, :-2, :]) * 0.5).astype(jnp.bfloat16)
+    partial_value = partial_plain + jnp.einsum(
+        "fpk,pkl->pfl",
+        grad_y[:, pair_atm, :],
+        weights[:, 2 * row_width :, :],
+        preferred_element_type=jnp.float32,
+    )
+    owned_sums = route_partials(partial_value, plan, sub_count, tile_count)
+    forcing = owned_sums.reshape(field_count, LB_DEV * LBLK)
+    land_forcing = forcing.astype(jnp.bfloat16)
+    source, surface = soil_inputs(forcing, wetness.reshape(cell_count))
+    moisture, runoff = soil_update(source, surface, wetness, cond_tiles, moist_tiles)
+    runoff_blocks = runoff.reshape(block_count, RBLK)
+    values = jnp.dot(placing_f, runoff_blocks, precision=lax.Precision.HIGHEST)
+    values = values.reshape(tile_count, capacity * RBLK)
     packed = jnp.concatenate([values, numbers], axis=1)
     got = lax.all_to_all(packed, "tile", split_axis=0, concat_axis=0, tiled=True)
     river_runoff = got[:, : capacity * RBLK].reshape(tile_count, capacity, RBLK)[None, None]

time: 79.3 us -> 89.6 us (1.13)
  blocking collectives: 0 us -> 10 us
  starting transfers between devices: 29.6 us -> 27.5 us
  local copies, waits for them, and re-layouts: 11.6 us -> 13.5 us
  matrix products: 6.14 us -> 7.15 us
    all_to_all x0 -> x1, blocking collectives: none -> 10 us  [route_partials(): lax.all_to_all(chunks, 'sub', split_axis=0, concat_axis=0, tiled=True)]
    ppermute x1, starting transfers between devices: 3.09 us -> 13 us  [route_partials(): lax.ppermute(messages[0], 'tile', [(i, (i - 1) % tile_count) for i in dev...]
    ppermute x1, starting transfers between devices: 5.8 us -> 0.08 us  [route_partials(): lax.ppermute(messages[2], 'tile', [(i, (i + 1) % tile_count) for i in dev...]
    all_to_all x1 -> x0, waiting for transfers between devices: 4.66 us -> none  [route_partials(): lax.all_to_all(chunks, 'sub', split_axis=0, concat_axis=0, tiled=True)]
    ppermute x1, waiting for transfers between devices: 0.01 us -> 3.49 us  [padded(): before = lax.ppermute(last, axis, up)]
    all_to_all x1 -> x0, starting transfers between devices: 3.48 us -> none  [route_partials(): lax.all_to_all(chunks, 'sub', split_axis=0, concat_axis=0, tiled=True)]
    all_to_all x1, starting transfers between devices: 13.2 us -> 10.4 us  [on_device(): lax.all_to_all(packed, 'tile', split_axis=0, concat_axis=0, tiled=True)]
    unnamed x16 -> x10, local copies, waits for them, and re-layouts: 4.26 us -> 6.48 us
  transfers between devices with their start and end apart: 6 -> 5, of which waited for: 4 -> 5; matrix products, arithmetic and copies ran while one was open for 19% -> 4% of each run, Pallas kernels for 0% -> 0%
where the time goes in v4:
time: 89.6 us; the launch traced here: 88.7 us
  starting transfers between devices  27.5 us (31%)
  local copies, waits for them, and re-layouts  13.5 us (15%)
  waiting for transfers between devices  13.5 us (15%)
  other arithmetic  10 us (11%)
  blocking collectives  10 us (11%)
  matrix products  7.15 us (8%)
  Pallas kernels  5.96 us (7%)
  between operations  1.03 us (1%)
    ppermute x1, starting transfers between devices, route_partials(): lax.ppermute(messages[0], 'tile', [(i, (i - 1) % tile_count) for i in dev...  13 us
    all_to_all x1, starting transfers between devices, on_device(): lax.all_to_all(packed, 'tile', split_axis=0, concat_axis=0, tiled=True)  10.4 us
    all_to_all x1, blocking collectives, route_partials(): lax.all_to_all(chunks, 'sub', split_axis=0, concat_axis=0, tiled=True)  10 us
    all_to_all x1, waiting for transfers between devices, on_device(): lax.all_to_all(packed, 'tile', split_axis=0, concat_axis=0, tiled=True)  7.05 us
    unnamed x10, local copies, waits for them, and re-layouts  6.48 us
    pallas_call x1, Pallas kernels, soil_update(): pl.pallas_call(soil_kernel, grid=(grid,), in_specs=[plane, plane, plane,...  5.96 us
    ppermute x1, starting transfers between devices, padded(): after = lax.ppermute(initial, axis, down)  3.95 us
    ppermute x1, waiting for transfers between devices, padded(): before = lax.ppermute(last, axis, up)  3.49 us
  transfers between devices with their start and end apart: 5, of which 5 were waited for; matrix products, arithmetic and copies ran while one was open for 4% of the time, Pallas kernels for 0%

profile of v4, /device:TPU:1, one launch (start us, length us, event | category | flops | bytes accessed | tf_op | source)
XLA Modules:
  0.0 88.7 jit_solution(3160945307452048696)
XLA Ops:
  0.6 0.7 fusion.30
  1.4 0.2 select_reduce_fusion.3
  1.6 0.7 iota_add_fusion
  2.3 0.1 select_reduce_fusion.2
  2.4 1.0 %subtract_convert_fusion.1 = (bf16[6,8,1]{2,1,0:T(8,128)(2,1)S(1)}, bf16[6,8,1]{2,1,0:T(8,128)(2,1)S(1)}) fusion(f32[6,8,128]{2,1,0:T(8,128)} %param.8), kind=kLoop, calls=%fused_computation.50 | loop fusion | flops 192 | bytes 960 | tf_op jit(solution)/shard_map/convert.1
  3.4 0.7 convert.12
  4.2 0.9 %multiply_convert_fusion = bf16[6,8,126]{2,1,0:T(8,128)(2,1)S(1)} fusion(f32[6,8,128]{2,1,0:T(8,128)} %param.8), kind=kLoop, calls=%fused_computation.49 | loop fusion | flops 18144 | bytes 60480 | tf_op jit(solution)/shard_map/convert.2
  5.1 1.4 %gather_fusion.1 = s32[48]{0:T(128)S(1)} fusion(s32[20]{0:T(128)} %param.10, s32[1024]{0:T(1024)S(1)} %pad_clamp_fusion.1), kind=kCustom, calls=%fused_computation.1 | custom fusion | bytes 576 | tf_op jit(solution)/shard_map/gather | solution.py:171
  6.5 0.7 fusion.24
  7.2 0.1 reduce_window_sum.23
  7.3 0.8 select_reduce_fusion.1
  8.2 0.7 add_add_fusion
  8.9 0.1 select_reduce_fusion
  9.0 0.1 convert_element_type.53
  9.3 0.7 compare_select_fusion.3
  9.9 1.3 %copy.71 = f32[3,8,64,128]{3,2,1,0:T(8,128)S(1)} copy(f32[3,8,64,128]{3,1,2,0:T(8,128)} %bitcast.48) | data formatting | bytes 1572864
  11.2 0.9 slice.175.cond_ref
  12.1 1.3 %copy.72 = f32[3,8,64,128]{3,2,1,0:T(8,128)S(1)} copy(f32[3,8,64,128]{3,1,2,0:T(8,128)} %bitcast.49) | data formatting | bytes 1572864
  13.4 0.9 %slice.176.moist_ref = f32[20,64,128]{2,1,0:T(8,128)} slice(f32[24,64,128]{2,1,0:T(8,128)S(1)} %bitcast.46), slice={[0:20], [0:64], [0:128]} | slice | bytes 1310720 | tf_op jit(solution)/shard_map/reshape | solution.py:234
  14.3 0.8 convert_bitcast_fusion.1.wet_ref
  15.0 0.6 gather_fusion
  15.6 3.3 %fusion = f32[20,6,512]{2,1,0:T(8,128)S(1)} fusion(bf16[20,384,512]{2,1,0:T(8,128)(2,1)} %bitcast.42, bf16[20,6,256]{2,1,0:T(8,128)(2,1)S(1)} %gather_fusion), kind=kOutput, calls=%fused_computation.4 | convolution fusion | flops 31457280 | bytes 5550080 | tf_op jit(solution)/shard_map/fpk,pkl->pfl/dot_general | solution.py:225
  18.9 4.0 %collective-permute-start = (f32[6,1,128]{2,0,1:T(8,128)S(1)}, f32[6,1,128]{2,0,1:T(8,128)S(1)}, u32[]{:S(2)}, u32[]{:S(2)}) collective-permute-start(f32[6,1,128]{2,0,1:T(8,128)S(1)} %get-tuple-element.41), channel_id=1, source_target_pairs={{1,0},{2,1},{3,2},{4,3},{5,4},{6,5},{7,6},{8,7},{9,8},{10,9},{11,1... | collective-permute-start | bytes 9224 | tf_op jit(solution)/shard_map/ppermute | solution.py:28
  23.1 0.1 broadcast_in_dim.75
  23.3 0.3 collective-permute-done
  23.6 3.5 %collective-permute-done.1 = f32[6,1,128]{2,0,1:T(8,128)S(1)} collective-permute-done((f32[6,1,128]{2,0,1:T(8,128)S(1)}, f32[6,1,128]{2,0,1:T(8,128)S(1)}, u32[]{:S(2)}, u32[]{:S(2)}) %collective-permute-start.1) | collective-permute-done | bytes 3104 | tf_op jit(solution)/shard_map/ppermute | solution.py:27
  27.1 0.6 gather_fusion.2
  27.7 2.2 %fusion.4 = f32[20,6,512]{2,1,0:T(8,128)S(1)} fusion(f32[20,6,512]{2,1,0:T(8,128)S(1)} %fusion, bf16[20,384,512]{2,1,0:T(8,128)(2,1)} %bitcast.43, bf16[20,6,128]{2,1,0:T(8,128)(2,1)S(1)} %gather_fusion.2), kind=kOutput, calls=%fused_computation.8 | convolution fusion | flops 15790080 | bytes 3143680 | tf_op jit(solution)/shard_map/fpk,pkl->pfl/dot_general | solution.py:260
  29.9 0.6 gather_fusion.3
  30.5 0.1 gather.18
  30.6 0.1 broadcast_select_fusion
  30.8 10.0 %all_to_all.17 = f32[4,80,512]{2,1,0:T(8,128)S(1)} all-to-all(f32[4,80,512]{2,1,0:T(8,128)S(1)} %maximum_maximum_fusion), channel_id=1, replica_groups=mesh['tile'=64,'sub'=4] {'sub'}, dimensions={0} | all-to-all | bytes 1310720 | tf_op jit(solution)/shard_map/all_to_all | solution.py:188
  41.1 13.0 %collective-permute-start.2 = (f32[104,512]{1,0:T(8,128)S(1)}, f32[104,512]{1,0:T(8,128)S(1)}, u32[]{:S(2)}, u32[]{:S(2)}) collective-permute-start(f32[104,512]{1,0:T(8,128)S(1)} %pad_maximum_fusion.1), channel_id=1, source_target_pairs={{0,252},{4,0},{8,4},{12,8},{16,12},{20,16},{24,20},{28,24},{32,28}... | collective-permute-start | bytes 638984 | tf_op jit(solution)/shard_map/ppermute | solution.py:199
  54.4 0.8 collective-permute-done.2
  55.2 1.9 %collective-permute-done.3 = f32[104,512]{1,0:T(8,128)S(1)} collective-permute-done((f32[104,512]{1,0:T(8,128)S(1)}, f32[104,512]{1,0:T(8,128)S(1)}, u32[]{:S(2)}, u32[]{:S(2)}) %collective-permute-start.3) | collective-permute-done | bytes 213024 | tf_op jit(solution)/shard_map/ppermute | solution.py:201
  57.3 0.6 convolution_bitcast_fusion
  58.1 0.7 subtract_multiply_fusion
  58.8 6.0 %shard_map.111 = (f32[20,64,128]{2,1,0:T(8,128)}, f32[64,128]{1,0:T(8,128)}) custom-call(f32[64,128]{1,0:T(8,128)} %get-tuple-element.40.source_ref, f32[64,128]{1,0:T(8,128)} %get-tuple-element.39.surface_ref, f32[64,128]{1,0:T(8,128)} %copy-done.1, f32[20,64,128]{2,1,0:T(8,128)} %slice.175.cond_ref, f32[20,64,128]{2,1,0:T(8,128)} %slice.176.moist_ref), custom_call_target="tpu_custom_call" | custom-call | tf_op jit(solution)/shard_map/pallas_call | solution.py:128
  64.7 1.0 %fusion.41 = f32[128,128]{1,0:T(8,128)S(1)} fusion(f32[128,64]{0,1:T(8,128)S(1)} %fusion.23, f32[64,128]{1,0:T(8,128)} %get-tuple-element.26), kind=kOutput, calls=%fused_computation.103 | convolution fusion | flops 12582912 | bytes 131072 | tf_op jit(solution)/shard_map/dot_general | solution.py:272
  65.8 0.7 all_to_all.12
  66.5 10.4 %all-to-all-start.1 = ((f32[64,1,384]{2,1,0:T(1,128)}), f32[64,1,384]{2,1,0:T(1,128)S(1)}, u32[]{:S(2)}, u32[]{:S(2)}) async-start(f32[64,1,384]{2,1,0:T(1,128)} %all_to_all.12), calls=%async_computation.1 | async-start | bytes 196608 | tf_op jit(solution)/shard_map/all_to_all | solution.py:275
  77.0 1.2 %pad.68 = f32[24,64,128]{2,1,0:T(8,128)S(1)} pad(f32[20,64,128]{2,1,0:T(8,128)} %get-tuple-element.24, f32[]{:T(128)} %constant.110.clone.1), padding=0_4x0_0x0_0 | pad | bytes 1441796
  78.1 1.3 %copy.74 = f32[3,8,64,128]{3,1,2,0:T(8,128)} copy(f32[3,8,64,128]{3,2,1,0:T(8,128)S(1)} %bitcast.44) | data formatting | bytes 1572864
  79.5 0.7 copy.73
  80.2 7.1 %all-to-all-done.1 = f32[64,1,384]{2,1,0:T(1,128)S(1)} async-done(((f32[64,1,384]{2,1,0:T(1,128)}), f32[64,1,384]{2,1,0:T(1,128)S(1)}, u32[]{:S(2)}, u32[]{:S(2)}) %all-to-all-start.1) | async-done | bytes 98336 | tf_op jit(solution)/shard_map/all_to_all | solution.py:275
  87.3 0.1 copy.69
  87.4 0.6 fusion.29
  88.0 0.7 copy.70
  (66 shorter events, 1.6 us)
Async XLA Ops:
  0.6 18.2 %copy-start = (f32[6,8,128]{2,1,0:T(8,128)S(1)}, f32[6,8,128]{2,1,0:T(8,128)}, u32[]{:S(2)}) copy-start(f32[6,8,128]{2,1,0:T(8,128)} %param.8) | copy-start | bytes 73732
  15.0 43.1 %copy-start.1 = (f32[64,128]{1,0:T(8,128)}, f32[64,128]{1,0:T(8,128)S(1)}, u32[]{:S(2)}) copy-start(f32[64,128]{1,0:T(8,128)S(1)} %convert_bitcast_fusion.1.wet_ref) | copy-start | bytes 98308
  18.9 4.7 %collective-permute-start = (f32[6,1,128]{2,0,1:T(8,128)S(1)}, f32[6,1,128]{2,0,1:T(8,128)S(1)}, u32[]{:S(2)}, u32[]{:S(2)}) collective-permute-start(f32[6,1,128]{2,0,1:T(8,128)S(1)} %get-tuple-element.41), channel_id=1, source_target_pairs={{1,0},{2,1},{3,2},{4,3},{5,4},{6,5},{7,6},{8,7},{9,8},{10,9},{11,1... | collective-permute-start | bytes 9224 | tf_op jit(solution)/shard_map/ppermute | solution.py:28
  22.9 4.2 %collective-permute-start.1 = (f32[6,1,128]{2,0,1:T(8,128)S(1)}, f32[6,1,128]{2,0,1:T(8,128)S(1)}, u32[]{:S(2)}, u32[]{:S(2)}) collective-permute-start(f32[6,1,128]{2,0,1:T(8,128)S(1)} %get-tuple-element.42), channel_id=1, source_target_pairs={{0,1},{1,2},{2,3},{3,4},{4,5},{5,6},{6,7},{7,8},{8,9},{9,10},{10,1... | collective-permute-start | bytes 9224 | tf_op jit(solution)/shard_map/ppermute | solution.py:27
  41.1 14.1 %collective-permute-start.2 = (f32[104,512]{1,0:T(8,128)S(1)}, f32[104,512]{1,0:T(8,128)S(1)}, u32[]{:S(2)}, u32[]{:S(2)}) collective-permute-start(f32[104,512]{1,0:T(8,128)S(1)} %pad_maximum_fusion.1), channel_id=1, source_target_pairs={{0,252},{4,0},{8,4},{12,8},{16,12},{20,16},{24,20},{28,24},{32,28}... | collective-permute-start | bytes 638984 | tf_op jit(solution)/shard_map/ppermute | solution.py:199
  54.2 2.9 %collective-permute-start.3 = (f32[104,512]{1,0:T(8,128)S(1)}, f32[104,512]{1,0:T(8,128)S(1)}, u32[]{:S(2)}, u32[]{:S(2)}) collective-permute-start(f32[104,512]{1,0:T(8,128)S(1)} %pad_maximum_fusion.2), channel_id=1, source_target_pairs={{0,4},{4,8},{8,12},{12,16},{16,20},{20,24},{24,28},{28,32},{32,36}... | collective-permute-start | bytes 638984 | tf_op jit(solution)/shard_map/ppermute | solution.py:201
  66.5 20.7 %all-to-all-start.1 = ((f32[64,1,384]{2,1,0:T(1,128)}), f32[64,1,384]{2,1,0:T(1,128)S(1)}, u32[]{:S(2)}, u32[]{:S(2)}) async-start(f32[64,1,384]{2,1,0:T(1,128)} %all_to_all.12), calls=%async_computation.1 | async-start | bytes 196608 | tf_op jit(solution)/shard_map/all_to_all | solution.py:275

commit v5 on v3

--- a/solution.py
+++ b/solution.py
@@ -208,11 +208,18 @@
     tile_index = lax.axis_index("tile")
     sub_index = lax.axis_index("sub")
     field_count, row_count, row_width = atm_fields.shape
+    pair_count = pair_atm.shape[0]
+    owners = river_owner.shape[0]
+    small = lax.optimization_barrier(jnp.concatenate([pair_atm, pair_land, river_owner]))
+    pair_atm = small[:pair_count]
+    pair_land = small[pair_count : 2 * pair_count]
+    river_owner = small[2 * pair_count : 2 * pair_count + owners]
+    local_rows = lax.optimization_barrier(jnp.pad(atm_fields, ((0, 0), (0, 0), (0, row_width))))
+    atm_fields = local_rows[:, :, :row_width]
     extended = padded(atm_fields, ((("tile", "sub"), 1),), 1)
     grad_x = x_gradient(atm_fields)
     grad_y = (extended[:, 2:, :] - extended[:, :-2, :]) * 0.5
     stacked = jnp.concatenate([atm_fields, grad_x, grad_y], axis=2).astype(jnp.bfloat16)
-    pair_count = pair_atm.shape[0]
     picked = stacked[:, pair_atm, :]
     weights = pair_weight.reshape(pair_count, 3 * row_width, LBLK)
     partial_value = jnp.einsum("fpk,pkl->pfl", picked, weights, preferred_element_type=jnp.float32)

time: 79.3 us -> 72.9 us (0.919)
  other arithmetic: 10.7 us -> 5.08 us
  waiting for transfers between devices: 13.7 us -> 14.9 us
  starting transfers between devices: 29.6 us -> 28.5 us
    another operation x3, other arithmetic: 2.73 us -> 0.18 us
    ppermute x1, starting transfers between devices: 3.09 us -> 1.95 us  [route_partials(): lax.ppermute(messages[0], 'tile', [(i, (i - 1) % tile_count) for i in dev...]
    ppermute x1, waiting for transfers between devices: 1.49 us -> 2.63 us  [route_partials(): lax.ppermute(messages[0], 'tile', [(i, (i - 1) % tile_count) for i in dev...]
    all_to_all x1, starting transfers between devices: 13.2 us -> 12.1 us  [on_device(): lax.all_to_all(packed, 'tile', split_axis=0, concat_axis=0, tiled=True)]
    all_to_all x1, starting transfers between devices: 3.48 us -> 4.6 us  [route_partials(): lax.all_to_all(chunks, 'sub', split_axis=0, concat_axis=0, tiled=True)]
    slice x1, local copies, waits for them, and re-layouts: 0.82 us -> 0.01 us  [padded(): initial = lax.slice_in_dim(array, 0, width, axis=dim)]
    unnamed x16 -> x17, local copies, waits for them, and re-layouts: 4.26 us -> 5 us
  transfers between devices with their start and end apart: 6 -> 6, of which waited for: 4 -> 4; matrix products, arithmetic and copies ran while one was open for 19% -> 13% of each run, Pallas kernels for 0% -> 0%
where the time goes in v5:
time: 72.9 us; the launch traced here: 72.5 us
  starting transfers between devices  28.5 us (39%)
  waiting for transfers between devices  14.9 us (20%)
  local copies, waits for them, and re-layouts  10.9 us (15%)
  matrix products  6.14 us (8%)
  Pallas kernels  5.93 us (8%)
  other arithmetic  5.08 us (7%)
  between operations  1.03 us (1%)
    all_to_all x1, starting transfers between devices, on_device(): lax.all_to_all(packed, 'tile', split_axis=0, concat_axis=0, tiled=True)  12.1 us
    all_to_all x1, waiting for transfers between devices, on_device(): lax.all_to_all(packed, 'tile', split_axis=0, concat_axis=0, tiled=True)  6.94 us
    pallas_call x1, Pallas kernels, soil_update(): pl.pallas_call(soil_kernel, grid=(grid,), in_specs=[plane, plane, plane,...  5.93 us
    ppermute x1, starting transfers between devices, route_partials(): lax.ppermute(messages[2], 'tile', [(i, (i + 1) % tile_count) for i in dev...  5.8 us
    unnamed x17, local copies, waits for them, and re-layouts  5 us
    all_to_all x1, waiting for transfers between devices, route_partials(): lax.all_to_all(chunks, 'sub', split_axis=0, concat_axis=0, tiled=True)  4.7 us
    all_to_all x1, starting transfers between devices, route_partials(): lax.all_to_all(chunks, 'sub', split_axis=0, concat_axis=0, tiled=True)  4.6 us
    dot_general x1, matrix products, on_device(): jnp.einsum('fpk,pkl->pfl', picked, weights, preferred_element_type=jnp.fl...  4.42 us
  transfers between devices with their start and end apart: 6, of which 4 were waited for; matrix products, arithmetic and copies ran while one was open for 13% of the time, Pallas kernels for 0%

profile of v5, /device:TPU:1, one launch (start us, length us, event | category | flops | bytes accessed | tf_op | source)
XLA Modules:
  0.0 72.5 jit_solution(17244593485919544511)
XLA Ops:
  0.6 0.7 %copy.32 = f32[6,8,128]{2,0,1:T(8,128)S(1)} copy(f32[6,8,128]{2,1,0:T(8,128)} %param.8) | data formatting | bytes 49152 | tf_op args[0]
  1.4 2.1 %collective-permute-start.1 = (f32[6,1,128]{2,0,1:T(8,128)S(1)}, f32[6,1,128]{2,0,1:T(8,128)S(1)}, u32[]{:S(2)}, u32[]{:S(2)}) collective-permute-start(f32[6,1,128]{2,0,1:T(8,128)S(1)} %get-tuple-element.22), channel_id=1, source_target_pairs={{0,1},{1,2},{2,3},{3,4},{4,5},{5,6},{6,7},{7,8},{8,9},{9,10},{10,1... | collective-permute-start | bytes 9224 | tf_op jit(solution)/shard_map/ppermute | solution.py:27
  3.5 1.9 %collective-permute-start = (f32[6,1,128]{2,0,1:T(8,128)S(1)}, f32[6,1,128]{2,0,1:T(8,128)S(1)}, u32[]{:S(2)}, u32[]{:S(2)}) collective-permute-start(f32[6,1,128]{2,0,1:T(8,128)S(1)} %get-tuple-element.21), channel_id=1, source_target_pairs={{1,0},{2,1},{3,2},{4,3},{5,4},{6,5},{7,6},{8,7},{9,8},{10,9},{11,1... | collective-permute-start | bytes 9224 | tf_op jit(solution)/shard_map/ppermute | solution.py:28
  5.4 0.1 fusion.19
  5.6 0.8 %pad_add_fusion = s32[104]{0:T(128)S(1)} fusion(s32[64]{0:T(128)} %param.15, s32[20]{0:T(128)} %param.10, s32[20]{0:T(128)} %param.9), kind=kLoop, calls=%fused_computation.91 | loop fusion | flops 208 | bytes 832 | tf_op jit(solution)/shard_map/concatenate | solution.py:213
  6.4 0.1 compare_select_fusion.2
  6.6 0.2 select_reduce_fusion.3
  6.8 0.1 select_reduce_fusion.2
  7.0 0.8 %gather_fusion.2 = s32[48]{0:T(128)S(1)} fusion(s32[20]{0:T(128)S(1)} %get-tuple-element.30, s32[1024]{0:T(1024)S(1)} %pad_clamp_fusion), kind=kCustom, calls=%fused_computation.2 | custom fusion | bytes 576 | tf_op jit(solution)/shard_map/gather | solution.py:170
  7.9 0.1 reduce_window_sum.23
  8.0 0.2 select_reduce_fusion.1
  8.4 0.1 ge.11
  8.6 0.1 broadcast_in_dim.66
  8.7 0.1 concatenate.35
  8.8 0.6 gather_fusion
  9.4 4.4 %fusion.1 = f32[20,6,512]{2,1,0:T(8,128)S(1)} fusion(bf16[20,384,512]{2,1,0:T(8,128)(2,1)} %bitcast.55, bf16[20,6,384]{2,1,0:T(8,128)(2,1)S(1)} %gather_fusion), kind=kOutput, calls=%fused_computation.10 | convolution fusion | flops 47185920 | bytes 8202240 | tf_op jit(solution)/shard_map/fpk,pkl->pfl/dot_general | solution.py:225
  13.9 0.6 gather_fusion.1
  14.5 0.1 gather.13
  14.6 0.1 broadcast_select_fusion
  14.7 0.9 %maximum_maximum_fusion = f32[4,80,512]{2,1,0:T(8,128)} fusion(f32[1,8,512]{2,1,0:T(8,128)S(1)} %stack_reshape.15, f32[1,8,512]{2,1,0:T(8,128)S(1)} %stack_reshape.14, f32[1,8,512]{2,1,0:T(8,128)S(1)} %stack_reshape.13, f32[1,8,512]{2,1,0:T(8,128)S(1)} %stack_reshape.12, f32[4,72,512]{2,1,0:T(8,128)S(1)} %broadcast_select_fusion), kind=kLoop, calls=%fused_computation.4 | loop fusion | flops 655360 | bytes 1310720 | tf_op jit(solution)/shard_map/concatenate | solution.py:173
  15.6 4.6 %all-to-all-start = ((f32[4,80,512]{2,1,0:T(8,128)}), f32[4,80,512]{2,1,0:T(8,128)S(1)}, u32[]{:S(2)}, u32[]{:S(2)}) async-start(f32[4,80,512]{2,1,0:T(8,128)} %maximum_maximum_fusion), calls=%async_computation | async-start | bytes 1310720 | tf_op jit(solution)/shard_map/all_to_all | solution.py:180
  20.2 0.1 select_reduce_fusion
  20.3 0.1 copy.41
  20.4 0.9 %slice.194.cond_ref = f32[20,64,128]{2,1,0:T(8,128)} slice(f32[24,64,128]{2,1,0:T(8,128)S(1)} %bitcast.57), slice={[0:20], [0:64], [0:128]} | slice | bytes 1310720 | tf_op jit(solution)/shard_map/reshape | solution.py:139
  21.3 0.1 copy.42
  21.5 0.9 %slice.195.moist_ref = f32[20,64,128]{2,1,0:T(8,128)} slice(f32[24,64,128]{2,1,0:T(8,128)S(1)} %bitcast.58), slice={[0:20], [0:64], [0:128]} | slice | bytes 1310720 | tf_op jit(solution)/shard_map/reshape | solution.py:140
  22.4 0.1 convert_element_type.51
  22.5 0.6 convert_bitcast_fusion.1.wet_ref
  23.1 4.7 %all-to-all-done = f32[4,80,512]{2,1,0:T(8,128)S(1)} async-done(((f32[4,80,512]{2,1,0:T(8,128)}), f32[4,80,512]{2,1,0:T(8,128)S(1)}, u32[]{:S(2)}, u32[]{:S(2)}) %all-to-all-start) | async-done | bytes 655392 | tf_op jit(solution)/shard_map/all_to_all | solution.py:180
  27.9 0.1 reshape.151
  28.1 5.8 %collective-permute-start.3 = (f32[104,512]{1,0:T(8,128)S(1)}, f32[104,512]{1,0:T(8,128)S(1)}, u32[]{:S(2)}, u32[]{:S(2)}) collective-permute-start(f32[104,512]{1,0:T(8,128)S(1)} %pad_maximum_fusion.2), channel_id=1, source_target_pairs={{0,4},{4,8},{8,12},{12,16},{16,20},{20,24},{24,28},{28,32},{32,36}... | collective-permute-start | bytes 638984 | tf_op jit(solution)/shard_map/ppermute | solution.py:193
  34.0 2.0 %collective-permute-start.2 = (f32[104,512]{1,0:T(8,128)S(1)}, f32[104,512]{1,0:T(8,128)S(1)}, u32[]{:S(2)}, u32[]{:S(2)}) collective-permute-start(f32[104,512]{1,0:T(8,128)S(1)} %pad_maximum_fusion.1), channel_id=1, source_target_pairs={{0,252},{4,0},{8,4},{12,8},{16,12},{20,16},{24,20},{28,24},{32,28}... | collective-permute-start | bytes 638984 | tf_op jit(solution)/shard_map/ppermute | solution.py:191
  36.0 0.1 reshape.154
  36.1 0.6 collective-permute-done.3
  36.7 2.6 %collective-permute-done.2 = f32[104,512]{1,0:T(8,128)S(1)} collective-permute-done((f32[104,512]{1,0:T(8,128)S(1)}, f32[104,512]{1,0:T(8,128)S(1)}, u32[]{:S(2)}, u32[]{:S(2)}) %collective-permute-start.2) | collective-permute-done | bytes 213024 | tf_op jit(solution)/shard_map/ppermute | solution.py:191
  39.6 0.6 convolution_bitcast_fusion
  40.4 0.7 multiply_bitcast_fusion
  41.0 5.9 %shard_map.111 = (f32[20,64,128]{2,1,0:T(8,128)}, f32[64,128]{1,0:T(8,128)}) custom-call(f32[64,128]{1,0:T(8,128)} %get-tuple-element.20.source_ref, f32[64,128]{1,0:T(8,128)} %get-tuple-element.19.surface_ref, f32[64,128]{1,0:T(8,128)} %convert_bitcast_fusion.1.wet_ref, f32[20,64,128]{2,1,0:T(8,128)} %slice.194.cond_ref, f32[20,64,128]{2,1,0:T(8,128)} %slice.195.moist_ref), custom_call_target="tpu_custom_call" | custom-call | tf_op jit(solution)/shard_map/pallas_call | solution.py:126
  47.0 1.1 %fusion.23 = f32[128,128]{1,0:T(8,128)S(1)} fusion(f32[64,128]{1,0:T(8,128)} %get-tuple-element.7, s32[64]{0:T(128)S(1)} %get-tuple-element.38), kind=kOutput, calls=%fused_computation.48 | convolution fusion | flops 12591104 | bytes 98560 | tf_op jit(solution)/shard_map/dot_general | solution.py:239
  48.1 0.7 all_to_all.12
  48.8 12.1 %all-to-all-start.1 = ((f32[64,1,384]{2,1,0:T(1,128)}), f32[64,1,384]{2,1,0:T(1,128)S(1)}, u32[]{:S(2)}, u32[]{:S(2)}) async-start(f32[64,1,384]{2,1,0:T(1,128)} %all_to_all.12), calls=%async_computation.1 | async-start | bytes 196608 | tf_op jit(solution)/shard_map/all_to_all | solution.py:248
  60.9 0.7 copy.36
  61.6 1.2 %pad.72 = f32[24,64,128]{2,1,0:T(8,128)S(1)} pad(f32[20,64,128]{2,1,0:T(8,128)} %get-tuple-element.6, f32[]{:T(128)} %constant.106.clone.1), padding=0_4x0_0x0_0 | pad | bytes 1441796
  62.8 1.3 %copy.43 = f32[3,8,64,128]{3,1,2,0:T(8,128)} copy(f32[3,8,64,128]{3,2,1,0:T(8,128)S(1)} %bitcast.56) | data formatting | bytes 1572864
  64.1 6.9 %all-to-all-done.1 = f32[64,1,384]{2,1,0:T(1,128)S(1)} async-done(((f32[64,1,384]{2,1,0:T(1,128)}), f32[64,1,384]{2,1,0:T(1,128)S(1)}, u32[]{:S(2)}, u32[]{:S(2)}) %all-to-all-start.1) | async-done | bytes 98336 | tf_op jit(solution)/shard_map/all_to_all | solution.py:248
  71.1 0.1 copy.34
  71.2 0.6 fusion.30
  71.8 0.7 copy.35
  (65 shorter events, 1.3 us)
Async XLA Ops:
  1.4 7.3 %collective-permute-start.1 = (f32[6,1,128]{2,0,1:T(8,128)S(1)}, f32[6,1,128]{2,0,1:T(8,128)S(1)}, u32[]{:S(2)}, u32[]{:S(2)}) collective-permute-start(f32[6,1,128]{2,0,1:T(8,128)S(1)} %get-tuple-element.22), channel_id=1, source_target_pairs={{0,1},{1,2},{2,3},{3,4},{4,5},{5,6},{6,7},{7,8},{8,9},{9,10},{10,1... | collective-permute-start | bytes 9224 | tf_op jit(solution)/shard_map/ppermute | solution.py:27
  3.5 5.2 %collective-permute-start = (f32[6,1,128]{2,0,1:T(8,128)S(1)}, f32[6,1,128]{2,0,1:T(8,128)S(1)}, u32[]{:S(2)}, u32[]{:S(2)}) collective-permute-start(f32[6,1,128]{2,0,1:T(8,128)S(1)} %get-tuple-element.21), channel_id=1, source_target_pairs={{1,0},{2,1},{3,2},{4,3},{5,4},{6,5},{7,6},{8,7},{9,8},{10,9},{11,1... | collective-permute-start | bytes 9224 | tf_op jit(solution)/shard_map/ppermute | solution.py:28
  9.4 10.9 %copy-start = (f32[20,8192]{1,0:T(8,128)S(1)}, f32[20,8192]{1,0:T(8,128)}, u32[]{:S(2)}) copy-start(f32[20,8192]{1,0:T(8,128)} %param.13) | copy-start | bytes 1966084
  13.9 7.5 %copy-start.1 = (f32[20,8192]{1,0:T(8,128)S(1)}, f32[20,8192]{1,0:T(8,128)}, u32[]{:S(2)}) copy-start(f32[20,8192]{1,0:T(8,128)} %param.14) | copy-start | bytes 1966084
  13.9 8.6 %copy-start.2 = (s32[8192]{0:T(1024)S(1)}, s32[8192]{0:T(1024)}, u32[]{:S(2)}) copy-start(s32[8192]{0:T(1024)} %param.12) | copy-start | bytes 98308
  15.6 12.2 %all-to-all-start = ((f32[4,80,512]{2,1,0:T(8,128)}), f32[4,80,512]{2,1,0:T(8,128)S(1)}, u32[]{:S(2)}, u32[]{:S(2)}) async-start(f32[4,80,512]{2,1,0:T(8,128)} %maximum_maximum_fusion), calls=%async_computation | async-start | bytes 1310720 | tf_op jit(solution)/shard_map/all_to_all | solution.py:180
  28.1 8.6 %collective-permute-start.3 = (f32[104,512]{1,0:T(8,128)S(1)}, f32[104,512]{1,0:T(8,128)S(1)}, u32[]{:S(2)}, u32[]{:S(2)}) collective-permute-start(f32[104,512]{1,0:T(8,128)S(1)} %pad_maximum_fusion.2), channel_id=1, source_target_pairs={{0,4},{4,8},{8,12},{12,16},{16,20},{20,24},{24,28},{28,32},{32,36}... | collective-permute-start | bytes 638984 | tf_op jit(solution)/shard_map/ppermute | solution.py:193
  34.0 5.3 %collective-permute-start.2 = (f32[104,512]{1,0:T(8,128)S(1)}, f32[104,512]{1,0:T(8,128)S(1)}, u32[]{:S(2)}, u32[]{:S(2)}) collective-permute-start(f32[104,512]{1,0:T(8,128)S(1)} %pad_maximum_fusion.1), channel_id=1, source_target_pairs={{0,252},{4,0},{8,4},{12,8},{16,12},{20,16},{24,20},{28,24},{32,28}... | collective-permute-start | bytes 638984 | tf_op jit(solution)/shard_map/ppermute | solution.py:191
  48.8 22.3 %all-to-all-start.1 = ((f32[64,1,384]{2,1,0:T(1,128)}), f32[64,1,384]{2,1,0:T(1,128)S(1)}, u32[]{:S(2)}, u32[]{:S(2)}) async-start(f32[64,1,384]{2,1,0:T(1,128)} %all_to_all.12), calls=%async_computation.1 | async-start | bytes 196608 | tf_op jit(solution)/shard_map/all_to_all | solution.py:248

commit v6 on v5

--- a/solution.py
+++ b/solution.py
@@ -70,22 +70,40 @@
     return jnp.stack(solved)
 
 
-def soil_kernel(source_ref, surface_ref, wet_ref, cond_ref, moist_ref, out_ref, runoff_ref):
+def factor_kernel(cond_ref, inverse_ref, ratio_ref):
+    layers = cond_ref.shape[0]
+    groups = cond_ref.shape[1] // 8
+
+    def one_group(g, carry):
+        rows = pl.ds(pl.multiple_of(g * 8, 8), 8)
+        previous_cond = None
+        previous_inv = None
+        for k in range(layers):
+            cond = cond_ref[k, rows, :]
+            diagonal = 1.0 + cond
+            if k > 0:
+                diagonal = diagonal + previous_cond - previous_cond * previous_cond * previous_inv
+            pivot_inv = 1.0 / diagonal
+            inverse_ref[k, rows, :] = pivot_inv
+            ratio_ref[k, rows, :] = -cond * pivot_inv
+            previous_cond = cond
+            previous_inv = pivot_inv
+        return carry
+
+    lax.fori_loop(0, groups, one_group, 0)
+
+
+def soil_kernel(
+    source_ref, surface_ref, wet_ref, cond_ref, inverse_ref, ratio_ref, moist_ref, out_ref, runoff_ref
+):
     layers = cond_ref.shape[0]
     groups = cond_ref.shape[1] // 8
 
     def one_group(g, carry):
         rows = pl.ds(pl.multiple_of(g * 8, 8), 8)
         cond = [cond_ref[k, rows, :] for k in range(layers)]
-        inverse = []
-        ratios = []
-        for k in range(layers):
-            diagonal = 1.0 + cond[k]
-            if k > 0:
-                diagonal = diagonal + cond[k - 1] - cond[k - 1] * cond[k - 1] * inverse[k - 1]
-            pivot_inv = 1.0 / diagonal
-            inverse.append(pivot_inv)
-            ratios.append(-cond[k] * pivot_inv)
+        inverse = [inverse_ref[k, rows, :] for k in range(layers)]
+        ratios = [ratio_ref[k, rows, :] for k in range(layers)]
         source = source_ref[rows, :]
         moisture = [moist_ref[k, rows, :] for k in range(layers)]
         drainage = jnp.zeros_like(source)
@@ -123,20 +141,28 @@
     block = rows // grid
     plane = pl.BlockSpec((block, 128), lambda i: (i, 0))
     stack = pl.BlockSpec((layers, block, 128), lambda i: (0, i, 0))
+    cond_tiles = conductance.reshape(layers, rows, 128)
+    layer_shape = jax.ShapeDtypeStruct((layers, rows, 128), jnp.float32)
+    inverse, ratios = pl.pallas_call(
+        factor_kernel,
+        grid=(grid,),
+        in_specs=[stack],
+        out_specs=[stack, stack],
+        out_shape=[layer_shape, layer_shape],
+    )(cond_tiles)
     moisture, runoff = pl.pallas_call(
         soil_kernel,
         grid=(grid,),
-        in_specs=[plane, plane, plane, stack, stack],
+        in_specs=[plane, plane, plane, stack, stack, stack, stack],
         out_specs=[stack, plane],
-        out_shape=[
-            jax.ShapeDtypeStruct((layers, rows, 128), jnp.float32),
-            jax.ShapeDtypeStruct((rows, 128), jnp.float32),
-        ],
+        out_shape=[layer_shape, jax.ShapeDtypeStruct((rows, 128), jnp.float32)],
     )(
         source.reshape(rows, 128),
         surface.reshape(rows, 128),
         wetness.reshape(rows, 128),
-        conductance.reshape(layers, rows, 128),
+        cond_tiles,
+        inverse,
+        ratios,
         soil_moisture.reshape(layers, rows, 128),
     )
     return (moisture.reshape(layers, cells), runoff.reshape(cells))

time: 72.9 us -> 77.6 us (1.064)
  starting transfers between devices: 28.5 us -> 34.9 us
  waiting for transfers between devices: 14.9 us -> 10.6 us
  Pallas kernels: 5.93 us -> 8.51 us
    ppermute x1, starting transfers between devices: 1.95 us -> 7.17 us  [route_partials(): lax.ppermute(messages[0], 'tile', [(i, (i - 1) % tile_count) for i in dev...]
    pallas_call x0 -> x1, Pallas kernels: none -> 3.12 us  [soil_update(): pl.pallas_call(factor_kernel, grid=(grid,), in_specs=[stack], out_specs=[...]
    all_to_all x1, waiting for transfers between devices: 4.7 us -> 1.59 us  [route_partials(): lax.all_to_all(chunks, 'sub', split_axis=0, concat_axis=0, tiled=True)]
    ppermute x1, waiting for transfers between devices: 2.63 us -> 0.23 us  [route_partials(): lax.ppermute(messages[0], 'tile', [(i, (i - 1) % tile_count) for i in dev...]
    all_to_all x1, starting transfers between devices: 12.1 us -> 14.4 us  [on_device(): lax.all_to_all(packed, 'tile', split_axis=0, concat_axis=0, tiled=True)]
    ppermute x1, starting transfers between devices: 2.12 us -> 0.01 us  [padded(): before = lax.ppermute(last, axis, up)]
    ppermute x1, starting transfers between devices: 1.92 us -> 3.95 us  [padded(): after = lax.ppermute(initial, axis, down)]
    all_to_all x1, starting transfers between devices: 4.6 us -> 3.6 us  [route_partials(): lax.all_to_all(chunks, 'sub', split_axis=0, concat_axis=0, tiled=True)]
  transfers between devices with their start and end apart: 6 -> 6, of which waited for: 4 -> 5; matrix products, arithmetic and copies ran while one was open for 13% -> 12% of each run, Pallas kernels for 0% -> 4%
where the time goes in v6:
time: 77.6 us; the launch traced here: 77.2 us
  starting transfers between devices  34.9 us (45%)
  local copies, waits for them, and re-layouts  10.9 us (14%)
  waiting for transfers between devices  10.6 us (14%)
  Pallas kernels  8.51 us (11%)
  matrix products  6.14 us (8%)
  other arithmetic  5.07 us (7%)
  between operations  1.05 us (1%)
    all_to_all x1, starting transfers between devices, on_device(): lax.all_to_all(packed, 'tile', split_axis=0, concat_axis=0, tiled=True)  14.4 us
    ppermute x1, starting transfers between devices, route_partials(): lax.ppermute(messages[0], 'tile', [(i, (i - 1) % tile_count) for i in dev...  7.17 us
    all_to_all x1, waiting for transfers between devices, on_device(): lax.all_to_all(packed, 'tile', split_axis=0, concat_axis=0, tiled=True)  6.94 us
    ppermute x1, starting transfers between devices, route_partials(): lax.ppermute(messages[2], 'tile', [(i, (i + 1) % tile_count) for i in dev...  5.8 us
    pallas_call x1, Pallas kernels, soil_update(): pl.pallas_call(soil_kernel, grid=(grid,), in_specs=[plane, plane, plane,...  5.38 us
    unnamed x17, local copies, waits for them, and re-layouts  5 us
    dot_general x1, matrix products, on_device(): jnp.einsum('fpk,pkl->pfl', picked, weights, preferred_element_type=jnp.fl...  4.42 us
    ppermute x1, starting transfers between devices, padded(): after = lax.ppermute(initial, axis, down)  3.95 us
  transfers between devices with their start and end apart: 6, of which 5 were waited for; matrix products, arithmetic and copies ran while one was open for 12% of the time, Pallas kernels for 4%

profile of v6, /device:TPU:1, one launch (start us, length us, event | category | flops | bytes accessed | tf_op | source)
XLA Modules:
  0.0 77.2 jit_solution(5092749257962991445)
XLA Ops:
  0.6 0.7 copy.32
  1.4 4.0 %collective-permute-start = (f32[6,1,128]{2,0,1:T(8,128)S(1)}, f32[6,1,128]{2,0,1:T(8,128)S(1)}, u32[]{:S(2)}, u32[]{:S(2)}) collective-permute-start(f32[6,1,128]{2,0,1:T(8,128)S(1)} %get-tuple-element.25), channel_id=1, source_target_pairs={{1,0},{2,1},{3,2},{4,3},{5,4},{6,5},{7,6},{8,7},{9,8},{10,9},{11,1... | collective-permute-start | bytes 9224 | tf_op jit(solution)/shard_map/ppermute | solution.py:28
  5.4 0.8 pad_add_fusion
  6.2 0.1 compare_select_fusion.2
  6.4 0.2 select_reduce_fusion.3
  6.6 0.1 select_reduce_fusion.2
  6.8 0.1 fusion.19
  6.9 0.8 %gather_fusion.2 = s32[48]{0:T(128)S(1)} fusion(s32[20]{0:T(128)S(1)} %get-tuple-element.34, s32[1024]{0:T(1024)S(1)} %pad_clamp_fusion), kind=kCustom, calls=%fused_computation.2 | custom fusion | bytes 576 | tf_op jit(solution)/shard_map/gather | solution.py:196
  7.8 0.1 reduce_window_sum.23
  7.9 0.2 select_reduce_fusion.1
  8.2 0.1 ge.11
  8.4 0.1 broadcast_in_dim.66
  8.6 1.0 %collective-permute-done.1 = f32[6,1,128]{2,0,1:T(8,128)S(1)} collective-permute-done((f32[6,1,128]{2,0,1:T(8,128)S(1)}, f32[6,1,128]{2,0,1:T(8,128)S(1)}, u32[]{:S(2)}, u32[]{:S(2)}) %collective-permute-start.1) | collective-permute-done | bytes 3104 | tf_op jit(solution)/shard_map/ppermute | solution.py:27
  9.6 0.1 concatenate.35
  9.7 0.6 gather_fusion
  10.3 4.4 %fusion.1 = f32[20,6,512]{2,1,0:T(8,128)S(1)} fusion(bf16[20,384,512]{2,1,0:T(8,128)(2,1)} %bitcast.55, bf16[20,6,384]{2,1,0:T(8,128)(2,1)S(1)} %gather_fusion), kind=kOutput, calls=%fused_computation.10 | convolution fusion | flops 47185920 | bytes 8202240 | tf_op jit(solution)/shard_map/fpk,pkl->pfl/dot_general | solution.py:251
  14.7 0.6 gather_fusion.1
  15.4 0.1 gather.13
  15.5 0.1 broadcast_select_fusion
  15.6 0.9 %maximum_maximum_fusion = f32[4,80,512]{2,1,0:T(8,128)} fusion(f32[1,8,512]{2,1,0:T(8,128)S(1)} %stack_reshape.15, f32[1,8,512]{2,1,0:T(8,128)S(1)} %stack_reshape.14, f32[1,8,512]{2,1,0:T(8,128)S(1)} %stack_reshape.13, f32[1,8,512]{2,1,0:T(8,128)S(1)} %stack_reshape.12, f32[4,72,512]{2,1,0:T(8,128)S(1)} %broadcast_select_fusion), kind=kLoop, calls=%fused_computation.4 | loop fusion | flops 655360 | bytes 1310720 | tf_op jit(solution)/shard_map/concatenate | solution.py:199
  16.5 3.6 %all-to-all-start = ((f32[4,80,512]{2,1,0:T(8,128)}), f32[4,80,512]{2,1,0:T(8,128)S(1)}, u32[]{:S(2)}, u32[]{:S(2)}) async-start(f32[4,80,512]{2,1,0:T(8,128)} %maximum_maximum_fusion), calls=%async_computation | async-start | bytes 1310720 | tf_op jit(solution)/shard_map/all_to_all | solution.py:206
  20.1 0.1 select_reduce_fusion
  20.2 0.1 convert_element_type.51
  20.3 0.1 copy.41
  20.5 0.9 %slice.194.cond_ref = f32[20,64,128]{2,1,0:T(8,128)} slice(f32[24,64,128]{2,1,0:T(8,128)S(1)} %bitcast.57), slice={[0:20], [0:64], [0:128]} | slice | bytes 1310720 | tf_op jit(solution)/shard_map/reshape | solution.py:144
  21.4 0.1 copy.42
  21.5 0.9 %slice.195.moist_ref = f32[20,64,128]{2,1,0:T(8,128)} slice(f32[24,64,128]{2,1,0:T(8,128)S(1)} %bitcast.58), slice={[0:20], [0:64], [0:128]} | slice | bytes 1310720 | tf_op jit(solution)/shard_map/reshape | solution.py:166
  22.4 3.1 %shard_map.111 = (f32[20,64,128]{2,1,0:T(8,128)}, f32[20,64,128]{2,1,0:T(8,128)}) custom-call(f32[20,64,128]{2,1,0:T(8,128)} %slice.194.cond_ref), custom_call_target="tpu_custom_call" | custom-call | tf_op jit(solution)/shard_map/pallas_call | solution.py:146
  25.5 0.6 convert_bitcast_fusion.1.wet_ref
  26.1 1.6 %all-to-all-done = f32[4,80,512]{2,1,0:T(8,128)S(1)} async-done(((f32[4,80,512]{2,1,0:T(8,128)}), f32[4,80,512]{2,1,0:T(8,128)S(1)}, u32[]{:S(2)}, u32[]{:S(2)}) %all-to-all-start) | async-done | bytes 655392 | tf_op jit(solution)/shard_map/all_to_all | solution.py:206
  27.8 0.1 reshape.154
  28.2 5.8 %collective-permute-start.3 = (f32[104,512]{1,0:T(8,128)S(1)}, f32[104,512]{1,0:T(8,128)S(1)}, u32[]{:S(2)}, u32[]{:S(2)}) collective-permute-start(f32[104,512]{1,0:T(8,128)S(1)} %pad_maximum_fusion.2), channel_id=1, source_target_pairs={{0,4},{4,8},{8,12},{12,16},{16,20},{20,24},{24,28},{28,32},{32,36}... | collective-permute-start | bytes 638984 | tf_op jit(solution)/shard_map/ppermute | solution.py:219
  34.0 7.2 %collective-permute-start.2 = (f32[104,512]{1,0:T(8,128)S(1)}, f32[104,512]{1,0:T(8,128)S(1)}, u32[]{:S(2)}, u32[]{:S(2)}) collective-permute-start(f32[104,512]{1,0:T(8,128)S(1)} %pad_maximum_fusion.1), channel_id=1, source_target_pairs={{0,252},{4,0},{8,4},{12,8},{16,12},{20,16},{24,20},{28,24},{32,28}... | collective-permute-start | bytes 638984 | tf_op jit(solution)/shard_map/ppermute | solution.py:217
  41.2 0.8 %collective-permute-done.3 = f32[104,512]{1,0:T(8,128)S(1)} collective-permute-done((f32[104,512]{1,0:T(8,128)S(1)}, f32[104,512]{1,0:T(8,128)S(1)}, u32[]{:S(2)}, u32[]{:S(2)}) %collective-permute-start.3) | collective-permute-done | bytes 213024 | tf_op jit(solution)/shard_map/ppermute | solution.py:219
  42.0 0.2 collective-permute-done.2
  42.5 0.6 convolution_bitcast_fusion
  43.3 0.7 multiply_bitcast_fusion
  43.9 5.4 %shard_map.112 = (f32[20,64,128]{2,1,0:T(8,128)}, f32[64,128]{1,0:T(8,128)}) custom-call(f32[64,128]{1,0:T(8,128)} %get-tuple-element.24.source_ref, f32[64,128]{1,0:T(8,128)} %get-tuple-element.23.surface_ref, f32[64,128]{1,0:T(8,128)} %convert_bitcast_fusion.1.wet_ref, f32[20,64,128]{2,1,0:T(8,128)} %slice.194.cond_ref, ...), custom_call_target="tpu_custom_call" | custom-call | tf_op jit(solution)/shard_map/pallas_call | solution.py:153
  49.3 1.1 %fusion.23 = f32[128,128]{1,0:T(8,128)S(1)} fusion(f32[64,128]{1,0:T(8,128)} %get-tuple-element.11, s32[64]{0:T(128)S(1)} %get-tuple-element.42), kind=kOutput, calls=%fused_computation.48 | convolution fusion | flops 12591104 | bytes 98560 | tf_op jit(solution)/shard_map/dot_general | solution.py:265
  50.5 0.7 all_to_all.12
  51.2 14.4 %all-to-all-start.1 = ((f32[64,1,384]{2,1,0:T(1,128)}), f32[64,1,384]{2,1,0:T(1,128)S(1)}, u32[]{:S(2)}, u32[]{:S(2)}) async-start(f32[64,1,384]{2,1,0:T(1,128)} %all_to_all.12), calls=%async_computation.1 | async-start | bytes 196608 | tf_op jit(solution)/shard_map/all_to_all | solution.py:274
  65.6 0.7 copy.36
  66.3 1.2 %pad.72 = f32[24,64,128]{2,1,0:T(8,128)S(1)} pad(f32[20,64,128]{2,1,0:T(8,128)} %get-tuple-element.10, f32[]{:T(128)} %constant.106.clone.1), padding=0_4x0_0x0_0 | pad | bytes 1441796
  67.4 1.3 %copy.43 = f32[3,8,64,128]{3,1,2,0:T(8,128)} copy(f32[3,8,64,128]{3,2,1,0:T(8,128)S(1)} %bitcast.56) | data formatting | bytes 1572864
  68.8 6.9 %all-to-all-done.1 = f32[64,1,384]{2,1,0:T(1,128)S(1)} async-done(((f32[64,1,384]{2,1,0:T(1,128)}), f32[64,1,384]{2,1,0:T(1,128)S(1)}, u32[]{:S(2)}, u32[]{:S(2)}) %all-to-all-start.1) | async-done | bytes 98336 | tf_op jit(solution)/shard_map/all_to_all | solution.py:274
  75.7 0.1 copy.34
  75.9 0.6 fusion.30
  76.5 0.7 copy.35
  (66 shorter events, 1.4 us)
Async XLA Ops:
  1.4 7.2 %collective-permute-start = (f32[6,1,128]{2,0,1:T(8,128)S(1)}, f32[6,1,128]{2,0,1:T(8,128)S(1)}, u32[]{:S(2)}, u32[]{:S(2)}) collective-permute-start(f32[6,1,128]{2,0,1:T(8,128)S(1)} %get-tuple-element.25), channel_id=1, source_target_pairs={{1,0},{2,1},{3,2},{4,3},{5,4},{6,5},{7,6},{8,7},{9,8},{10,9},{11,1... | collective-permute-start | bytes 9224 | tf_op jit(solution)/shard_map/ppermute | solution.py:28
  5.3 4.2 %collective-permute-start.1 = (f32[6,1,128]{2,0,1:T(8,128)S(1)}, f32[6,1,128]{2,0,1:T(8,128)S(1)}, u32[]{:S(2)}, u32[]{:S(2)}) collective-permute-start(f32[6,1,128]{2,0,1:T(8,128)S(1)} %get-tuple-element.26), channel_id=1, source_target_pairs={{0,1},{1,2},{2,3},{3,4},{4,5},{5,6},{6,7},{7,8},{8,9},{9,10},{10,1... | collective-permute-start | bytes 9224 | tf_op jit(solution)/shard_map/ppermute | solution.py:27
  10.3 10.0 %copy-start = (f32[20,8192]{1,0:T(8,128)S(1)}, f32[20,8192]{1,0:T(8,128)}, u32[]{:S(2)}) copy-start(f32[20,8192]{1,0:T(8,128)} %param.13) | copy-start | bytes 1966084
  14.7 6.6 %copy-start.1 = (f32[20,8192]{1,0:T(8,128)S(1)}, f32[20,8192]{1,0:T(8,128)}, u32[]{:S(2)}) copy-start(f32[20,8192]{1,0:T(8,128)} %param.14) | copy-start | bytes 1966084
  14.7 10.8 %copy-start.2 = (s32[8192]{0:T(1024)S(1)}, s32[8192]{0:T(1024)}, u32[]{:S(2)}) copy-start(s32[8192]{0:T(1024)} %param.12) | copy-start | bytes 98308
  16.5 11.2 %all-to-all-start = ((f32[4,80,512]{2,1,0:T(8,128)}), f32[4,80,512]{2,1,0:T(8,128)S(1)}, u32[]{:S(2)}, u32[]{:S(2)}) async-start(f32[4,80,512]{2,1,0:T(8,128)} %maximum_maximum_fusion), calls=%async_computation | async-start | bytes 1310720 | tf_op jit(solution)/shard_map/all_to_all | solution.py:206
  28.2 13.8 %collective-permute-start.3 = (f32[104,512]{1,0:T(8,128)S(1)}, f32[104,512]{1,0:T(8,128)S(1)}, u32[]{:S(2)}, u32[]{:S(2)}) collective-permute-start(f32[104,512]{1,0:T(8,128)S(1)} %pad_maximum_fusion.2), channel_id=1, source_target_pairs={{0,4},{4,8},{8,12},{12,16},{16,20},{20,24},{24,28},{28,32},{32,36}... | collective-permute-start | bytes 638984 | tf_op jit(solution)/shard_map/ppermute | solution.py:219
  34.0 8.3 %collective-permute-start.2 = (f32[104,512]{1,0:T(8,128)S(1)}, f32[104,512]{1,0:T(8,128)S(1)}, u32[]{:S(2)}, u32[]{:S(2)}) collective-permute-start(f32[104,512]{1,0:T(8,128)S(1)} %pad_maximum_fusion.1), channel_id=1, source_target_pairs={{0,252},{4,0},{8,4},{12,8},{16,12},{20,16},{24,20},{28,24},{32,28}... | collective-permute-start | bytes 638984 | tf_op jit(solution)/shard_map/ppermute | solution.py:217
  51.2 24.6 %all-to-all-start.1 = ((f32[64,1,384]{2,1,0:T(1,128)}), f32[64,1,384]{2,1,0:T(1,128)S(1)}, u32[]{:S(2)}, u32[]{:S(2)}) async-start(f32[64,1,384]{2,1,0:T(1,128)} %all_to_all.12), calls=%async_computation.1 | async-start | bytes 196608 | tf_op jit(solution)/shard_map/all_to_all | solution.py:274

commit v7 on v5

--- a/solution.py
+++ b/solution.py
@@ -188,9 +188,9 @@
         messages.append(jnp.concatenate([data, id_rows(step_ids, width)], axis=0))
     devices = range(tile_count)
     received = [
-        lax.ppermute(messages[0], "tile", [(i, (i - 1) % tile_count) for i in devices]),
+        lax.ppermute(messages[0], TILE, [(i, (i - 1) % tile_count) for i in devices]),
         messages[1],
-        lax.ppermute(messages[2], "tile", [(i, (i + 1) % tile_count) for i in devices]),
+        lax.ppermute(messages[2], TILE, [(i, (i + 1) % tile_count) for i in devices]),
     ]
     message_rows = sub_count * part_rows
     data = jnp.concatenate([m[:message_rows] for m in received], axis=0)
@@ -203,9 +203,9 @@
 def on_device(
     atm_fields, pair_atm, pair_land, pair_weight, land_mask, conductance, soil_moisture, river_owner
 ):
-    tile_count = lax.axis_size("tile")
+    tile_count = lax.axis_size(TILE)
     sub_count = lax.axis_size("sub")
-    tile_index = lax.axis_index("tile")
+    tile_index = lax.axis_index(TILE)
     sub_index = lax.axis_index("sub")
     field_count, row_count, row_width = atm_fields.shape
     pair_count = pair_atm.shape[0]
@@ -216,7 +216,7 @@
     river_owner = small[2 * pair_count : 2 * pair_count + owners]
     local_rows = lax.optimization_barrier(jnp.pad(atm_fields, ((0, 0), (0, 0), (0, row_width))))
     atm_fields = local_rows[:, :, :row_width]
-    extended = padded(atm_fields, ((("tile", "sub"), 1),), 1)
+    extended = padded(atm_fields, (((*TILE, "sub"), 1),), 1)
     grad_x = x_gradient(atm_fields)
     grad_y = (extended[:, 2:, :] - extended[:, :-2, :]) * 0.5
     stacked = jnp.concatenate([atm_fields, grad_x, grad_y], axis=2).astype(jnp.bfloat16)
@@ -245,31 +245,44 @@
     numbers = numbers.astype(jnp.float32).reshape(tile_count, capacity)
     numbers = jnp.pad(numbers, ((0, 0), (0, RBLK - capacity)))
     packed = jnp.concatenate([values, numbers], axis=1)
-    got = lax.all_to_all(packed, "tile", split_axis=0, concat_axis=0, tiled=True)
+    high = lax.axis_size("tile_hi")
+    low = lax.axis_size("tile_lo")
+    packed = packed.reshape(high, low, packed.shape[1]).transpose(1, 0, 2)
+    packed = lax.all_to_all(packed, "tile_lo", split_axis=0, concat_axis=0, tiled=True)
+    packed = packed.transpose(1, 0, 2)
+    got = lax.all_to_all(packed, "tile_hi", split_axis=0, concat_axis=0, tiled=True)
+    got = got.reshape(tile_count, got.shape[2])
     river_runoff = got[:, : capacity * RBLK].reshape(tile_count, capacity, RBLK)[None, None]
     river_blocks = got[:, capacity * RBLK : capacity * RBLK + capacity].astype(jnp.int32)[None, None]
     return (land_forcing, moisture, river_runoff, river_blocks)
 
 
+TILE = ("tile_hi", "tile_lo")
+
+
 def solution(mesh):
+    tiles, subs = mesh.devices.shape
+    low = 8 if tiles % 8 == 0 else tiles
+    split_mesh = jax.sharding.Mesh(mesh.devices.reshape(tiles // low, low, subs), (*TILE, "sub"))
+    lined = (*TILE, "sub")
     return jax.shard_map(
         on_device,
-        mesh=mesh,
+        mesh=split_mesh,
         in_specs=(
-            P(None, ("tile", "sub"), None),
-            P(("tile", "sub")),
-            P(("tile", "sub")),
-            P(("tile", "sub"), None, None, None),
-            P(("tile", "sub")),
-            P(None, ("tile", "sub")),
-            P(None, ("tile", "sub")),
-            P(("tile", "sub")),
+            P(None, lined, None),
+            P(lined),
+            P(lined),
+            P(lined, None, None, None),
+            P(lined),
+            P(None, lined),
+            P(None, lined),
+            P(lined),
         ),
         out_specs=(
-            P(None, ("tile", "sub")),
-            P(None, ("tile", "sub")),
-            P("tile", "sub", None, None, None),
-            P("tile", "sub", None, None),
+            P(None, lined),
+            P(None, lined),
+            P(TILE, "sub", None, None, None),
+            P(TILE, "sub", None, None),
         ),
         check_vma=False,
     )

time: 72.9 us -> 85.5 us (1.17)
  blocking collectives: 0 us -> 14 us
  starting transfers between devices: 28.5 us -> 24.6 us
  local copies, waits for them, and re-layouts: 10.9 us -> 13.6 us
    all_to_all x0 -> x1, blocking collectives: none -> 14 us  [on_device(): lax.all_to_all(packed, 'tile_lo', split_axis=0, concat_axis=0, tiled=True)]
    all_to_all x1, starting transfers between devices: 12.1 us -> 8.17 us  [on_device(): lax.all_to_all(packed, 'tile_hi', split_axis=0, concat_axis=0, tiled=True)]
    unnamed x17 -> x13, local copies, waits for them, and re-layouts: 5 us -> 7.19 us
    all_to_all x1, waiting for transfers between devices: 4.7 us -> 6.8 us  [route_partials(): lax.all_to_all(chunks, 'sub', split_axis=0, concat_axis=0, tiled=True)]
    ppermute x2, starting transfers between devices: 7.75 us -> 8.89 us  [the longest x1 5.8 us: route_partials(): lax.ppermute(messages[2], TILE, [(i, (i + 1) % tile_count) for i in devic...]
    ppermute x2, waiting for transfers between devices: 3.27 us -> 2.13 us  [the longest x1 1.49 us: route_partials(): lax.ppermute(messages[0], TILE, [(i, (i - 1) % tile_count) for i in devic...]
    all_to_all x1, starting transfers between devices: 4.6 us -> 3.48 us  [route_partials(): lax.all_to_all(chunks, 'sub', split_axis=0, concat_axis=0, tiled=True)]
  transfers between devices with their start and end apart: 6 -> 6, of which waited for: 4 -> 4; matrix products, arithmetic and copies ran while one was open for 13% -> 14% of each run, Pallas kernels for 0% -> 0%
where the time goes in v7:
time: 85.5 us; the launch traced here: 84.9 us
  starting transfers between devices  24.6 us (29%)
  waiting for transfers between devices  15.1 us (18%)
  blocking collectives  14 us (16%)
  local copies, waits for them, and re-layouts  13.6 us (16%)
  matrix products  6.07 us (7%)
  Pallas kernels  5.93 us (7%)
  other arithmetic  4.52 us (5%)
  between operations  1.03 us (1%)
    all_to_all x1, blocking collectives, on_device(): lax.all_to_all(packed, 'tile_lo', split_axis=0, concat_axis=0, tiled=True)  14 us
    all_to_all x1, starting transfers between devices, on_device(): lax.all_to_all(packed, 'tile_hi', split_axis=0, concat_axis=0, tiled=True)  8.17 us
    unnamed x13, local copies, waits for them, and re-layouts  7.19 us
    all_to_all x1, waiting for transfers between devices, route_partials(): lax.all_to_all(chunks, 'sub', split_axis=0, concat_axis=0, tiled=True)  6.8 us
    all_to_all x1, waiting for transfers between devices, on_device(): lax.all_to_all(packed, 'tile_hi', split_axis=0, concat_axis=0, tiled=True)  6.15 us
    pallas_call x1, Pallas kernels, soil_update(): pl.pallas_call(soil_kernel, grid=(grid,), in_specs=[plane, plane, plane,...  5.93 us
    ppermute x1, starting transfers between devices, route_partials(): lax.ppermute(messages[2], TILE, [(i, (i + 1) % tile_count) for i in devic...  5.8 us
    dot_general x1, matrix products, on_device(): jnp.einsum('fpk,pkl->pfl', picked, weights, preferred_element_type=jnp.fl...  4.35 us
  transfers between devices with their start and end apart: 6, of which 4 were waited for; matrix products, arithmetic and copies ran while one was open for 14% of the time, Pallas kernels for 0%

profile of v7, /device:TPU:1, one launch (start us, length us, event | category | flops | bytes accessed | tf_op | source)
XLA Modules:
  0.0 84.9 jit_solution(10075269424889248608)
XLA Ops:
  0.6 0.7 copy.35
  1.4 2.1 %collective-permute-start.1 = (f32[6,1,128]{2,0,1:T(8,128)S(1)}, f32[6,1,128]{2,0,1:T(8,128)S(1)}, u32[]{:S(2)}, u32[]{:S(2)}) collective-permute-start(f32[6,1,128]{2,0,1:T(8,128)S(1)} %get-tuple-element.18), channel_id=1, source_target_pairs={{0,1},{1,2},{2,3},{3,4},{4,5},{5,6},{6,7},{7,8},{8,9},{9,10},{10,1... | collective-permute-start | bytes 9224 | tf_op jit(solution)/shard_map/ppermute | solution.py:27
  3.5 1.9 %collective-permute-start = (f32[6,1,128]{2,0,1:T(8,128)S(1)}, f32[6,1,128]{2,0,1:T(8,128)S(1)}, u32[]{:S(2)}, u32[]{:S(2)}) collective-permute-start(f32[6,1,128]{2,0,1:T(8,128)S(1)} %get-tuple-element.17), channel_id=1, source_target_pairs={{1,0},{2,1},{3,2},{4,3},{5,4},{6,5},{7,6},{8,7},{9,8},{10,9},{11,1... | collective-permute-start | bytes 9224 | tf_op jit(solution)/shard_map/ppermute | solution.py:28
  5.4 0.1 fusion.19
  5.6 0.8 pad_add_fusion
  6.4 0.1 compare_select_fusion.2
  6.6 0.2 select_reduce_fusion.3
  6.8 0.1 select_reduce_fusion.2
  7.0 0.8 gather_fusion.2
  7.9 0.1 reduce_window_sum.23
  8.0 0.2 select_reduce_fusion.1
  8.3 0.1 select_reduce_fusion
  8.5 0.1 ge.11
  8.7 0.1 broadcast_in_dim.66
  8.8 1.3 %copy.47 = f32[3,8,64,128]{3,2,1,0:T(8,128)S(1)} copy(f32[3,8,64,128]{3,1,2,0:T(8,128)} %bitcast.65) | data formatting | bytes 1572864
  10.1 0.9 %slice.194.cond_ref = f32[20,64,128]{2,1,0:T(8,128)} slice(f32[24,64,128]{2,1,0:T(8,128)S(1)} %bitcast.62), slice={[0:20], [0:64], [0:128]} | slice | bytes 1310720 | tf_op jit(solution)/shard_map/reshape | solution.py:139
  11.0 1.3 %copy.48 = f32[3,8,64,128]{3,2,1,0:T(8,128)S(1)} copy(f32[3,8,64,128]{3,1,2,0:T(8,128)} %bitcast.66) | data formatting | bytes 1572864
  12.2 0.9 %slice.195.moist_ref = f32[20,64,128]{2,1,0:T(8,128)} slice(f32[24,64,128]{2,1,0:T(8,128)S(1)} %bitcast.63), slice={[0:20], [0:64], [0:128]} | slice | bytes 1310720 | tf_op jit(solution)/shard_map/reshape | solution.py:140
  13.2 0.1 concatenate.40
  13.3 0.6 gather_fusion
  13.9 4.4 %fusion.1 = f32[20,6,512]{2,1,0:T(8,128)S(1)} fusion(bf16[20,384,512]{2,1,0:T(8,128)(2,1)} %bitcast.60, bf16[20,6,384]{2,1,0:T(8,128)(2,1)S(1)} %gather_fusion), kind=kOutput, calls=%fused_computation.10 | convolution fusion | flops 47185920 | bytes 8202240 | tf_op jit(solution)/shard_map/fpk,pkl->pfl/dot_general | solution.py:225
  18.2 0.6 gather_fusion.1
  18.8 0.1 gather.13
  18.9 0.1 broadcast_select_fusion
  19.0 0.9 %maximum_maximum_fusion = f32[4,80,512]{2,1,0:T(8,128)} fusion(f32[1,8,512]{2,1,0:T(8,128)S(1)} %stack_reshape.15, f32[1,8,512]{2,1,0:T(8,128)S(1)} %stack_reshape.14, f32[1,8,512]{2,1,0:T(8,128)S(1)} %stack_reshape.13, f32[1,8,512]{2,1,0:T(8,128)S(1)} %stack_reshape.12, f32[4,72,512]{2,1,0:T(8,128)S(1)} %broadcast_select_fusion), kind=kLoop, calls=%fused_computation.4 | loop fusion | flops 655360 | bytes 1310720 | tf_op jit(solution)/shard_map/concatenate | solution.py:173
  19.9 3.5 %all-to-all-start = ((f32[4,80,512]{2,1,0:T(8,128)}), f32[4,80,512]{2,1,0:T(8,128)S(1)}, u32[]{:S(2)}, u32[]{:S(2)}) async-start(f32[4,80,512]{2,1,0:T(8,128)} %maximum_maximum_fusion), calls=%async_computation | async-start | bytes 1310720 | tf_op jit(solution)/shard_map/all_to_all | solution.py:180
  23.4 0.1 convert_element_type.51
  23.6 0.6 convert_bitcast_fusion.1.wet_ref
  24.2 6.8 %all-to-all-done = f32[4,80,512]{2,1,0:T(8,128)S(1)} async-done(((f32[4,80,512]{2,1,0:T(8,128)}), f32[4,80,512]{2,1,0:T(8,128)S(1)}, u32[]{:S(2)}, u32[]{:S(2)}) %all-to-all-start) | async-done | bytes 655392 | tf_op jit(solution)/shard_map/all_to_all | solution.py:180
  31.1 0.1 reshape.154
  31.3 5.8 %collective-permute-start.3 = (f32[104,512]{1,0:T(8,128)S(1)}, f32[104,512]{1,0:T(8,128)S(1)}, u32[]{:S(2)}, u32[]{:S(2)}) collective-permute-start(f32[104,512]{1,0:T(8,128)S(1)} %pad_maximum_fusion.2), channel_id=1, source_target_pairs={{0,4},{4,8},{8,12},{12,16},{16,20},{20,24},{24,28},{28,32},{32,36}... | collective-permute-start | bytes 638984 | tf_op jit(solution)/shard_map/ppermute | solution.py:193
  37.1 0.1 reshape.150
  37.2 3.1 %collective-permute-start.2 = (f32[104,512]{1,0:T(8,128)S(1)}, f32[104,512]{1,0:T(8,128)S(1)}, u32[]{:S(2)}, u32[]{:S(2)}) collective-permute-start(f32[104,512]{1,0:T(8,128)S(1)} %pad_maximum_fusion.1), channel_id=1, source_target_pairs={{0,252},{4,0},{8,4},{12,8},{16,12},{20,16},{24,20},{28,24},{32,28}... | collective-permute-start | bytes 638984 | tf_op jit(solution)/shard_map/ppermute | solution.py:191
  40.4 0.6 collective-permute-done.3
  41.1 1.5 %collective-permute-done.2 = f32[104,512]{1,0:T(8,128)S(1)} collective-permute-done((f32[104,512]{1,0:T(8,128)S(1)}, f32[104,512]{1,0:T(8,128)S(1)}, u32[]{:S(2)}, u32[]{:S(2)}) %collective-permute-start.2) | collective-permute-done | bytes 213024 | tf_op jit(solution)/shard_map/ppermute | solution.py:191
  42.8 0.6 convolution_bitcast_fusion
  43.6 0.7 multiply_bitcast_fusion
  44.2 5.9 %shard_map.111 = (f32[20,64,128]{2,1,0:T(8,128)}, f32[64,128]{1,0:T(8,128)}) custom-call(f32[64,128]{1,0:T(8,128)} %get-tuple-element.16.source_ref, f32[64,128]{1,0:T(8,128)} %get-tuple-element.15.surface_ref, f32[64,128]{1,0:T(8,128)} %convert_bitcast_fusion.1.wet_ref, f32[20,64,128]{2,1,0:T(8,128)} %slice.194.cond_ref, f32[20,64,128]{2,1,0:T(8,128)} %slice.195.moist_ref), custom_call_target="tpu_custom_call" | custom-call | tf_op jit(solution)/shard_map/pallas_call | solution.py:126
  50.2 1.1 %fusion.23 = f32[128,128]{1,0:T(8,128)S(1)} fusion(f32[64,128]{1,0:T(8,128)} %get-tuple-element.7, s32[64]{0:T(128)S(1)} %get-tuple-element.34), kind=kOutput, calls=%fused_computation.50 | convolution fusion | flops 12591104 | bytes 98560 | tf_op jit(solution)/shard_map/dot_general | solution.py:239
  51.3 14.0 %all_to_all.15 = f32[8,8,384]{2,1,0:T(8,128)S(1)} all-to-all(f32[8,8,384]{2,1,0:T(8,128)S(1)} %maximum_bitcast_fusion), channel_id=1, replica_groups=mesh['tile_hi'=8,'tile_lo'=8,'sub'=4] {'tile_lo'}, dimensions={0} | all-to-all | bytes 196608 | tf_op jit(solution)/shard_map/all_to_all | solution.py:251
  65.3 0.6 copy.54
  66.0 8.2 %all-to-all-start.2 = ((f32[8,8,384]{2,1,0:T(8,128)}), f32[8,8,384]{2,1,0:T(8,128)S(1)}, u32[]{:S(2)}, u32[]{:S(2)}) async-start(f32[8,8,384]{2,1,0:T(8,128)} %bitcast.59), calls=%async_computation.2 | async-start | bytes 196608 | tf_op jit(solution)/shard_map/all_to_all | solution.py:253
  74.2 0.7 copy.42
  74.9 1.2 %pad.71 = f32[24,64,128]{2,1,0:T(8,128)S(1)} pad(f32[20,64,128]{2,1,0:T(8,128)} %get-tuple-element.6, f32[]{:T(128)} %constant.112.clone.1), padding=0_4x0_0x0_0 | pad | bytes 1441796
  76.1 1.3 %copy.49 = f32[3,8,64,128]{3,1,2,0:T(8,128)} copy(f32[3,8,64,128]{3,2,1,0:T(8,128)S(1)} %bitcast.61) | data formatting | bytes 1572864
  77.4 6.2 %all-to-all-done.2 = f32[8,8,384]{2,1,0:T(8,128)S(1)} async-done(((f32[8,8,384]{2,1,0:T(8,128)}), f32[8,8,384]{2,1,0:T(8,128)S(1)}, u32[]{:S(2)}, u32[]{:S(2)}) %all-to-all-start.2) | async-done | bytes 98336 | tf_op jit(solution)/shard_map/all_to_all | solution.py:253
  83.6 0.7 broadcast_in_dim_reshape.3
  84.2 0.6 copy.50
  (65 shorter events, 1.4 us)
Async XLA Ops:
  1.4 11.7 %collective-permute-start.1 = (f32[6,1,128]{2,0,1:T(8,128)S(1)}, f32[6,1,128]{2,0,1:T(8,128)S(1)}, u32[]{:S(2)}, u32[]{:S(2)}) collective-permute-start(f32[6,1,128]{2,0,1:T(8,128)S(1)} %get-tuple-element.18), channel_id=1, source_target_pairs={{0,1},{1,2},{2,3},{3,4},{4,5},{5,6},{6,7},{7,8},{8,9},{9,10},{10,1... | collective-permute-start | bytes 9224 | tf_op jit(solution)/shard_map/ppermute | solution.py:27
  3.5 9.6 %collective-permute-start = (f32[6,1,128]{2,0,1:T(8,128)S(1)}, f32[6,1,128]{2,0,1:T(8,128)S(1)}, u32[]{:S(2)}, u32[]{:S(2)}) collective-permute-start(f32[6,1,128]{2,0,1:T(8,128)S(1)} %get-tuple-element.17), channel_id=1, source_target_pairs={{1,0},{2,1},{3,2},{4,3},{5,4},{6,5},{7,6},{8,7},{9,8},{10,9},{11,1... | collective-permute-start | bytes 9224 | tf_op jit(solution)/shard_map/ppermute | solution.py:28
  13.8 9.8 %copy-start = (s32[8192]{0:T(1024)S(1)}, s32[8192]{0:T(1024)}, u32[]{:S(2)}) copy-start(s32[8192]{0:T(1024)} %param.12) | copy-start | bytes 98308
  19.9 11.1 %all-to-all-start = ((f32[4,80,512]{2,1,0:T(8,128)}), f32[4,80,512]{2,1,0:T(8,128)S(1)}, u32[]{:S(2)}, u32[]{:S(2)}) async-start(f32[4,80,512]{2,1,0:T(8,128)} %maximum_maximum_fusion), calls=%async_computation | async-start | bytes 1310720 | tf_op jit(solution)/shard_map/all_to_all | solution.py:180
  31.3 9.8 %collective-permute-start.3 = (f32[104,512]{1,0:T(8,128)S(1)}, f32[104,512]{1,0:T(8,128)S(1)}, u32[]{:S(2)}, u32[]{:S(2)}) collective-permute-start(f32[104,512]{1,0:T(8,128)S(1)} %pad_maximum_fusion.2), channel_id=1, source_target_pairs={{0,4},{4,8},{8,12},{12,16},{16,20},{20,24},{24,28},{28,32},{32,36}... | collective-permute-start | bytes 638984 | tf_op jit(solution)/shard_map/ppermute | solution.py:193
  37.2 5.3 %collective-permute-start.2 = (f32[104,512]{1,0:T(8,128)S(1)}, f32[104,512]{1,0:T(8,128)S(1)}, u32[]{:S(2)}, u32[]{:S(2)}) collective-permute-start(f32[104,512]{1,0:T(8,128)S(1)} %pad_maximum_fusion.1), channel_id=1, source_target_pairs={{0,252},{4,0},{8,4},{12,8},{16,12},{20,16},{24,20},{28,24},{32,28}... | collective-permute-start | bytes 638984 | tf_op jit(solution)/shard_map/ppermute | solution.py:191
  66.0 17.6 %all-to-all-start.2 = ((f32[8,8,384]{2,1,0:T(8,128)}), f32[8,8,384]{2,1,0:T(8,128)S(1)}, u32[]{:S(2)}, u32[]{:S(2)}) async-start(f32[8,8,384]{2,1,0:T(8,128)} %bitcast.59), calls=%async_computation.2 | async-start | bytes 196608 | tf_op jit(solution)/shard_map/all_to_all | solution.py:253

commit v8 on v5

--- a/solution.py
+++ b/solution.py
@@ -70,22 +70,26 @@
     return jnp.stack(solved)
 
 
-def soil_kernel(source_ref, surface_ref, wet_ref, cond_ref, moist_ref, out_ref, runoff_ref):
+def soil_kernel(
+    source_ref, surface_ref, wet_ref, cond_ref, moist_ref, out_ref, runoff_ref, inv_ref, ratio_ref
+):
     layers = cond_ref.shape[0]
-    groups = cond_ref.shape[1] // 8
+    groups = cond_ref.shape[1] // 32
 
     def one_group(g, carry):
-        rows = pl.ds(pl.multiple_of(g * 8, 8), 8)
-        cond = [cond_ref[k, rows, :] for k in range(layers)]
-        inverse = []
-        ratios = []
+        rows = pl.ds(pl.multiple_of(g * 32, 32), 32)
+        previous_cond = None
+        previous_inv = None
         for k in range(layers):
-            diagonal = 1.0 + cond[k]
+            cond = cond_ref[k, rows, :]
+            diagonal = 1.0 + cond
             if k > 0:
-                diagonal = diagonal + cond[k - 1] - cond[k - 1] * cond[k - 1] * inverse[k - 1]
+                diagonal = diagonal + previous_cond - previous_cond * previous_cond * previous_inv
             pivot_inv = 1.0 / diagonal
-            inverse.append(pivot_inv)
-            ratios.append(-cond[k] * pivot_inv)
+            inv_ref[k] = pivot_inv
+            ratio_ref[k] = -cond * pivot_inv
+            previous_cond = cond
+            previous_inv = pivot_inv
         source = source_ref[rows, :]
         moisture = [moist_ref[k, rows, :] for k in range(layers)]
         drainage = jnp.zeros_like(source)
@@ -95,13 +99,13 @@
                 if k == 0:
                     column_value = moisture[0] + source
                 else:
-                    column_value = moisture[k] + cond[k - 1] * forward[k - 1]
-                forward.append(column_value * inverse[k])
+                    column_value = moisture[k] + cond_ref[k - 1, rows, :] * forward[k - 1]
+                forward.append(column_value * inv_ref[k])
             solved = [forward[layers - 1]]
             for k in range(layers - 2, -1, -1):
-                solved.insert(0, forward[k] - ratios[k] * solved[0])
+                solved.insert(0, forward[k] - ratio_ref[k] * solved[0])
             moisture = solved
-            drainage = drainage + cond[layers - 1] * moisture[layers - 1]
+            drainage = drainage + cond_ref[layers - 1, rows, :] * moisture[layers - 1]
         for k in range(layers):
             out_ref[k, rows, :] = moisture[k]
         runoff_ref[rows, :] = wet_ref[rows, :] * (SOIL_STEPS * surface_ref[rows, :] + drainage)
@@ -128,6 +132,7 @@
         grid=(grid,),
         in_specs=[plane, plane, plane, stack, stack],
         out_specs=[stack, plane],
+        scratch_shapes=[pltpu.VMEM((layers, 32, 128), jnp.float32)] * 2,
         out_shape=[
             jax.ShapeDtypeStruct((layers, rows, 128), jnp.float32),
             jax.ShapeDtypeStruct((rows, 128), jnp.float32),

time: 72.9 us -> 69.9 us (0.959)
  Pallas kernels: 5.93 us -> 2.94 us
    pallas_call x1, Pallas kernels: 5.93 us -> 2.94 us  [soil_update(): pl.pallas_call(soil_kernel, grid=(grid,), in_specs=[plane, plane, plane,...]
  transfers between devices with their start and end apart: 6 -> 6, of which waited for: 4 -> 4; matrix products, arithmetic and copies ran while one was open for 13% -> 14% of each run, Pallas kernels for 0% -> 0%
where the time goes in v8:
time: 69.9 us; the launch traced here: 69.5 us
  starting transfers between devices  28.5 us (41%)
  waiting for transfers between devices  14.9 us (21%)
  local copies, waits for them, and re-layouts  10.9 us (16%)
  matrix products  6.14 us (9%)
  other arithmetic  5.08 us (7%)
  Pallas kernels  2.94 us (4%)
  between operations  1.03 us (1%)
    all_to_all x1, starting transfers between devices, on_device(): lax.all_to_all(packed, 'tile', split_axis=0, concat_axis=0, tiled=True)  12.1 us
    all_to_all x1, waiting for transfers between devices, on_device(): lax.all_to_all(packed, 'tile', split_axis=0, concat_axis=0, tiled=True)  6.94 us
    ppermute x1, starting transfers between devices, route_partials(): lax.ppermute(messages[2], 'tile', [(i, (i + 1) % tile_count) for i in dev...  5.8 us
    unnamed x17, local copies, waits for them, and re-layouts  5 us
    all_to_all x1, waiting for transfers between devices, route_partials(): lax.all_to_all(chunks, 'sub', split_axis=0, concat_axis=0, tiled=True)  4.7 us
    all_to_all x1, starting transfers between devices, route_partials(): lax.all_to_all(chunks, 'sub', split_axis=0, concat_axis=0, tiled=True)  4.6 us
    dot_general x1, matrix products, on_device(): jnp.einsum('fpk,pkl->pfl', picked, weights, preferred_element_type=jnp.fl...  4.42 us
    pallas_call x1, Pallas kernels, soil_update(): pl.pallas_call(soil_kernel, grid=(grid,), in_specs=[plane, plane, plane,...  2.94 us
  transfers between devices with their start and end apart: 6, of which 4 were waited for; matrix products, arithmetic and copies ran while one was open for 14% of the time, Pallas kernels for 0%

profile of v8, /device:TPU:1, one launch (start us, length us, event | category | flops | bytes accessed | tf_op | source)
XLA Modules:
  0.0 69.5 jit_solution(4812554830495912649)
XLA Ops:
  0.6 0.7 %copy.32 = f32[6,8,128]{2,0,1:T(8,128)S(1)} copy(f32[6,8,128]{2,1,0:T(8,128)} %param.8) | data formatting | bytes 49152 | tf_op args[0]
  1.4 2.1 %collective-permute-start.1 = (f32[6,1,128]{2,0,1:T(8,128)S(1)}, f32[6,1,128]{2,0,1:T(8,128)S(1)}, u32[]{:S(2)}, u32[]{:S(2)}) collective-permute-start(f32[6,1,128]{2,0,1:T(8,128)S(1)} %get-tuple-element.22), channel_id=1, source_target_pairs={{0,1},{1,2},{2,3},{3,4},{4,5},{5,6},{6,7},{7,8},{8,9},{9,10},{10,1... | collective-permute-start | bytes 9224 | tf_op jit(solution)/shard_map/ppermute | solution.py:27
  3.5 1.9 %collective-permute-start = (f32[6,1,128]{2,0,1:T(8,128)S(1)}, f32[6,1,128]{2,0,1:T(8,128)S(1)}, u32[]{:S(2)}, u32[]{:S(2)}) collective-permute-start(f32[6,1,128]{2,0,1:T(8,128)S(1)} %get-tuple-element.21), channel_id=1, source_target_pairs={{1,0},{2,1},{3,2},{4,3},{5,4},{6,5},{7,6},{8,7},{9,8},{10,9},{11,1... | collective-permute-start | bytes 9224 | tf_op jit(solution)/shard_map/ppermute | solution.py:28
  5.4 0.1 fusion.19
  5.6 0.8 %pad_add_fusion = s32[104]{0:T(128)S(1)} fusion(s32[64]{0:T(128)} %param.15, s32[20]{0:T(128)} %param.10, s32[20]{0:T(128)} %param.9), kind=kLoop, calls=%fused_computation.91 | loop fusion | flops 208 | bytes 832 | tf_op jit(solution)/shard_map/concatenate | solution.py:218
  6.4 0.1 compare_select_fusion.2
  6.6 0.2 select_reduce_fusion.3
  6.8 0.1 select_reduce_fusion.2
  7.0 0.8 %gather_fusion.2 = s32[48]{0:T(128)S(1)} fusion(s32[20]{0:T(128)S(1)} %get-tuple-element.30, s32[1024]{0:T(1024)S(1)} %pad_clamp_fusion), kind=kCustom, calls=%fused_computation.2 | custom fusion | bytes 576 | tf_op jit(solution)/shard_map/gather | solution.py:175
  7.9 0.1 reduce_window_sum.23
  8.0 0.2 select_reduce_fusion.1
  8.4 0.1 ge.11
  8.6 0.1 broadcast_in_dim.66
  8.7 0.1 concatenate.35
  8.8 0.6 gather_fusion
  9.4 4.4 %fusion.1 = f32[20,6,512]{2,1,0:T(8,128)S(1)} fusion(bf16[20,384,512]{2,1,0:T(8,128)(2,1)} %bitcast.55, bf16[20,6,384]{2,1,0:T(8,128)(2,1)S(1)} %gather_fusion), kind=kOutput, calls=%fused_computation.10 | convolution fusion | flops 47185920 | bytes 8202240 | tf_op jit(solution)/shard_map/fpk,pkl->pfl/dot_general | solution.py:230
  13.9 0.6 gather_fusion.1
  14.5 0.1 gather.13
  14.6 0.1 broadcast_select_fusion
  14.7 0.9 %maximum_maximum_fusion = f32[4,80,512]{2,1,0:T(8,128)} fusion(f32[1,8,512]{2,1,0:T(8,128)S(1)} %stack_reshape.15, f32[1,8,512]{2,1,0:T(8,128)S(1)} %stack_reshape.14, f32[1,8,512]{2,1,0:T(8,128)S(1)} %stack_reshape.13, f32[1,8,512]{2,1,0:T(8,128)S(1)} %stack_reshape.12, f32[4,72,512]{2,1,0:T(8,128)S(1)} %broadcast_select_fusion), kind=kLoop, calls=%fused_computation.4 | loop fusion | flops 655360 | bytes 1310720 | tf_op jit(solution)/shard_map/concatenate | solution.py:178
  15.6 4.6 %all-to-all-start = ((f32[4,80,512]{2,1,0:T(8,128)}), f32[4,80,512]{2,1,0:T(8,128)S(1)}, u32[]{:S(2)}, u32[]{:S(2)}) async-start(f32[4,80,512]{2,1,0:T(8,128)} %maximum_maximum_fusion), calls=%async_computation | async-start | bytes 1310720 | tf_op jit(solution)/shard_map/all_to_all | solution.py:185
  20.2 0.1 select_reduce_fusion
  20.3 0.1 copy.41
  20.4 0.9 %slice.194.cond_ref = f32[20,64,128]{2,1,0:T(8,128)} slice(f32[24,64,128]{2,1,0:T(8,128)S(1)} %bitcast.57), slice={[0:20], [0:64], [0:128]} | slice | bytes 1310720 | tf_op jit(solution)/shard_map/reshape | solution.py:144
  21.3 0.1 copy.42
  21.5 0.9 %slice.195.moist_ref = f32[20,64,128]{2,1,0:T(8,128)} slice(f32[24,64,128]{2,1,0:T(8,128)S(1)} %bitcast.58), slice={[0:20], [0:64], [0:128]} | slice | bytes 1310720 | tf_op jit(solution)/shard_map/reshape | solution.py:145
  22.4 0.1 convert_element_type.51
  22.5 0.6 convert_bitcast_fusion.1.wet_ref
  23.1 4.7 %all-to-all-done = f32[4,80,512]{2,1,0:T(8,128)S(1)} async-done(((f32[4,80,512]{2,1,0:T(8,128)}), f32[4,80,512]{2,1,0:T(8,128)S(1)}, u32[]{:S(2)}, u32[]{:S(2)}) %all-to-all-start) | async-done | bytes 655392 | tf_op jit(solution)/shard_map/all_to_all | solution.py:185
  27.9 0.1 reshape.151
  28.1 5.8 %collective-permute-start.3 = (f32[104,512]{1,0:T(8,128)S(1)}, f32[104,512]{1,0:T(8,128)S(1)}, u32[]{:S(2)}, u32[]{:S(2)}) collective-permute-start(f32[104,512]{1,0:T(8,128)S(1)} %pad_maximum_fusion.2), channel_id=1, source_target_pairs={{0,4},{4,8},{8,12},{12,16},{16,20},{20,24},{24,28},{28,32},{32,36}... | collective-permute-start | bytes 638984 | tf_op jit(solution)/shard_map/ppermute | solution.py:198
  33.9 0.1 reshape.147
  34.0 2.0 %collective-permute-start.2 = (f32[104,512]{1,0:T(8,128)S(1)}, f32[104,512]{1,0:T(8,128)S(1)}, u32[]{:S(2)}, u32[]{:S(2)}) collective-permute-start(f32[104,512]{1,0:T(8,128)S(1)} %pad_maximum_fusion.1), channel_id=1, source_target_pairs={{0,252},{4,0},{8,4},{12,8},{16,12},{20,16},{24,20},{28,24},{32,28}... | collective-permute-start | bytes 638984 | tf_op jit(solution)/shard_map/ppermute | solution.py:196
  36.1 0.6 collective-permute-done.3
  36.7 2.6 %collective-permute-done.2 = f32[104,512]{1,0:T(8,128)S(1)} collective-permute-done((f32[104,512]{1,0:T(8,128)S(1)}, f32[104,512]{1,0:T(8,128)S(1)}, u32[]{:S(2)}, u32[]{:S(2)}) %collective-permute-start.2) | collective-permute-done | bytes 213024 | tf_op jit(solution)/shard_map/ppermute | solution.py:196
  39.6 0.6 convolution_bitcast_fusion
  40.4 0.7 multiply_bitcast_fusion
  41.0 2.9 %shard_map.111 = (f32[20,64,128]{2,1,0:T(8,128)}, f32[64,128]{1,0:T(8,128)}) custom-call(f32[64,128]{1,0:T(8,128)} %get-tuple-element.20.source_ref, f32[64,128]{1,0:T(8,128)} %get-tuple-element.19.surface_ref, f32[64,128]{1,0:T(8,128)} %convert_bitcast_fusion.1.wet_ref, f32[20,64,128]{2,1,0:T(8,128)} %slice.194.cond_ref, f32[20,64,128]{2,1,0:T(8,128)} %slice.195.moist_ref), custom_call_target="tpu_custom_call" | custom-call | tf_op jit(solution)/shard_map/pallas_call | solution.py:130
  44.0 1.1 %fusion.23 = f32[128,128]{1,0:T(8,128)S(1)} fusion(f32[64,128]{1,0:T(8,128)} %get-tuple-element.7, s32[64]{0:T(128)S(1)} %get-tuple-element.38), kind=kOutput, calls=%fused_computation.48 | convolution fusion | flops 12591104 | bytes 98560 | tf_op jit(solution)/shard_map/dot_general | solution.py:244
  45.1 0.7 %all_to_all.12 = f32[64,1,384]{2,1,0:T(1,128)} reshape(f32[64,384]{1,0:T(8,128)S(1)} %select_maximum_fusion) | data formatting | bytes 196608 | tf_op jit(solution)/shard_map/all_to_all | solution.py:253
  45.8 12.1 %all-to-all-start.1 = ((f32[64,1,384]{2,1,0:T(1,128)}), f32[64,1,384]{2,1,0:T(1,128)S(1)}, u32[]{:S(2)}, u32[]{:S(2)}) async-start(f32[64,1,384]{2,1,0:T(1,128)} %all_to_all.12), calls=%async_computation.1 | async-start | bytes 196608 | tf_op jit(solution)/shard_map/all_to_all | solution.py:253
  57.9 0.7 %copy.36 = bf16[1,6,16,512]{3,1,2,0:T(8,128)(2,1)} copy(bf16[1,6,16,512]{3,2,1,0:T(8,128)(2,1)S(1)} %convert_bitcast_fusion) | data formatting | bytes 196608
  58.6 1.2 %pad.72 = f32[24,64,128]{2,1,0:T(8,128)S(1)} pad(f32[20,64,128]{2,1,0:T(8,128)} %get-tuple-element.6, f32[]{:T(128)} %constant.106.clone.1), padding=0_4x0_0x0_0 | pad | bytes 1441796
  59.8 1.3 %copy.43 = f32[3,8,64,128]{3,1,2,0:T(8,128)} copy(f32[3,8,64,128]{3,2,1,0:T(8,128)S(1)} %bitcast.56) | data formatting | bytes 1572864
  61.2 6.9 %all-to-all-done.1 = f32[64,1,384]{2,1,0:T(1,128)S(1)} async-done(((f32[64,1,384]{2,1,0:T(1,128)}), f32[64,1,384]{2,1,0:T(1,128)S(1)}, u32[]{:S(2)}, u32[]{:S(2)}) %all-to-all-start.1) | async-done | bytes 98336 | tf_op jit(solution)/shard_map/all_to_all | solution.py:253
  68.1 0.1 copy.34
  68.3 0.6 fusion.30
  68.8 0.7 %copy.35 = f32[1,1,64,2,128]{4,3,2,1,0:T(2,128)} copy(f32[1,1,64,2,128]{2,4,3,1,0:T(8,128)S(1)} %bitcast.67) | data formatting | bytes 131072
  (65 shorter events, 1.3 us)
Async XLA Ops:
  1.4 7.3 %collective-permute-start.1 = (f32[6,1,128]{2,0,1:T(8,128)S(1)}, f32[6,1,128]{2,0,1:T(8,128)S(1)}, u32[]{:S(2)}, u32[]{:S(2)}) collective-permute-start(f32[6,1,128]{2,0,1:T(8,128)S(1)} %get-tuple-element.22), channel_id=1, source_target_pairs={{0,1},{1,2},{2,3},{3,4},{4,5},{5,6},{6,7},{7,8},{8,9},{9,10},{10,1... | collective-permute-start | bytes 9224 | tf_op jit(solution)/shard_map/ppermute | solution.py:27
  3.5 5.2 %collective-permute-start = (f32[6,1,128]{2,0,1:T(8,128)S(1)}, f32[6,1,128]{2,0,1:T(8,128)S(1)}, u32[]{:S(2)}, u32[]{:S(2)}) collective-permute-start(f32[6,1,128]{2,0,1:T(8,128)S(1)} %get-tuple-element.21), channel_id=1, source_target_pairs={{1,0},{2,1},{3,2},{4,3},{5,4},{6,5},{7,6},{8,7},{9,8},{10,9},{11,1... | collective-permute-start | bytes 9224 | tf_op jit(solution)/shard_map/ppermute | solution.py:28
  9.4 10.9 %copy-start = (f32[20,8192]{1,0:T(8,128)S(1)}, f32[20,8192]{1,0:T(8,128)}, u32[]{:S(2)}) copy-start(f32[20,8192]{1,0:T(8,128)} %param.13) | copy-start | bytes 1966084
  13.9 7.5 %copy-start.1 = (f32[20,8192]{1,0:T(8,128)S(1)}, f32[20,8192]{1,0:T(8,128)}, u32[]{:S(2)}) copy-start(f32[20,8192]{1,0:T(8,128)} %param.14) | copy-start | bytes 1966084
  13.9 8.6 %copy-start.2 = (s32[8192]{0:T(1024)S(1)}, s32[8192]{0:T(1024)}, u32[]{:S(2)}) copy-start(s32[8192]{0:T(1024)} %param.12) | copy-start | bytes 98308
  15.6 12.2 %all-to-all-start = ((f32[4,80,512]{2,1,0:T(8,128)}), f32[4,80,512]{2,1,0:T(8,128)S(1)}, u32[]{:S(2)}, u32[]{:S(2)}) async-start(f32[4,80,512]{2,1,0:T(8,128)} %maximum_maximum_fusion), calls=%async_computation | async-start | bytes 1310720 | tf_op jit(solution)/shard_map/all_to_all | solution.py:185
  28.1 8.6 %collective-permute-start.3 = (f32[104,512]{1,0:T(8,128)S(1)}, f32[104,512]{1,0:T(8,128)S(1)}, u32[]{:S(2)}, u32[]{:S(2)}) collective-permute-start(f32[104,512]{1,0:T(8,128)S(1)} %pad_maximum_fusion.2), channel_id=1, source_target_pairs={{0,4},{4,8},{8,12},{12,16},{16,20},{20,24},{24,28},{28,32},{32,36}... | collective-permute-start | bytes 638984 | tf_op jit(solution)/shard_map/ppermute | solution.py:198
  34.0 5.3 %collective-permute-start.2 = (f32[104,512]{1,0:T(8,128)S(1)}, f32[104,512]{1,0:T(8,128)S(1)}, u32[]{:S(2)}, u32[]{:S(2)}) collective-permute-start(f32[104,512]{1,0:T(8,128)S(1)} %pad_maximum_fusion.1), channel_id=1, source_target_pairs={{0,252},{4,0},{8,4},{12,8},{16,12},{20,16},{24,20},{28,24},{32,28}... | collective-permute-start | bytes 638984 | tf_op jit(solution)/shard_map/ppermute | solution.py:196
  45.8 22.3 %all-to-all-start.1 = ((f32[64,1,384]{2,1,0:T(1,128)}), f32[64,1,384]{2,1,0:T(1,128)S(1)}, u32[]{:S(2)}, u32[]{:S(2)}) async-start(f32[64,1,384]{2,1,0:T(1,128)} %all_to_all.12), calls=%async_computation.1 | async-start | bytes 196608 | tf_op jit(solution)/shard_map/all_to_all | solution.py:253

commit v9 on v8

--- a/solution.py
+++ b/solution.py
@@ -241,18 +241,17 @@
     ranks = jnp.sum((jnp.cumsum(hits, axis=0) - hits) * hits, axis=1)
     slot_id = river_owner * capacity + ranks
     placing = slot_id[None, :] == jnp.arange(tile_count * capacity, dtype=jnp.int32)[:, None]
-    values = jnp.dot(placing.astype(jnp.float32), runoff_blocks, precision=lax.Precision.HIGHEST)
-    values = values.reshape(tile_count, capacity * RBLK)
-    block_ids = (tile_index * sub_count + sub_index) * block_count + jnp.arange(
-        block_count, dtype=jnp.int32
-    )
-    numbers = jnp.sum(jnp.where(placing, block_ids[None, :] + 1, 0), axis=1) - 1
-    numbers = numbers.astype(jnp.float32).reshape(tile_count, capacity)
-    numbers = jnp.pad(numbers, ((0, 0), (0, RBLK - capacity)))
+    source_block = jnp.sum(jnp.where(placing, jnp.arange(block_count, dtype=jnp.int32)[None, :] + 1, 0), axis=1) - 1
+    taken = source_block >= 0
+    values = jnp.where(taken[:, None], runoff_blocks[jnp.maximum(source_block, 0)], 0.0)
+    values = values.reshape(tile_count, capacity, RBLK)
+    block_ids = (tile_index * sub_count + sub_index) * block_count + source_block
+    numbers = jnp.where(taken, block_ids, -1).astype(jnp.float32).reshape(tile_count, 1, capacity)
+    numbers = jnp.pad(numbers, ((0, 0), (0, 0), (0, RBLK - capacity)))
     packed = jnp.concatenate([values, numbers], axis=1)
     got = lax.all_to_all(packed, "tile", split_axis=0, concat_axis=0, tiled=True)
-    river_runoff = got[:, : capacity * RBLK].reshape(tile_count, capacity, RBLK)[None, None]
-    river_blocks = got[:, capacity * RBLK : capacity * RBLK + capacity].astype(jnp.int32)[None, None]
+    river_runoff = got[:, :capacity, :][None, None]
+    river_blocks = got[:, capacity, :capacity].astype(jnp.int32)[None, None]
     return (land_forcing, moisture, river_runoff, river_blocks)
 
 

time: 69.9 us -> 75 us (1.073)
  local copies, waits for them, and re-layouts: 10.9 us -> 13.9 us
  waiting for transfers between devices: 14.9 us -> 16.1 us
  matrix products: 6.14 us -> 5 us
  starting transfers between devices: 28.5 us -> 29.6 us
  other arithmetic: 5.08 us -> 5.95 us
    all_to_all x1, waiting for transfers between devices: 4.7 us -> 6.81 us  [route_partials(): lax.all_to_all(chunks, 'sub', split_axis=0, concat_axis=0, tiled=True)]
    unnamed x17 -> x13, local copies, waits for them, and re-layouts: 5 us -> 6.62 us
    gather x0 -> x1, local copies, waits for them, and re-layouts: none -> 1.4 us  [on_device(): runoff_blocks[jnp.maximum(source_block, 0)]]
    ppermute x1, starting transfers between devices: 1.95 us -> 3.1 us  [route_partials(): lax.ppermute(messages[0], 'tile', [(i, (i - 1) % tile_count) for i in dev...]
    ppermute x1, waiting for transfers between devices: 2.63 us -> 1.49 us  [route_partials(): lax.ppermute(messages[0], 'tile', [(i, (i - 1) % tile_count) for i in dev...]
    all_to_all x1, starting transfers between devices: 12.1 us -> 13.2 us  [on_device(): lax.all_to_all(packed, 'tile', split_axis=0, concat_axis=0, tiled=True)]
    all_to_all x1, starting transfers between devices: 4.6 us -> 3.48 us  [route_partials(): lax.all_to_all(chunks, 'sub', split_axis=0, concat_axis=0, tiled=True)]
    dot_general x1 -> x0, matrix products: 1.07 us -> none  [on_device(): jnp.dot(placing.astype(jnp.float32), runoff_blocks, precision=lax.Precisi...]
  transfers between devices with their start and end apart: 6 -> 6, of which waited for: 4 -> 4; matrix products, arithmetic and copies ran while one was open for 14% -> 16% of each run, Pallas kernels for 0% -> 0%
where the time goes in v9:
time: 75 us; the launch traced here: 74.5 us
  starting transfers between devices  29.6 us (39%)
  waiting for transfers between devices  16.1 us (21%)
  local copies, waits for them, and re-layouts  13.9 us (19%)
  other arithmetic  5.95 us (8%)
  matrix products  5 us (7%)
  Pallas kernels  2.94 us (4%)
  between operations  1.04 us (1%)
    all_to_all x1, starting transfers between devices, on_device(): lax.all_to_all(packed, 'tile', split_axis=0, concat_axis=0, tiled=True)  13.2 us
    all_to_all x1, waiting for transfers between devices, on_device(): lax.all_to_all(packed, 'tile', split_axis=0, concat_axis=0, tiled=True)  7.12 us
    all_to_all x1, waiting for transfers between devices, route_partials(): lax.all_to_all(chunks, 'sub', split_axis=0, concat_axis=0, tiled=True)  6.81 us
    unnamed x13, local copies, waits for them, and re-layouts  6.62 us
    ppermute x1, starting transfers between devices, route_partials(): lax.ppermute(messages[2], 'tile', [(i, (i + 1) % tile_count) for i in dev...  5.8 us
    dot_general x1, matrix products, on_device(): jnp.einsum('fpk,pkl->pfl', picked, weights, preferred_element_type=jnp.fl...  4.35 us
    all_to_all x1, starting transfers between devices, route_partials(): lax.all_to_all(chunks, 'sub', split_axis=0, concat_axis=0, tiled=True)  3.48 us
    ppermute x1, starting transfers between devices, route_partials(): lax.ppermute(messages[0], 'tile', [(i, (i - 1) % tile_count) for i in dev...  3.1 us
  transfers between devices with their start and end apart: 6, of which 4 were waited for; matrix products, arithmetic and copies ran while one was open for 16% of the time, Pallas kernels for 0%

profile of v9, /device:TPU:1, one launch (start us, length us, event | category | flops | bytes accessed | tf_op | source)
XLA Modules:
  0.0 74.5 jit_solution(11599762893233058012)
XLA Ops:
  0.6 0.7 %copy.39 = f32[6,8,128]{2,0,1:T(8,128)S(1)} copy(f32[6,8,128]{2,1,0:T(8,128)} %param.8) | data formatting | bytes 49152 | tf_op args[0]
  1.4 2.1 %collective-permute-start.1 = (f32[6,1,128]{2,0,1:T(8,128)S(1)}, f32[6,1,128]{2,0,1:T(8,128)S(1)}, u32[]{:S(2)}, u32[]{:S(2)}) collective-permute-start(f32[6,1,128]{2,0,1:T(8,128)S(1)} %get-tuple-element.26), channel_id=1, source_target_pairs={{0,1},{1,2},{2,3},{3,4},{4,5},{5,6},{6,7},{7,8},{8,9},{9,10},{10,1... | collective-permute-start | bytes 9224 | tf_op jit(solution)/shard_map/ppermute | solution.py:27
  3.5 1.9 %collective-permute-start = (f32[6,1,128]{2,0,1:T(8,128)S(1)}, f32[6,1,128]{2,0,1:T(8,128)S(1)}, u32[]{:S(2)}, u32[]{:S(2)}) collective-permute-start(f32[6,1,128]{2,0,1:T(8,128)S(1)} %get-tuple-element.25), channel_id=1, source_target_pairs={{1,0},{2,1},{3,2},{4,3},{5,4},{6,5},{7,6},{8,7},{9,8},{10,9},{11,1... | collective-permute-start | bytes 9224 | tf_op jit(solution)/shard_map/ppermute | solution.py:28
  5.4 0.1 fusion.19
  5.6 0.8 %pad_add_fusion = s32[104]{0:T(128)S(1)} fusion(s32[64]{0:T(128)} %param.15, s32[20]{0:T(128)} %param.10, s32[20]{0:T(128)} %param.9), kind=kLoop, calls=%fused_computation.92 | loop fusion | flops 208 | bytes 832 | tf_op jit(solution)/shard_map/concatenate | solution.py:218
  6.4 0.1 compare_select_fusion.2
  6.6 0.2 select_reduce_fusion.3
  6.8 0.1 select_reduce_fusion.2
  7.0 0.8 %gather_fusion.2 = s32[48]{0:T(128)S(1)} fusion(s32[20]{0:T(128)S(1)} %get-tuple-element.36, s32[1024]{0:T(1024)S(1)} %pad_clamp_fusion.1), kind=kCustom, calls=%fused_computation.2 | custom fusion | bytes 576 | tf_op jit(solution)/shard_map/gather | solution.py:175
  7.9 0.1 reduce_window_sum.23
  8.0 0.2 select_reduce_fusion.1
  8.3 0.1 select_reduce_fusion
  8.6 0.1 ge.29
  8.7 0.1 broadcast_in_dim.83
  8.8 1.3 %copy.49 = f32[3,8,64,128]{3,2,1,0:T(8,128)S(1)} copy(f32[3,8,64,128]{3,1,2,0:T(8,128)} %bitcast.61) | data formatting | bytes 1572864
  10.1 0.9 %slice.196.cond_ref = f32[20,64,128]{2,1,0:T(8,128)} slice(f32[24,64,128]{2,1,0:T(8,128)S(1)} %bitcast.58), slice={[0:20], [0:64], [0:128]} | slice | bytes 1310720 | tf_op jit(solution)/shard_map/reshape | solution.py:144
  11.0 1.3 %copy.50 = f32[3,8,64,128]{3,2,1,0:T(8,128)S(1)} copy(f32[3,8,64,128]{3,1,2,0:T(8,128)} %bitcast.62) | data formatting | bytes 1572864
  12.3 0.9 %slice.197.moist_ref = f32[20,64,128]{2,1,0:T(8,128)} slice(f32[24,64,128]{2,1,0:T(8,128)S(1)} %bitcast.59), slice={[0:20], [0:64], [0:128]} | slice | bytes 1310720 | tf_op jit(solution)/shard_map/reshape | solution.py:145
  13.1 0.1 convert_element_type.66
  13.3 0.1 concatenate.35
  13.4 0.6 gather_fusion
  14.0 4.4 %fusion.1 = f32[20,6,512]{2,1,0:T(8,128)S(1)} fusion(bf16[20,384,512]{2,1,0:T(8,128)(2,1)} %bitcast.56, bf16[20,6,384]{2,1,0:T(8,128)(2,1)S(1)} %gather_fusion), kind=kOutput, calls=%fused_computation.13 | convolution fusion | flops 47185920 | bytes 8202240 | tf_op jit(solution)/shard_map/fpk,pkl->pfl/dot_general | solution.py:230
  18.4 0.6 gather_fusion.1
  19.0 0.1 gather.18
  19.1 0.1 broadcast_select_fusion
  19.2 0.9 %maximum_maximum_fusion = f32[4,80,512]{2,1,0:T(8,128)} fusion(f32[1,8,512]{2,1,0:T(8,128)S(1)} %stack_reshape.15, f32[1,8,512]{2,1,0:T(8,128)S(1)} %stack_reshape.14, f32[1,8,512]{2,1,0:T(8,128)S(1)} %stack_reshape.13, f32[1,8,512]{2,1,0:T(8,128)S(1)} %stack_reshape.12, f32[4,72,512]{2,1,0:T(8,128)S(1)} %broadcast_select_fusion), kind=kLoop, calls=%fused_computation.5 | loop fusion | flops 655360 | bytes 1310720 | tf_op jit(solution)/shard_map/concatenate | solution.py:178
  20.1 3.5 %all-to-all-start = ((f32[4,80,512]{2,1,0:T(8,128)}), f32[4,80,512]{2,1,0:T(8,128)S(1)}, u32[]{:S(2)}, u32[]{:S(2)}) async-start(f32[4,80,512]{2,1,0:T(8,128)} %maximum_maximum_fusion), calls=%async_computation | async-start | bytes 1310720 | tf_op jit(solution)/shard_map/all_to_all | solution.py:185
  23.6 0.1 ge.31
  23.8 0.6 convert_bitcast_fusion.1.wet_ref
  24.4 6.8 %all-to-all-done = f32[4,80,512]{2,1,0:T(8,128)S(1)} async-done(((f32[4,80,512]{2,1,0:T(8,128)}), f32[4,80,512]{2,1,0:T(8,128)S(1)}, u32[]{:S(2)}, u32[]{:S(2)}) %all-to-all-start) | async-done | bytes 655392 | tf_op jit(solution)/shard_map/all_to_all | solution.py:185
  31.3 0.1 reshape.212
  31.4 5.8 %collective-permute-start.3 = (f32[104,512]{1,0:T(8,128)S(1)}, f32[104,512]{1,0:T(8,128)S(1)}, u32[]{:S(2)}, u32[]{:S(2)}) collective-permute-start(f32[104,512]{1,0:T(8,128)S(1)} %pad_maximum_fusion.2), channel_id=1, source_target_pairs={{0,4},{4,8},{8,12},{12,16},{16,20},{20,24},{24,28},{28,32},{32,36}... | collective-permute-start | bytes 638984 | tf_op jit(solution)/shard_map/ppermute | solution.py:198
  37.4 3.1 %collective-permute-start.2 = (f32[104,512]{1,0:T(8,128)S(1)}, f32[104,512]{1,0:T(8,128)S(1)}, u32[]{:S(2)}, u32[]{:S(2)}) collective-permute-start(f32[104,512]{1,0:T(8,128)S(1)} %pad_maximum_fusion.1), channel_id=1, source_target_pairs={{0,252},{4,0},{8,4},{12,8},{16,12},{20,16},{24,20},{28,24},{32,28}... | collective-permute-start | bytes 638984 | tf_op jit(solution)/shard_map/ppermute | solution.py:196
  40.6 0.6 collective-permute-done.3
  41.2 1.5 %collective-permute-done.2 = f32[104,512]{1,0:T(8,128)S(1)} collective-permute-done((f32[104,512]{1,0:T(8,128)S(1)}, f32[104,512]{1,0:T(8,128)S(1)}, u32[]{:S(2)}, u32[]{:S(2)}) %collective-permute-start.2) | collective-permute-done | bytes 213024 | tf_op jit(solution)/shard_map/ppermute | solution.py:196
  43.0 0.6 convolution_bitcast_fusion
  43.7 0.7 multiply_bitcast_fusion
  44.4 2.9 %shard_map.111 = (f32[20,64,128]{2,1,0:T(8,128)}, f32[64,128]{1,0:T(8,128)}) custom-call(f32[64,128]{1,0:T(8,128)} %get-tuple-element.24.source_ref, f32[64,128]{1,0:T(8,128)} %get-tuple-element.23.surface_ref, f32[64,128]{1,0:T(8,128)} %convert_bitcast_fusion.1.wet_ref, f32[20,64,128]{2,1,0:T(8,128)} %slice.196.cond_ref, f32[20,64,128]{2,1,0:T(8,128)} %slice.197.moist_ref), custom_call_target="tpu_custom_call" | custom-call | tf_op jit(solution)/shard_map/pallas_call | solution.py:130
  47.3 1.4 %gather_fusion.3 = f32[128,128]{1,0:T(8,128)S(1)} fusion(f32[64,128]{1,0:T(8,128)} %get-tuple-element.7, s32[1024]{0:T(1024)S(1)} %pad_clamp_fusion), kind=kCustom, calls=%fused_computation.3 | custom fusion | bytes 131584 | tf_op jit(solution)/shard_map/gather | solution.py:246
  48.7 0.1 broadcast_select_fusion.1
  48.9 0.7 select_maximum_fusion
  49.6 13.2 %all-to-all-start.1 = ((f32[64,3,128]{2,1,0:T(4,128)}), f32[64,3,128]{2,1,0:T(4,128)S(1)}, u32[]{:S(2)}, u32[]{:S(2)}) async-start(f32[64,3,128]{2,1,0:T(4,128)} %select_maximum_fusion), calls=%async_computation.1 | async-start | bytes 262144 | tf_op jit(solution)/shard_map/all_to_all | solution.py:252
  62.9 0.7 copy.44
  63.6 1.2 %pad.73 = f32[24,64,128]{2,1,0:T(8,128)S(1)} pad(f32[20,64,128]{2,1,0:T(8,128)} %get-tuple-element.6, f32[]{:T(128)} %constant.109.clone.1), padding=0_4x0_0x0_0 | pad | bytes 1441796
  64.7 1.3 %copy.51 = f32[3,8,64,128]{3,1,2,0:T(8,128)} copy(f32[3,8,64,128]{3,2,1,0:T(8,128)S(1)} %bitcast.57) | data formatting | bytes 1572864
  66.1 7.1 %all-to-all-done.1 = f32[64,3,128]{2,1,0:T(4,128)S(1)} async-done(((f32[64,3,128]{2,1,0:T(4,128)}), f32[64,3,128]{2,1,0:T(4,128)S(1)}, u32[]{:S(2)}, u32[]{:S(2)}) %all-to-all-start.1) | async-done | bytes 98336 | tf_op jit(solution)/shard_map/all_to_all | solution.py:252
  73.3 0.6 convert_bitcast_fusion.2
  73.9 0.7 slice_bitcast_fusion
  (63 shorter events, 1.5 us)
Async XLA Ops:
  1.4 11.9 %collective-permute-start.1 = (f32[6,1,128]{2,0,1:T(8,128)S(1)}, f32[6,1,128]{2,0,1:T(8,128)S(1)}, u32[]{:S(2)}, u32[]{:S(2)}) collective-permute-start(f32[6,1,128]{2,0,1:T(8,128)S(1)} %get-tuple-element.26), channel_id=1, source_target_pairs={{0,1},{1,2},{2,3},{3,4},{4,5},{5,6},{6,7},{7,8},{8,9},{9,10},{10,1... | collective-permute-start | bytes 9224 | tf_op jit(solution)/shard_map/ppermute | solution.py:27
  3.5 9.8 %collective-permute-start = (f32[6,1,128]{2,0,1:T(8,128)S(1)}, f32[6,1,128]{2,0,1:T(8,128)S(1)}, u32[]{:S(2)}, u32[]{:S(2)}) collective-permute-start(f32[6,1,128]{2,0,1:T(8,128)S(1)} %get-tuple-element.25), channel_id=1, source_target_pairs={{1,0},{2,1},{3,2},{4,3},{5,4},{6,5},{7,6},{8,7},{9,8},{10,9},{11,1... | collective-permute-start | bytes 9224 | tf_op jit(solution)/shard_map/ppermute | solution.py:28
  14.0 9.8 %copy-start = (s32[8192]{0:T(1024)S(1)}, s32[8192]{0:T(1024)}, u32[]{:S(2)}) copy-start(s32[8192]{0:T(1024)} %param.12) | copy-start | bytes 98308
  20.1 11.1 %all-to-all-start = ((f32[4,80,512]{2,1,0:T(8,128)}), f32[4,80,512]{2,1,0:T(8,128)S(1)}, u32[]{:S(2)}, u32[]{:S(2)}) async-start(f32[4,80,512]{2,1,0:T(8,128)} %maximum_maximum_fusion), calls=%async_computation | async-start | bytes 1310720 | tf_op jit(solution)/shard_map/all_to_all | solution.py:185
  31.4 9.8 %collective-permute-start.3 = (f32[104,512]{1,0:T(8,128)S(1)}, f32[104,512]{1,0:T(8,128)S(1)}, u32[]{:S(2)}, u32[]{:S(2)}) collective-permute-start(f32[104,512]{1,0:T(8,128)S(1)} %pad_maximum_fusion.2), channel_id=1, source_target_pairs={{0,4},{4,8},{8,12},{12,16},{16,20},{20,24},{24,28},{28,32},{32,36}... | collective-permute-start | bytes 638984 | tf_op jit(solution)/shard_map/ppermute | solution.py:198
  37.4 5.3 %collective-permute-start.2 = (f32[104,512]{1,0:T(8,128)S(1)}, f32[104,512]{1,0:T(8,128)S(1)}, u32[]{:S(2)}, u32[]{:S(2)}) collective-permute-start(f32[104,512]{1,0:T(8,128)S(1)} %pad_maximum_fusion.1), channel_id=1, source_target_pairs={{0,252},{4,0},{8,4},{12,8},{16,12},{20,16},{24,20},{28,24},{32,28}... | collective-permute-start | bytes 638984 | tf_op jit(solution)/shard_map/ppermute | solution.py:196
  49.6 23.6 %all-to-all-start.1 = ((f32[64,3,128]{2,1,0:T(4,128)}), f32[64,3,128]{2,1,0:T(4,128)S(1)}, u32[]{:S(2)}, u32[]{:S(2)}) async-start(f32[64,3,128]{2,1,0:T(4,128)} %select_maximum_fusion), calls=%async_computation.1 | async-start | bytes 262144 | tf_op jit(solution)/shard_map/all_to_all | solution.py:252

commit v10 on v8

--- a/solution.py
+++ b/solution.py
@@ -182,7 +182,13 @@
         ],
         axis=1,
     )
-    by_sub = lax.all_to_all(chunks, "sub", split_axis=0, concat_axis=0, tiled=True)
+    sub_index = lax.axis_index("sub")
+    by_sub = [lax.dynamic_index_in_dim(chunks, sub_index, 0, keepdims=False)]
+    for shift in range(1, sub_count):
+        chunk = lax.dynamic_index_in_dim(chunks, (sub_index + shift) % sub_count, 0, keepdims=False)
+        route = [(i, (i + shift) % sub_count) for i in range(sub_count)]
+        by_sub.append(lax.ppermute(chunk, "sub", route))
+    by_sub = jnp.stack(by_sub)
     part_rows = CAP_P * field_count
     got_ids = by_sub[:, chunk_rows, : 3 * CAP_P]
     messages = []

time: 69.9 us -> 70.3 us (level)
  starting transfers between devices: 28.5 us -> 26.2 us
  local copies, waits for them, and re-layouts: 10.9 us -> 13.2 us
  waiting for transfers between devices: 14.9 us -> 16 us
  other arithmetic: 5.08 us -> 4.32 us
    ppermute x0 -> x3, waiting for transfers between devices: none -> 5.84 us  [route_partials(): by_sub.append(lax.ppermute(chunk, 'sub', route))]
    all_to_all x1 -> x0, waiting for transfers between devices: 4.7 us -> none  [route_partials(): lax.all_to_all(chunks, 'sub', split_axis=0, concat_axis=0, tiled=True)]
    all_to_all x1 -> x0, starting transfers between devices: 4.6 us -> none  [route_partials(): lax.all_to_all(chunks, 'sub', split_axis=0, concat_axis=0, tiled=True)]
    unnamed x17 -> x13, local copies, waits for them, and re-layouts: 5 us -> 7.26 us
    ppermute x0 -> x3, starting transfers between devices: none -> 2.21 us  [route_partials(): by_sub.append(lax.ppermute(chunk, 'sub', route))]
    concatenate x1, other arithmetic: 0.89 us -> 0.05 us  [route_partials(): jnp.concatenate([rows.reshape(sub_count, chunk_rows, width), jnp.stack([i...]
  transfers between devices with their start and end apart: 6 -> 8, of which waited for: 4 -> 6; matrix products, arithmetic and copies ran while one was open for 14% -> 17% of each run, Pallas kernels for 0% -> 0%
where the time goes in v10:
time: 70.3 us; the launch traced here: 69.9 us
  starting transfers between devices  26.2 us (37%)
  waiting for transfers between devices  16 us (23%)
  local copies, waits for them, and re-layouts  13.2 us (19%)
  matrix products  6.07 us (9%)
  other arithmetic  4.32 us (6%)
  Pallas kernels  2.98 us (4%)
  between operations  1.1 us (2%)
    all_to_all x1, starting transfers between devices, on_device(): lax.all_to_all(packed, 'tile', split_axis=0, concat_axis=0, tiled=True)  12.2 us
    unnamed x13, local copies, waits for them, and re-layouts  7.26 us
    all_to_all x1, waiting for transfers between devices, on_device(): lax.all_to_all(packed, 'tile', split_axis=0, concat_axis=0, tiled=True)  6.94 us
    ppermute x3, waiting for transfers between devices, route_partials(): by_sub.append(lax.ppermute(chunk, 'sub', route))  5.84 us
    ppermute x1, starting transfers between devices, route_partials(): lax.ppermute(messages[2], 'tile', [(i, (i + 1) % tile_count) for i in dev...  5.8 us
    dot_general x1, matrix products, on_device(): jnp.einsum('fpk,pkl->pfl', picked, weights, preferred_element_type=jnp.fl...  4.35 us
    pallas_call x1, Pallas kernels, soil_update(): pl.pallas_call(soil_kernel, grid=(grid,), in_specs=[plane, plane, plane,...  2.98 us
    ppermute x1, waiting for transfers between devices, route_partials(): lax.ppermute(messages[0], 'tile', [(i, (i - 1) % tile_count) for i in dev...  2.57 us
  transfers between devices with their start and end apart: 8, of which 6 were waited for; matrix products, arithmetic and copies ran while one was open for 17% of the time, Pallas kernels for 0%

profile of v10, /device:TPU:1, one launch (start us, length us, event | category | flops | bytes accessed | tf_op | source)
XLA Modules:
  0.0 69.9 jit_solution(1513797013030170302)
XLA Ops:
  0.6 0.7 %copy.32 = f32[6,8,128]{2,0,1:T(8,128)S(1)} copy(f32[6,8,128]{2,1,0:T(8,128)} %param.8) | data formatting | bytes 49152 | tf_op args[0]
  1.4 2.1 %collective-permute-start.1 = (f32[6,1,128]{2,0,1:T(8,128)S(1)}, f32[6,1,128]{2,0,1:T(8,128)S(1)}, u32[]{:S(2)}, u32[]{:S(2)}) collective-permute-start(f32[6,1,128]{2,0,1:T(8,128)S(1)} %get-tuple-element.25), channel_id=1, source_target_pairs={{0,1},{1,2},{2,3},{3,4},{4,5},{5,6},{6,7},{7,8},{8,9},{9,10},{10,1... | collective-permute-start | bytes 9224 | tf_op jit(solution)/shard_map/ppermute | solution.py:27
  3.5 1.9 %collective-permute-start = (f32[6,1,128]{2,0,1:T(8,128)S(1)}, f32[6,1,128]{2,0,1:T(8,128)S(1)}, u32[]{:S(2)}, u32[]{:S(2)}) collective-permute-start(f32[6,1,128]{2,0,1:T(8,128)S(1)} %get-tuple-element.24), channel_id=1, source_target_pairs={{1,0},{2,1},{3,2},{4,3},{5,4},{6,5},{7,6},{8,7},{9,8},{10,9},{11,1... | collective-permute-start | bytes 9224 | tf_op jit(solution)/shard_map/ppermute | solution.py:28
  5.5 0.1 fusion.19
  5.6 0.8 %pad_add_fusion = s32[104]{0:T(128)S(1)} fusion(s32[64]{0:T(128)} %param.15, s32[20]{0:T(128)} %param.10, s32[20]{0:T(128)} %param.9), kind=kLoop, calls=%fused_computation.99 | loop fusion | flops 208 | bytes 832 | tf_op jit(solution)/shard_map/concatenate | solution.py:224
  6.4 0.1 compare_select_fusion.2
  6.6 0.2 select_reduce_fusion.3
  6.8 0.1 select_reduce_fusion.2
  7.0 0.8 %gather_fusion.2 = s32[48]{0:T(128)S(1)} fusion(s32[20]{0:T(128)S(1)} %get-tuple-element.33, s32[1024]{0:T(1024)S(1)} %pad_clamp_fusion), kind=kCustom, calls=%fused_computation.2 | custom fusion | bytes 576 | tf_op jit(solution)/shard_map/gather | solution.py:175
  8.0 0.1 reduce_window_sum.23
  8.1 0.2 select_reduce_fusion.1
  8.3 0.1 select_reduce_fusion
  8.6 0.1 ge.11
  8.7 0.1 broadcast_in_dim.66
  8.8 1.3 %copy.41 = f32[3,8,64,128]{3,2,1,0:T(8,128)S(1)} copy(f32[3,8,64,128]{3,1,2,0:T(8,128)} %bitcast.78) | data formatting | bytes 1572864
  10.1 0.9 %slice.191.cond_ref = f32[20,64,128]{2,1,0:T(8,128)} slice(f32[24,64,128]{2,1,0:T(8,128)S(1)} %bitcast.66), slice={[0:20], [0:64], [0:128]} | slice | bytes 1310720 | tf_op jit(solution)/shard_map/reshape | solution.py:144
  11.0 1.3 %copy.42 = f32[3,8,64,128]{3,2,1,0:T(8,128)S(1)} copy(f32[3,8,64,128]{3,1,2,0:T(8,128)} %bitcast.79) | data formatting | bytes 1572864
  12.3 0.9 %slice.192.moist_ref = f32[20,64,128]{2,1,0:T(8,128)} slice(f32[24,64,128]{2,1,0:T(8,128)S(1)} %bitcast.67), slice={[0:20], [0:64], [0:128]} | slice | bytes 1310720 | tf_op jit(solution)/shard_map/reshape | solution.py:145
  13.2 0.1 convert_element_type.51
  13.3 0.1 concatenate.35
  13.4 0.6 gather_fusion
  14.0 4.4 %fusion.1 = f32[20,6,512]{2,1,0:T(8,128)S(1)} fusion(bf16[20,384,512]{2,1,0:T(8,128)(2,1)} %bitcast.64, bf16[20,6,384]{2,1,0:T(8,128)(2,1)S(1)} %gather_fusion), kind=kOutput, calls=%fused_computation.16 | convolution fusion | flops 47185920 | bytes 8202240 | tf_op jit(solution)/shard_map/fpk,pkl->pfl/dot_general | solution.py:236
  18.4 0.6 gather_fusion.1
  19.0 0.1 gather.13
  19.1 0.1 broadcast_select_fusion
  19.4 1.5 %collective-permute-start.4 = (f32[80,512]{1,0:T(8,128)S(1)}, f32[80,512]{1,0:T(8,128)S(1)}, u32[]{:S(2)}, u32[]{:S(2)}) collective-permute-start(f32[80,512]{1,0:T(8,128)S(1)} %get-tuple-element.15), channel_id=1, source_target_pairs={{0,3},{1,0},{2,1},{3,2},{4,7},{5,4},{6,5},{7,6},{8,11},{9,8},{10,9... | collective-permute-start | bytes 491528 | tf_op jit(solution)/shard_map/ppermute | solution.py:190
  20.9 0.7 collective-permute-start.2
  21.6 0.6 convert_bitcast_fusion.1.wet_ref
  22.2 1.4 %collective-permute-done.4 = f32[80,512]{1,0:T(8,128)S(1)} collective-permute-done((f32[80,512]{1,0:T(8,128)S(1)}, f32[80,512]{1,0:T(8,128)S(1)}, u32[]{:S(2)}, u32[]{:S(2)}) %collective-permute-start.4) | collective-permute-done | bytes 163872 | tf_op jit(solution)/shard_map/ppermute | solution.py:190
  23.6 3.1 %collective-permute-done.3 = f32[80,512]{1,0:T(8,128)S(1)} collective-permute-done((f32[80,512]{1,0:T(8,128)S(1)}, f32[80,512]{1,0:T(8,128)S(1)}, u32[]{:S(2)}, u32[]{:S(2)}) %collective-permute-start.3) | collective-permute-done | bytes 163872 | tf_op jit(solution)/shard_map/ppermute | solution.py:190
  26.7 1.4 %collective-permute-done.2 = f32[80,512]{1,0:T(8,128)S(1)} collective-permute-done((f32[80,512]{1,0:T(8,128)S(1)}, f32[80,512]{1,0:T(8,128)S(1)}, u32[]{:S(2)}, u32[]{:S(2)}) %collective-permute-start.2) | collective-permute-done | bytes 163872 | tf_op jit(solution)/shard_map/ppermute | solution.py:190
  28.3 5.8 %collective-permute-start.6 = (f32[104,512]{1,0:T(8,128)S(1)}, f32[104,512]{1,0:T(8,128)S(1)}, u32[]{:S(2)}, u32[]{:S(2)}) collective-permute-start(f32[104,512]{1,0:T(8,128)S(1)} %pad_maximum_fusion.3), channel_id=1, source_target_pairs={{0,4},{4,8},{8,12},{12,16},{16,20},{20,24},{24,28},{28,32},{32,36}... | collective-permute-start | bytes 638984 | tf_op jit(solution)/shard_map/ppermute | solution.py:204
  34.3 2.0 %collective-permute-start.5 = (f32[104,512]{1,0:T(8,128)S(1)}, f32[104,512]{1,0:T(8,128)S(1)}, u32[]{:S(2)}, u32[]{:S(2)}) collective-permute-start(f32[104,512]{1,0:T(8,128)S(1)} %pad_maximum_fusion.2), channel_id=1, source_target_pairs={{0,252},{4,0},{8,4},{12,8},{16,12},{20,16},{24,20},{28,24},{32,28}... | collective-permute-start | bytes 638984 | tf_op jit(solution)/shard_map/ppermute | solution.py:202
  36.4 0.6 collective-permute-done.6
  37.0 2.6 %collective-permute-done.5 = f32[104,512]{1,0:T(8,128)S(1)} collective-permute-done((f32[104,512]{1,0:T(8,128)S(1)}, f32[104,512]{1,0:T(8,128)S(1)}, u32[]{:S(2)}, u32[]{:S(2)}) %collective-permute-start.5) | collective-permute-done | bytes 213024 | tf_op jit(solution)/shard_map/ppermute | solution.py:202
  39.9 0.6 convolution_bitcast_fusion
  40.6 0.7 multiply_bitcast_fusion
  41.3 3.0 %shard_map.111 = (f32[20,64,128]{2,1,0:T(8,128)}, f32[64,128]{1,0:T(8,128)}) custom-call(f32[64,128]{1,0:T(8,128)} %get-tuple-element.23.source_ref, f32[64,128]{1,0:T(8,128)} %get-tuple-element.22.surface_ref, f32[64,128]{1,0:T(8,128)} %convert_bitcast_fusion.1.wet_ref, f32[20,64,128]{2,1,0:T(8,128)} %slice.191.cond_ref, f32[20,64,128]{2,1,0:T(8,128)} %slice.192.moist_ref), custom_call_target="tpu_custom_call" | custom-call | tf_op jit(solution)/shard_map/pallas_call | solution.py:130
  44.3 1.1 %fusion.23 = f32[128,128]{1,0:T(8,128)S(1)} fusion(f32[64,128]{1,0:T(8,128)} %get-tuple-element.7, s32[64]{0:T(128)S(1)} %get-tuple-element.41), kind=kOutput, calls=%fused_computation.54 | convolution fusion | flops 12591104 | bytes 98560 | tf_op jit(solution)/shard_map/dot_general | solution.py:250
  45.4 0.7 all_to_all.8
  46.1 12.2 %all-to-all-start = ((f32[64,1,384]{2,1,0:T(1,128)}), f32[64,1,384]{2,1,0:T(1,128)S(1)}, u32[]{:S(2)}, u32[]{:S(2)}) async-start(f32[64,1,384]{2,1,0:T(1,128)} %all_to_all.8), calls=%async_computation | async-start | bytes 196608 | tf_op jit(solution)/shard_map/all_to_all | solution.py:259
  58.3 0.7 %copy.36 = bf16[1,6,16,512]{3,1,2,0:T(8,128)(2,1)} copy(bf16[1,6,16,512]{3,2,1,0:T(8,128)(2,1)S(1)} %convert_bitcast_fusion) | data formatting | bytes 196608
  59.0 1.2 %pad.88 = f32[24,64,128]{2,1,0:T(8,128)S(1)} pad(f32[20,64,128]{2,1,0:T(8,128)} %get-tuple-element.6, f32[]{:T(128)} %constant.133.clone.1), padding=0_4x0_0x0_0 | pad | bytes 1441796
  60.2 1.3 %copy.43 = f32[3,8,64,128]{3,1,2,0:T(8,128)} copy(f32[3,8,64,128]{3,2,1,0:T(8,128)S(1)} %bitcast.65) | data formatting | bytes 1572864
  61.5 6.9 %all-to-all-done = f32[64,1,384]{2,1,0:T(1,128)S(1)} async-done(((f32[64,1,384]{2,1,0:T(1,128)}), f32[64,1,384]{2,1,0:T(1,128)S(1)}, u32[]{:S(2)}, u32[]{:S(2)}) %all-to-all-start) | async-done | bytes 98336 | tf_op jit(solution)/shard_map/all_to_all | solution.py:259
  68.5 0.1 copy.34
  68.6 0.6 fusion.30
  69.2 0.7 %copy.35 = f32[1,1,64,2,128]{4,3,2,1,0:T(2,128)} copy(f32[1,1,64,2,128]{2,4,3,1,0:T(8,128)S(1)} %bitcast.85) | data formatting | bytes 131072
  (68 shorter events, 1.6 us)
Async XLA Ops:
  1.4 11.9 %collective-permute-start.1 = (f32[6,1,128]{2,0,1:T(8,128)S(1)}, f32[6,1,128]{2,0,1:T(8,128)S(1)}, u32[]{:S(2)}, u32[]{:S(2)}) collective-permute-start(f32[6,1,128]{2,0,1:T(8,128)S(1)} %get-tuple-element.25), channel_id=1, source_target_pairs={{0,1},{1,2},{2,3},{3,4},{4,5},{5,6},{6,7},{7,8},{8,9},{9,10},{10,1... | collective-permute-start | bytes 9224 | tf_op jit(solution)/shard_map/ppermute | solution.py:27
  3.5 9.8 %collective-permute-start = (f32[6,1,128]{2,0,1:T(8,128)S(1)}, f32[6,1,128]{2,0,1:T(8,128)S(1)}, u32[]{:S(2)}, u32[]{:S(2)}) collective-permute-start(f32[6,1,128]{2,0,1:T(8,128)S(1)} %get-tuple-element.24), channel_id=1, source_target_pairs={{1,0},{2,1},{3,2},{4,3},{5,4},{6,5},{7,6},{8,7},{9,8},{10,9},{11,1... | collective-permute-start | bytes 9224 | tf_op jit(solution)/shard_map/ppermute | solution.py:28
  14.0 7.5 %copy-start = (s32[8192]{0:T(1024)S(1)}, s32[8192]{0:T(1024)}, u32[]{:S(2)}) copy-start(s32[8192]{0:T(1024)} %param.12) | copy-start | bytes 98308
  19.4 4.2 %collective-permute-start.4 = (f32[80,512]{1,0:T(8,128)S(1)}, f32[80,512]{1,0:T(8,128)S(1)}, u32[]{:S(2)}, u32[]{:S(2)}) collective-permute-start(f32[80,512]{1,0:T(8,128)S(1)} %get-tuple-element.15), channel_id=1, source_target_pairs={{0,3},{1,0},{2,1},{3,2},{4,7},{5,4},{6,5},{7,6},{8,11},{9,8},{10,9... | collective-permute-start | bytes 491528 | tf_op jit(solution)/shard_map/ppermute | solution.py:190
  20.9 5.8 %collective-permute-start.3 = (f32[80,512]{1,0:T(8,128)S(1)}, f32[80,512]{1,0:T(8,128)S(1)}, u32[]{:S(2)}, u32[]{:S(2)}) collective-permute-start(f32[80,512]{1,0:T(8,128)S(1)} %get-tuple-element.16), channel_id=1, source_target_pairs={{0,2},{1,3},{2,0},{3,1},{4,6},{5,7},{6,4},{7,5},{8,10},{9,11},{10,... | collective-permute-start | bytes 491528 | tf_op jit(solution)/shard_map/ppermute | solution.py:190
  20.9 7.1 %collective-permute-start.2 = (f32[80,512]{1,0:T(8,128)S(1)}, f32[80,512]{1,0:T(8,128)S(1)}, u32[]{:S(2)}, u32[]{:S(2)}) collective-permute-start(f32[80,512]{1,0:T(8,128)S(1)} %get-tuple-element.17), channel_id=1, source_target_pairs={{0,1},{1,2},{2,3},{3,0},{4,5},{5,6},{6,7},{7,4},{8,9},{9,10},{10,1... | collective-permute-start | bytes 491528 | tf_op jit(solution)/shard_map/ppermute | solution.py:190
  28.3 8.7 %collective-permute-start.6 = (f32[104,512]{1,0:T(8,128)S(1)}, f32[104,512]{1,0:T(8,128)S(1)}, u32[]{:S(2)}, u32[]{:S(2)}) collective-permute-start(f32[104,512]{1,0:T(8,128)S(1)} %pad_maximum_fusion.3), channel_id=1, source_target_pairs={{0,4},{4,8},{8,12},{12,16},{16,20},{20,24},{24,28},{28,32},{32,36}... | collective-permute-start | bytes 638984 | tf_op jit(solution)/shard_map/ppermute | solution.py:204
  34.3 5.3 %collective-permute-start.5 = (f32[104,512]{1,0:T(8,128)S(1)}, f32[104,512]{1,0:T(8,128)S(1)}, u32[]{:S(2)}, u32[]{:S(2)}) collective-permute-start(f32[104,512]{1,0:T(8,128)S(1)} %pad_maximum_fusion.2), channel_id=1, source_target_pairs={{0,252},{4,0},{8,4},{12,8},{16,12},{20,16},{24,20},{28,24},{32,28}... | collective-permute-start | bytes 638984 | tf_op jit(solution)/shard_map/ppermute | solution.py:202
  46.1 22.3 %all-to-all-start = ((f32[64,1,384]{2,1,0:T(1,128)}), f32[64,1,384]{2,1,0:T(1,128)S(1)}, u32[]{:S(2)}, u32[]{:S(2)}) async-start(f32[64,1,384]{2,1,0:T(1,128)} %all_to_all.8), calls=%async_computation | async-start | bytes 196608 | tf_op jit(solution)/shard_map/all_to_all | solution.py:259

commit v11 on v8

--- a/solution.py
+++ b/solution.py
@@ -70,34 +70,31 @@
     return jnp.stack(solved)
 
 
-def soil_kernel(
-    source_ref, surface_ref, wet_ref, cond_ref, moist_ref, out_ref, runoff_ref, inv_ref, ratio_ref
+def response_kernel(
+    cond_ref, moist_ref, base_ref, unit_ref, base_drain_ref, unit_drain_ref, inv_ref, ratio_ref
 ):
     layers = cond_ref.shape[0]
-    groups = cond_ref.shape[1] // 32
-
-    def one_group(g, carry):
-        rows = pl.ds(pl.multiple_of(g * 32, 32), 32)
-        previous_cond = None
-        previous_inv = None
-        for k in range(layers):
-            cond = cond_ref[k, rows, :]
-            diagonal = 1.0 + cond
-            if k > 0:
-                diagonal = diagonal + previous_cond - previous_cond * previous_cond * previous_inv
-            pivot_inv = 1.0 / diagonal
-            inv_ref[k] = pivot_inv
-            ratio_ref[k] = -cond * pivot_inv
-            previous_cond = cond
-            previous_inv = pivot_inv
-        source = source_ref[rows, :]
-        moisture = [moist_ref[k, rows, :] for k in range(layers)]
-        drainage = jnp.zeros_like(source)
+    rows = pl.ds(0, cond_ref.shape[1])
+    previous_cond = None
+    previous_inv = None
+    for k in range(layers):
+        cond = cond_ref[k, rows, :]
+        diagonal = 1.0 + cond
+        if k > 0:
+            diagonal = diagonal + previous_cond - previous_cond * previous_cond * previous_inv
+        pivot_inv = 1.0 / diagonal
+        inv_ref[k] = pivot_inv
+        ratio_ref[k] = -cond * pivot_inv
+        previous_cond = cond
+        previous_inv = pivot_inv
+
+    def solve(moisture, source):
+        drainage = None
         for substep in range(SOIL_STEPS):
             forward = []
             for k in range(layers):
                 if k == 0:
-                    column_value = moisture[0] + source
+                    column_value = moisture[0] if source is None else moisture[0] + source
                 else:
                     column_value = moisture[k] + cond_ref[k - 1, rows, :] * forward[k - 1]
                 forward.append(column_value * inv_ref[k])
@@ -105,46 +102,46 @@
             for k in range(layers - 2, -1, -1):
                 solved.insert(0, forward[k] - ratio_ref[k] * solved[0])
             moisture = solved
-            drainage = drainage + cond_ref[layers - 1, rows, :] * moisture[layers - 1]
-        for k in range(layers):
-            out_ref[k, rows, :] = moisture[k]
-        runoff_ref[rows, :] = wet_ref[rows, :] * (SOIL_STEPS * surface_ref[rows, :] + drainage)
-        return carry
-
-    lax.fori_loop(0, groups, one_group, 0)
-
-
-def soil_update(forcing, land_mask, conductance, soil_moisture):
-    wetness = land_mask.astype(jnp.float32)
-    source = wetness * (
-        jax.nn.softplus(forcing[0]) * jax.nn.sigmoid(forcing[1])
-        - 0.5 * jax.nn.sigmoid(forcing[2]) * jax.nn.softplus(forcing[3])
-    )
-    surface = wetness * jax.nn.softplus(forcing[0]) * (1.0 - jax.nn.sigmoid(forcing[1]))
-    layers, cells = conductance.shape
-    rows = cells // 128
+            drained = cond_ref[layers - 1, rows, :] * moisture[layers - 1]
+            drainage = drained if drainage is None else drainage + drained
+        return (moisture, drainage)
+
+    base, base_drain = solve([moist_ref[k, rows, :] for k in range(layers)], None)
+    for k in range(layers):
+        base_ref[k, rows, :] = base[k]
+    base_drain_ref[rows, :] = base_drain
+    zero = jnp.zeros_like(base_drain)
+    unit, unit_drain = solve([zero] * layers, zero + 1.0)
+    for k in range(layers):
+        unit_ref[k, rows, :] = unit[k]
+    unit_drain_ref[rows, :] = unit_drain
+
+
+def soil_response(conductance, soil_moisture):
+    layers, rows, lanes = conductance.shape
     grid = 2
     block = rows // grid
-    plane = pl.BlockSpec((block, 128), lambda i: (i, 0))
-    stack = pl.BlockSpec((layers, block, 128), lambda i: (0, i, 0))
-    moisture, runoff = pl.pallas_call(
-        soil_kernel,
+    plane = pl.BlockSpec((block, lanes), lambda i: (i, 0))
+    stack = pl.BlockSpec((layers, block, lanes), lambda i: (0, i, 0))
+    layer_shape = jax.ShapeDtypeStruct((layers, rows, lanes), jnp.float32)
+    plane_shape = jax.ShapeDtypeStruct((rows, lanes), jnp.float32)
+    return pl.pallas_call(
+        response_kernel,
         grid=(grid,),
-        in_specs=[plane, plane, plane, stack, stack],
-        out_specs=[stack, plane],
-        scratch_shapes=[pltpu.VMEM((layers, 32, 128), jnp.float32)] * 2,
-        out_shape=[
-            jax.ShapeDtypeStruct((layers, rows, 128), jnp.float32),
-            jax.ShapeDtypeStruct((rows, 128), jnp.float32),
-        ],
-    )(
-        source.reshape(rows, 128),
-        surface.reshape(rows, 128),
-        wetness.reshape(rows, 128),
-        conductance.reshape(layers, rows, 128),
-        soil_moisture.reshape(layers, rows, 128),
-    )
-    return (moisture.reshape(layers, cells), runoff.reshape(cells))
+        in_specs=[stack, stack],
+        out_specs=[stack, stack, plane, plane],
+        scratch_shapes=[pltpu.VMEM((layers, block, lanes), jnp.float32)] * 2,
+        out_shape=[layer_shape, layer_shape, plane_shape, plane_shape],
+    )(conductance, soil_moisture)
+
+
+def soil_update(source, surface, wetness, response):
+    base, unit, base_drain, unit_drain = response
+    layers, rows, lanes = base.shape
+    source = source.reshape(rows, lanes)
+    moisture = base + source[None] * unit
+    runoff = wetness * (SOIL_STEPS * surface.reshape(rows, lanes) + (base_drain + source * unit_drain))
+    return (moisture.reshape(layers, rows * lanes), runoff.reshape(rows * lanes))
 
 
 CAP_P = 4
@@ -231,7 +228,18 @@
     owned_sums = route_partials(partial_value, pair_land, tile_count, sub_count, tile_index)
     forcing = owned_sums.reshape(field_count, LB_DEV * LBLK)
     land_forcing = forcing.astype(jnp.bfloat16)
-    moisture, runoff = soil_update(forcing, land_mask, conductance, soil_moisture)
+    layers, cell_count = conductance.shape
+    tiles = (cell_count // RBLK, RBLK)
+    response = soil_response(
+        conductance.reshape((layers,) + tiles), soil_moisture.reshape((layers,) + tiles)
+    )
+    wetness = land_mask.astype(jnp.float32)
+    source = wetness * (
+        jax.nn.softplus(forcing[0]) * jax.nn.sigmoid(forcing[1])
+        - 0.5 * jax.nn.sigmoid(forcing[2]) * jax.nn.softplus(forcing[3])
+    )
+    surface = wetness * jax.nn.softplus(forcing[0]) * (1.0 - jax.nn.sigmoid(forcing[1]))
+    moisture, runoff = soil_update(source, surface, wetness.reshape(tiles), response)
     block_count = runoff.shape[0] // RBLK
     capacity = CAP_R
     runoff_blocks = runoff.reshape(block_count, RBLK)

time: 69.9 us -> 72.5 us (1.037)
  starting transfers between devices: 28.5 us -> 35 us
  waiting for transfers between devices: 14.9 us -> 12.9 us
  other arithmetic: 5.08 us -> 3.92 us
  local copies, waits for them, and re-layouts: 10.9 us -> 9.87 us
    ppermute x1, starting transfers between devices: 1.95 us -> 7.24 us  [route_partials(): lax.ppermute(messages[0], 'tile', [(i, (i - 1) % tile_count) for i in dev...]
    all_to_all x1, waiting for transfers between devices: 4.7 us -> 2.1 us  [route_partials(): lax.all_to_all(chunks, 'sub', split_axis=0, concat_axis=0, tiled=True)]
    ppermute x1, waiting for transfers between devices: 2.63 us -> 0.23 us  [route_partials(): lax.ppermute(messages[0], 'tile', [(i, (i - 1) % tile_count) for i in dev...]
    all_to_all x1, starting transfers between devices: 12.1 us -> 14.4 us  [on_device(): lax.all_to_all(packed, 'tile', split_axis=0, concat_axis=0, tiled=True)]
    ppermute x1, starting transfers between devices: 2.12 us -> 0.01 us  [padded(): before = lax.ppermute(last, axis, up)]
    ppermute x1, starting transfers between devices: 1.92 us -> 3.95 us  [padded(): after = lax.ppermute(initial, axis, down)]
    all_to_all x1, waiting for transfers between devices: 6.94 us -> 8.66 us  [on_device(): lax.all_to_all(packed, 'tile', split_axis=0, concat_axis=0, tiled=True)]
    reshape x2 -> x0, other arithmetic: 1.3 us -> none  [the longest x1 0.68 us: soil_update(): surface.reshape(rows, 128)]
  transfers between devices with their start and end apart: 6 -> 6, of which waited for: 4 -> 5; matrix products, arithmetic and copies ran while one was open for 14% -> 10% of each run, Pallas kernels for 0% -> 4%
where the time goes in v11:
time: 72.5 us; the launch traced here: 72.1 us
  starting transfers between devices  35 us (48%)
  waiting for transfers between devices  12.9 us (18%)
  local copies, waits for them, and re-layouts  9.87 us (14%)
  matrix products  6.16 us (8%)
  other arithmetic  3.92 us (5%)
  Pallas kernels  3.1 us (4%)
  between operations  1.09 us (2%)
    all_to_all x1, starting transfers between devices, on_device(): lax.all_to_all(packed, 'tile', split_axis=0, concat_axis=0, tiled=True)  14.4 us
    all_to_all x1, waiting for transfers between devices, on_device(): lax.all_to_all(packed, 'tile', split_axis=0, concat_axis=0, tiled=True)  8.66 us
    ppermute x1, starting transfers between devices, route_partials(): lax.ppermute(messages[0], 'tile', [(i, (i - 1) % tile_count) for i in dev...  7.24 us
    ppermute x1, starting transfers between devices, route_partials(): lax.ppermute(messages[2], 'tile', [(i, (i + 1) % tile_count) for i in dev...  5.8 us
    dot_general x1, matrix products, on_device(): jnp.einsum('fpk,pkl->pfl', picked, weights, preferred_element_type=jnp.fl...  4.42 us
    ppermute x1, starting transfers between devices, padded(): after = lax.ppermute(initial, axis, down)  3.95 us
    unnamed x21, local copies, waits for them, and re-layouts  3.92 us
    all_to_all x1, starting transfers between devices, route_partials(): lax.all_to_all(chunks, 'sub', split_axis=0, concat_axis=0, tiled=True)  3.66 us
  transfers between devices with their start and end apart: 6, of which 5 were waited for; matrix products, arithmetic and copies ran while one was open for 10% of the time, Pallas kernels for 4%

profile of v11, /device:TPU:1, one launch (start us, length us, event | category | flops | bytes accessed | tf_op | source)
XLA Modules:
  0.0 72.1 jit_solution(1866836813485512518)
XLA Ops:
  0.6 0.7 %copy.32 = f32[6,8,128]{2,0,1:T(8,128)S(1)} copy(f32[6,8,128]{2,1,0:T(8,128)} %param.8) | data formatting | bytes 49152 | tf_op args[0]
  1.4 4.0 %collective-permute-start = (f32[6,1,128]{2,0,1:T(8,128)S(1)}, f32[6,1,128]{2,0,1:T(8,128)S(1)}, u32[]{:S(2)}, u32[]{:S(2)}) collective-permute-start(f32[6,1,128]{2,0,1:T(8,128)S(1)} %get-tuple-element.23), channel_id=1, source_target_pairs={{1,0},{2,1},{3,2},{4,3},{5,4},{6,5},{7,6},{8,7},{9,8},{10,9},{11,1... | collective-permute-start | bytes 9224 | tf_op jit(solution)/shard_map/ppermute | solution.py:28
  5.4 0.8 %pad_add_fusion = s32[104]{0:T(128)S(1)} fusion(s32[64]{0:T(128)} %param.15, s32[20]{0:T(128)} %param.10, s32[20]{0:T(128)} %param.9), kind=kLoop, calls=%fused_computation.103 | loop fusion | flops 208 | bytes 832 | tf_op jit(solution)/shard_map/concatenate | solution.py:215
  6.2 0.1 compare_select_fusion.3
  6.4 0.2 select_reduce_fusion.3
  6.6 0.1 select_reduce_fusion.2
  6.8 0.1 fusion.19
  6.9 0.8 %gather_fusion.2 = s32[48]{0:T(128)S(1)} fusion(s32[20]{0:T(128)S(1)} %get-tuple-element.32, s32[1024]{0:T(1024)S(1)} %pad_clamp_fusion), kind=kCustom, calls=%fused_computation.2 | custom fusion | bytes 576 | tf_op jit(solution)/shard_map/gather | solution.py:172
  7.8 0.1 reduce_window_sum.23
  7.9 0.2 select_reduce_fusion.1
  8.2 0.1 ge.11
  8.3 0.1 broadcast_in_dim.66
  8.5 1.0 %collective-permute-done.1 = f32[6,1,128]{2,0,1:T(8,128)S(1)} collective-permute-done((f32[6,1,128]{2,0,1:T(8,128)S(1)}, f32[6,1,128]{2,0,1:T(8,128)S(1)}, u32[]{:S(2)}, u32[]{:S(2)}) %collective-permute-start.1) | collective-permute-done | bytes 3104 | tf_op jit(solution)/shard_map/ppermute | solution.py:27
  9.6 0.1 concatenate.35
  9.7 0.6 gather_fusion
  10.3 4.4 %fusion.1 = f32[20,6,512]{2,1,0:T(8,128)S(1)} fusion(bf16[20,384,512]{2,1,0:T(8,128)(2,1)} %bitcast.60, bf16[20,6,384]{2,1,0:T(8,128)(2,1)S(1)} %gather_fusion), kind=kOutput, calls=%fused_computation.11 | convolution fusion | flops 47185920 | bytes 8202240 | tf_op jit(solution)/shard_map/fpk,pkl->pfl/dot_general | solution.py:227
  14.7 0.6 gather_fusion.1
  15.4 0.1 gather.13
  15.5 0.1 broadcast_select_fusion
  15.6 0.9 %maximum_maximum_fusion = f32[4,80,512]{2,1,0:T(8,128)} fusion(f32[1,8,512]{2,1,0:T(8,128)S(1)} %stack_reshape.15, f32[1,8,512]{2,1,0:T(8,128)S(1)} %stack_reshape.14, f32[1,8,512]{2,1,0:T(8,128)S(1)} %stack_reshape.13, f32[1,8,512]{2,1,0:T(8,128)S(1)} %stack_reshape.12, f32[4,72,512]{2,1,0:T(8,128)S(1)} %broadcast_select_fusion), kind=kLoop, calls=%fused_computation.4 | loop fusion | flops 655360 | bytes 1310720 | tf_op jit(solution)/shard_map/concatenate | solution.py:175
  16.5 3.7 %all-to-all-start = ((f32[4,80,512]{2,1,0:T(8,128)}), f32[4,80,512]{2,1,0:T(8,128)S(1)}, u32[]{:S(2)}, u32[]{:S(2)}) async-start(f32[4,80,512]{2,1,0:T(8,128)} %maximum_maximum_fusion), calls=%async_computation | async-start | bytes 1310720 | tf_op jit(solution)/shard_map/all_to_all | solution.py:182
  20.2 0.1 select_reduce_fusion
  20.3 0.1 convert_element_type.51
  20.5 0.1 copy.37
  20.6 0.9 %slice.194.cond_ref = f32[20,64,128]{2,1,0:T(8,128)} slice(f32[24,64,128]{2,1,0:T(8,128)S(1)} %bitcast.62), slice={[0:20], [0:64], [0:128]} | slice | bytes 1310720 | tf_op jit(solution)/shard_map/reshape | solution.py:234
  21.5 0.1 copy.38
  21.7 0.9 %slice.195.moist_ref = f32[20,64,128]{2,1,0:T(8,128)} slice(f32[24,64,128]{2,1,0:T(8,128)S(1)} %bitcast.63), slice={[0:20], [0:64], [0:128]} | slice | bytes 1310720 | tf_op jit(solution)/shard_map/reshape | solution.py:234
  22.5 3.1 %shard_map.111 = (f32[20,64,128]{2,1,0:T(8,128)}, f32[20,64,128]{2,1,0:T(8,128)}, f32[64,128]{1,0:T(8,128)}, f32[64,128]{1,0:T(8,128)}) custom-call(f32[20,64,128]{2,1,0:T(8,128)} %slice.194.cond_ref, f32[20,64,128]{2,1,0:T(8,128)} %slice.195.moist_ref), custom_call_target="tpu_custom_call" | custom-call | tf_op jit(solution)/shard_map/pallas_call | solution.py:128
  25.7 2.1 %all-to-all-done = f32[4,80,512]{2,1,0:T(8,128)S(1)} async-done(((f32[4,80,512]{2,1,0:T(8,128)}), f32[4,80,512]{2,1,0:T(8,128)S(1)}, u32[]{:S(2)}, u32[]{:S(2)}) %all-to-all-start) | async-done | bytes 655392 | tf_op jit(solution)/shard_map/all_to_all | solution.py:182
  27.8 0.1 reshape.153
  27.9 0.1 reshape.150
  28.0 0.1 reshape.146
  28.2 5.8 %collective-permute-start.3 = (f32[104,512]{1,0:T(8,128)S(1)}, f32[104,512]{1,0:T(8,128)S(1)}, u32[]{:S(2)}, u32[]{:S(2)}) collective-permute-start(f32[104,512]{1,0:T(8,128)S(1)} %pad_maximum_fusion.2), channel_id=1, source_target_pairs={{0,4},{4,8},{8,12},{12,16},{16,20},{20,24},{24,28},{28,32},{32,36}... | collective-permute-start | bytes 638984 | tf_op jit(solution)/shard_map/ppermute | solution.py:195
  34.0 7.2 %collective-permute-start.2 = (f32[104,512]{1,0:T(8,128)S(1)}, f32[104,512]{1,0:T(8,128)S(1)}, u32[]{:S(2)}, u32[]{:S(2)}) collective-permute-start(f32[104,512]{1,0:T(8,128)S(1)} %pad_maximum_fusion.1), channel_id=1, source_target_pairs={{0,252},{4,0},{8,4},{12,8},{16,12},{20,16},{24,20},{28,24},{32,28}... | collective-permute-start | bytes 638984 | tf_op jit(solution)/shard_map/ppermute | solution.py:193
  41.3 0.8 %collective-permute-done.3 = f32[104,512]{1,0:T(8,128)S(1)} collective-permute-done((f32[104,512]{1,0:T(8,128)S(1)}, f32[104,512]{1,0:T(8,128)S(1)}, u32[]{:S(2)}, u32[]{:S(2)}) %collective-permute-start.3) | collective-permute-done | bytes 213024 | tf_op jit(solution)/shard_map/ppermute | solution.py:195
  42.2 0.2 collective-permute-done.2
  42.5 0.1 reshape.152
  42.6 0.6 convolution_bitcast_fusion
  43.4 0.7 copy.36
  44.2 1.1 %fusion.24 = f32[128,128]{1,0:T(8,128)S(1)} fusion(f32[64,128]{1,0:T(8,128)} %get-tuple-element.10, f32[64,128]{1,0:T(8,128)S(1)} %fusion.6, f32[64,128]{1,0:T(8,128)} %get-tuple-element.11, f32[8192]{0:T(1024)S(1)} %bitcast.76, s32[8192]{0:T(1024)S(1)} %copy-done.4, f32[8192]{0:T(1024)S(1)} %bitcast.74, s32[64]{0:T(128)S(1)} %get-tuple-element.40), kind=kOutput, calls=%fused_computation.49 | convolution fusion | flops 12713984 | bytes 262400 | tf_op jit(solution)/shard_map/dot_general | solution.py:252
  45.3 0.7 all_to_all.12
  46.0 14.4 %all-to-all-start.1 = ((f32[64,1,384]{2,1,0:T(1,128)}), f32[64,1,384]{2,1,0:T(1,128)S(1)}, u32[]{:S(2)}, u32[]{:S(2)}) async-start(f32[64,1,384]{2,1,0:T(1,128)} %all_to_all.12), calls=%async_computation.1 | async-start | bytes 196608 | tf_op jit(solution)/shard_map/all_to_all | solution.py:261
  60.4 0.1 multiply_add_fusion
  60.6 1.3 %copy.43 = f32[3,8,64,128]{3,1,2,0:T(8,128)} copy(f32[3,8,64,128]{3,2,1,0:T(8,128)S(1)} %bitcast.61) | data formatting | bytes 1572864
  62.0 8.7 %all-to-all-done.1 = f32[64,1,384]{2,1,0:T(1,128)S(1)} async-done(((f32[64,1,384]{2,1,0:T(1,128)}), f32[64,1,384]{2,1,0:T(1,128)S(1)}, u32[]{:S(2)}, u32[]{:S(2)}) %all-to-all-start.1) | async-done | bytes 98336 | tf_op jit(solution)/shard_map/all_to_all | solution.py:261
  70.6 0.1 copy.34
  70.8 0.6 fusion.43
  71.3 0.7 copy.35
  (69 shorter events, 1.3 us)
Async XLA Ops:
  1.4 7.1 %collective-permute-start = (f32[6,1,128]{2,0,1:T(8,128)S(1)}, f32[6,1,128]{2,0,1:T(8,128)S(1)}, u32[]{:S(2)}, u32[]{:S(2)}) collective-permute-start(f32[6,1,128]{2,0,1:T(8,128)S(1)} %get-tuple-element.23), channel_id=1, source_target_pairs={{1,0},{2,1},{3,2},{4,3},{5,4},{6,5},{7,6},{8,7},{9,8},{10,9},{11,1... | collective-permute-start | bytes 9224 | tf_op jit(solution)/shard_map/ppermute | solution.py:28
  5.3 4.2 %collective-permute-start.1 = (f32[6,1,128]{2,0,1:T(8,128)S(1)}, f32[6,1,128]{2,0,1:T(8,128)S(1)}, u32[]{:S(2)}, u32[]{:S(2)}) collective-permute-start(f32[6,1,128]{2,0,1:T(8,128)S(1)} %get-tuple-element.24), channel_id=1, source_target_pairs={{0,1},{1,2},{2,3},{3,4},{4,5},{5,6},{6,7},{7,8},{8,9},{9,10},{10,1... | collective-permute-start | bytes 9224 | tf_op jit(solution)/shard_map/ppermute | solution.py:27
  10.3 10.2 %copy-start = (f32[20,8192]{1,0:T(8,128)S(1)}, f32[20,8192]{1,0:T(8,128)}, u32[]{:S(2)}) copy-start(f32[20,8192]{1,0:T(8,128)} %param.13) | copy-start | bytes 1966084
  14.7 6.8 %copy-start.1 = (f32[20,8192]{1,0:T(8,128)S(1)}, f32[20,8192]{1,0:T(8,128)}, u32[]{:S(2)}) copy-start(f32[20,8192]{1,0:T(8,128)} %param.14) | copy-start | bytes 1966084
  16.5 27.7 %copy-start.4 = (s32[8192]{0:T(1024)S(1)}, s32[8192]{0:T(1024)}, u32[]{:S(2)}) copy-start(s32[8192]{0:T(1024)} %param.12) | copy-start | bytes 98308
  16.5 11.3 %all-to-all-start = ((f32[4,80,512]{2,1,0:T(8,128)}), f32[4,80,512]{2,1,0:T(8,128)S(1)}, u32[]{:S(2)}, u32[]{:S(2)}) async-start(f32[4,80,512]{2,1,0:T(8,128)} %maximum_maximum_fusion), calls=%async_computation | async-start | bytes 1310720 | tf_op jit(solution)/shard_map/all_to_all | solution.py:182
  25.6 34.8 %copy-start.2 = (f32[20,64,128]{2,1,0:T(8,128)S(1)}, f32[20,64,128]{2,1,0:T(8,128)}, u32[]{:S(2)}) copy-start(f32[20,64,128]{2,1,0:T(8,128)} %get-tuple-element.8) | copy-start | bytes 1966084
  25.7 34.8 %copy-start.3 = (f32[20,64,128]{2,1,0:T(8,128)S(1)}, f32[20,64,128]{2,1,0:T(8,128)}, u32[]{:S(2)}) copy-start(f32[20,64,128]{2,1,0:T(8,128)} %get-tuple-element.9) | copy-start | bytes 1966084
  28.2 13.9 %collective-permute-start.3 = (f32[104,512]{1,0:T(8,128)S(1)}, f32[104,512]{1,0:T(8,128)S(1)}, u32[]{:S(2)}, u32[]{:S(2)}) collective-permute-start(f32[104,512]{1,0:T(8,128)S(1)} %pad_maximum_fusion.2), channel_id=1, source_target_pairs={{0,4},{4,8},{8,12},{12,16},{16,20},{20,24},{24,28},{28,32},{32,36}... | collective-permute-start | bytes 638984 | tf_op jit(solution)/shard_map/ppermute | solution.py:195
  34.0 8.3 %collective-permute-start.2 = (f32[104,512]{1,0:T(8,128)S(1)}, f32[104,512]{1,0:T(8,128)S(1)}, u32[]{:S(2)}, u32[]{:S(2)}) collective-permute-start(f32[104,512]{1,0:T(8,128)S(1)} %pad_maximum_fusion.1), channel_id=1, source_target_pairs={{0,252},{4,0},{8,4},{12,8},{16,12},{20,16},{24,20},{28,24},{32,28}... | collective-permute-start | bytes 638984 | tf_op jit(solution)/shard_map/ppermute | solution.py:193
  46.0 24.6 %all-to-all-start.1 = ((f32[64,1,384]{2,1,0:T(1,128)}), f32[64,1,384]{2,1,0:T(1,128)S(1)}, u32[]{:S(2)}, u32[]{:S(2)}) async-start(f32[64,1,384]{2,1,0:T(1,128)} %all_to_all.12), calls=%async_computation.1 | async-start | bytes 196608 | tf_op jit(solution)/shard_map/all_to_all | solution.py:261

commit v12 on v11

--- a/solution.py
+++ b/solution.py
@@ -216,9 +216,14 @@
     pair_atm = small[:pair_count]
     pair_land = small[pair_count : 2 * pair_count]
     river_owner = small[2 * pair_count : 2 * pair_count + owners]
+    devices = tile_count * sub_count
+    up = [(i, (i + 1) % devices) for i in range(devices)]
+    down = [(j, i) for i, j in up]
+    before = lax.ppermute(atm_fields[:, row_count - 1 :, :], ("tile", "sub"), up)
     local_rows = lax.optimization_barrier(jnp.pad(atm_fields, ((0, 0), (0, 0), (0, row_width))))
     atm_fields = local_rows[:, :, :row_width]
-    extended = padded(atm_fields, ((("tile", "sub"), 1),), 1)
+    after = lax.ppermute(atm_fields[:, :1, :], ("tile", "sub"), down)
+    extended = jnp.concatenate([before, atm_fields, after], axis=1)
     grad_x = x_gradient(atm_fields)
     grad_y = (extended[:, 2:, :] - extended[:, :-2, :]) * 0.5
     stacked = jnp.concatenate([atm_fields, grad_x, grad_y], axis=2).astype(jnp.bfloat16)

time: 72.5 us -> 67.4 us (0.930)
  starting transfers between devices: 35 us -> 28.6 us
  waiting for transfers between devices: 12.9 us -> 14.2 us
    ppermute x1, starting transfers between devices: 7.24 us -> 1.83 us  [route_partials(): lax.ppermute(messages[0], 'tile', [(i, (i - 1) % tile_count) for i in dev...]
    all_to_all x1, starting transfers between devices: 14.4 us -> 12 us  [on_device(): lax.all_to_all(packed, 'tile', split_axis=0, concat_axis=0, tiled=True)]
    ppermute x1, waiting for transfers between devices: 0.23 us -> 2.56 us  [route_partials(): lax.ppermute(messages[0], 'tile', [(i, (i - 1) % tile_count) for i in dev...]
    all_to_all x1, starting transfers between devices: 3.66 us -> 4.86 us  [route_partials(): lax.all_to_all(chunks, 'sub', split_axis=0, concat_axis=0, tiled=True)]
    ppermute x2, waiting for transfers between devices: 1.05 us -> 0.01 us  [the longest x1 0.01 us: on_device(): after = lax.ppermute(atm_fields[:, :1, :], ('tile', 'sub'), down)]
  transfers between devices with their start and end apart: 6 -> 6, of which waited for: 5 -> 4; matrix products, arithmetic and copies ran while one was open for 10% -> 10% of each run, Pallas kernels for 4% -> 5%
where the time goes in v12:
time: 67.4 us; the launch traced here: 67 us
  starting transfers between devices  28.6 us (42%)
  waiting for transfers between devices  14.2 us (21%)
  local copies, waits for them, and re-layouts  9.87 us (15%)
  matrix products  6.16 us (9%)
  other arithmetic  3.92 us (6%)
  Pallas kernels  3.14 us (5%)
  between operations  1.09 us (2%)
    all_to_all x1, starting transfers between devices, on_device(): lax.all_to_all(packed, 'tile', split_axis=0, concat_axis=0, tiled=True)  12 us
    all_to_all x1, waiting for transfers between devices, on_device(): lax.all_to_all(packed, 'tile', split_axis=0, concat_axis=0, tiled=True)  8.66 us
    ppermute x1, starting transfers between devices, route_partials(): lax.ppermute(messages[2], 'tile', [(i, (i + 1) % tile_count) for i in dev...  5.8 us
    all_to_all x1, starting transfers between devices, route_partials(): lax.all_to_all(chunks, 'sub', split_axis=0, concat_axis=0, tiled=True)  4.86 us
    dot_general x1, matrix products, on_device(): jnp.einsum('fpk,pkl->pfl', picked, weights, preferred_element_type=jnp.fl...  4.42 us
    unnamed x21, local copies, waits for them, and re-layouts  3.92 us
    pallas_call x1, Pallas kernels, soil_response(): pl.pallas_call(response_kernel, grid=(grid,), in_specs=[stack, stack], ou...  3.14 us
    ppermute x1, waiting for transfers between devices, route_partials(): lax.ppermute(messages[0], 'tile', [(i, (i - 1) % tile_count) for i in dev...  2.56 us
  transfers between devices with their start and end apart: 6, of which 4 were waited for; matrix products, arithmetic and copies ran while one was open for 10% of the time, Pallas kernels for 5%

profile of v12, /device:TPU:1, one launch (start us, length us, event | category | flops | bytes accessed | tf_op | source)
XLA Modules:
  0.0 67.0 jit_solution(7909634851066673327)
XLA Ops:
  0.6 0.7 %copy.35 = f32[6,8,128]{2,0,1:T(8,128)S(1)} copy(f32[6,8,128]{2,1,0:T(8,128)} %param.8) | data formatting | bytes 49152 | tf_op args[0]
  1.4 2.1 %collective-permute-start.1 = (f32[6,1,128]{2,0,1:T(8,128)S(1)}, f32[6,1,128]{2,0,1:T(8,128)S(1)}, u32[]{:S(2)}, u32[]{:S(2)}) collective-permute-start(f32[6,1,128]{2,0,1:T(8,128)S(1)} %slice.177), channel_id=1, source_target_pairs={{0,1},{1,2},{2,3},{3,4},{4,5},{5,6},{6,7},{7,8},{8,9},{9,10},{10,1... | collective-permute-start | bytes 9224 | tf_op jit(solution)/shard_map/ppermute | solution.py:222
  3.5 1.9 %collective-permute-start = (f32[6,1,128]{2,0,1:T(8,128)S(1)}, f32[6,1,128]{2,0,1:T(8,128)S(1)}, u32[]{:S(2)}, u32[]{:S(2)}) collective-permute-start(f32[6,1,128]{2,0,1:T(8,128)S(1)} %slice.176), channel_id=1, source_target_pairs={{1,0},{2,1},{3,2},{4,3},{5,4},{6,5},{7,6},{8,7},{9,8},{10,9},{11,1... | collective-permute-start | bytes 9224 | tf_op jit(solution)/shard_map/ppermute | solution.py:225
  5.5 0.8 %pad_add_fusion = s32[104]{0:T(128)S(1)} fusion(s32[64]{0:T(128)} %param.15, s32[20]{0:T(128)} %param.10, s32[20]{0:T(128)} %param.9), kind=kLoop, calls=%fused_computation.103 | loop fusion | flops 208 | bytes 832 | tf_op jit(solution)/shard_map/concatenate | solution.py:215
  6.3 0.1 compare_select_fusion.3
  6.5 0.2 select_reduce_fusion.3
  6.7 0.1 select_reduce_fusion.2
  6.9 0.1 fusion.19
  7.0 0.8 %gather_fusion.2 = s32[48]{0:T(128)S(1)} fusion(s32[20]{0:T(128)S(1)} %get-tuple-element.30, s32[1024]{0:T(1024)S(1)} %pad_clamp_fusion), kind=kCustom, calls=%fused_computation.2 | custom fusion | bytes 576 | tf_op jit(solution)/shard_map/gather | solution.py:172
  8.0 0.1 reduce_window_sum.23
  8.1 0.2 select_reduce_fusion.1
  8.3 0.1 ge.11
  8.4 0.1 broadcast_in_dim.65
  8.4 0.1 broadcast_in_dim.66
  8.7 0.1 concatenate.35
  8.8 0.6 gather_fusion
  9.4 4.4 %fusion.1 = f32[20,6,512]{2,1,0:T(8,128)S(1)} fusion(bf16[20,384,512]{2,1,0:T(8,128)(2,1)} %bitcast.60, bf16[20,6,384]{2,1,0:T(8,128)(2,1)S(1)} %gather_fusion), kind=kOutput, calls=%fused_computation.11 | convolution fusion | flops 47185920 | bytes 8202240 | tf_op jit(solution)/shard_map/fpk,pkl->pfl/dot_general | solution.py:232
  13.8 0.6 gather_fusion.1
  14.4 0.1 gather.13
  14.5 0.1 broadcast_select_fusion
  14.6 0.9 %maximum_maximum_fusion = f32[4,80,512]{2,1,0:T(8,128)} fusion(f32[1,8,512]{2,1,0:T(8,128)S(1)} %stack_reshape.15, f32[1,8,512]{2,1,0:T(8,128)S(1)} %stack_reshape.14, f32[1,8,512]{2,1,0:T(8,128)S(1)} %stack_reshape.13, f32[1,8,512]{2,1,0:T(8,128)S(1)} %stack_reshape.12, f32[4,72,512]{2,1,0:T(8,128)S(1)} %broadcast_select_fusion), kind=kLoop, calls=%fused_computation.4 | loop fusion | flops 655360 | bytes 1310720 | tf_op jit(solution)/shard_map/concatenate | solution.py:175
  15.5 4.9 %all-to-all-start = ((f32[4,80,512]{2,1,0:T(8,128)}), f32[4,80,512]{2,1,0:T(8,128)S(1)}, u32[]{:S(2)}, u32[]{:S(2)}) async-start(f32[4,80,512]{2,1,0:T(8,128)} %maximum_maximum_fusion), calls=%async_computation | async-start | bytes 1310720 | tf_op jit(solution)/shard_map/all_to_all | solution.py:182
  20.5 0.1 select_reduce_fusion
  20.6 0.1 convert_element_type.51
  20.7 0.1 copy.41
  20.9 0.9 %slice.193.cond_ref = f32[20,64,128]{2,1,0:T(8,128)} slice(f32[24,64,128]{2,1,0:T(8,128)S(1)} %bitcast.62), slice={[0:20], [0:64], [0:128]} | slice | bytes 1310720 | tf_op jit(solution)/shard_map/reshape | solution.py:239
  21.8 0.1 copy.42
  21.9 0.9 %slice.194.moist_ref = f32[20,64,128]{2,1,0:T(8,128)} slice(f32[24,64,128]{2,1,0:T(8,128)S(1)} %bitcast.63), slice={[0:20], [0:64], [0:128]} | slice | bytes 1310720 | tf_op jit(solution)/shard_map/reshape | solution.py:239
  22.8 3.1 %shard_map.111 = (f32[20,64,128]{2,1,0:T(8,128)}, f32[20,64,128]{2,1,0:T(8,128)}, f32[64,128]{1,0:T(8,128)}, f32[64,128]{1,0:T(8,128)}) custom-call(f32[20,64,128]{2,1,0:T(8,128)} %slice.193.cond_ref, f32[20,64,128]{2,1,0:T(8,128)} %slice.194.moist_ref), custom_call_target="tpu_custom_call" | custom-call | tf_op jit(solution)/shard_map/pallas_call | solution.py:128
  26.0 2.1 %all-to-all-done = f32[4,80,512]{2,1,0:T(8,128)S(1)} async-done(((f32[4,80,512]{2,1,0:T(8,128)}), f32[4,80,512]{2,1,0:T(8,128)S(1)}, u32[]{:S(2)}, u32[]{:S(2)}) %all-to-all-start) | async-done | bytes 655392 | tf_op jit(solution)/shard_map/all_to_all | solution.py:182
  28.1 0.1 reshape.153
  28.2 0.1 reshape.150
  28.3 0.1 reshape.146
  28.5 5.8 %collective-permute-start.3 = (f32[104,512]{1,0:T(8,128)S(1)}, f32[104,512]{1,0:T(8,128)S(1)}, u32[]{:S(2)}, u32[]{:S(2)}) collective-permute-start(f32[104,512]{1,0:T(8,128)S(1)} %pad_maximum_fusion.2), channel_id=1, source_target_pairs={{0,4},{4,8},{8,12},{12,16},{16,20},{20,24},{24,28},{28,32},{32,36}... | collective-permute-start | bytes 638984 | tf_op jit(solution)/shard_map/ppermute | solution.py:195
  34.3 1.8 %collective-permute-start.2 = (f32[104,512]{1,0:T(8,128)S(1)}, f32[104,512]{1,0:T(8,128)S(1)}, u32[]{:S(2)}, u32[]{:S(2)}) collective-permute-start(f32[104,512]{1,0:T(8,128)S(1)} %pad_maximum_fusion.1), channel_id=1, source_target_pairs={{0,252},{4,0},{8,4},{12,8},{16,12},{20,16},{24,20},{28,24},{32,28}... | collective-permute-start | bytes 638984 | tf_op jit(solution)/shard_map/ppermute | solution.py:193
  36.1 0.9 %collective-permute-done.3 = f32[104,512]{1,0:T(8,128)S(1)} collective-permute-done((f32[104,512]{1,0:T(8,128)S(1)}, f32[104,512]{1,0:T(8,128)S(1)}, u32[]{:S(2)}, u32[]{:S(2)}) %collective-permute-start.3) | collective-permute-done | bytes 213024 | tf_op jit(solution)/shard_map/ppermute | solution.py:195
  37.1 2.6 %collective-permute-done.2 = f32[104,512]{1,0:T(8,128)S(1)} collective-permute-done((f32[104,512]{1,0:T(8,128)S(1)}, f32[104,512]{1,0:T(8,128)S(1)}, u32[]{:S(2)}, u32[]{:S(2)}) %collective-permute-start.2) | collective-permute-done | bytes 213024 | tf_op jit(solution)/shard_map/ppermute | solution.py:193
  39.9 0.6 convolution_bitcast_fusion
  40.7 0.7 %copy.40 = bf16[1,6,16,512]{3,1,2,0:T(8,128)(2,1)} copy(bf16[1,6,16,512]{3,2,1,0:T(8,128)(2,1)S(1)} %convert_bitcast_fusion) | data formatting | bytes 196608
  41.5 1.1 %fusion.24 = f32[128,128]{1,0:T(8,128)S(1)} fusion(f32[64,128]{1,0:T(8,128)} %get-tuple-element.10, f32[64,128]{1,0:T(8,128)S(1)} %fusion.6, f32[64,128]{1,0:T(8,128)} %get-tuple-element.11, f32[8192]{0:T(1024)S(1)} %bitcast.76, s32[8192]{0:T(1024)S(1)} %copy-done.4, f32[8192]{0:T(1024)S(1)} %bitcast.74, s32[64]{0:T(128)S(1)} %get-tuple-element.38), kind=kOutput, calls=%fused_computation.49 | convolution fusion | flops 12713984 | bytes 262400 | tf_op jit(solution)/shard_map/dot_general | solution.py:257
  42.6 0.7 %all_to_all.12 = f32[64,1,384]{2,1,0:T(1,128)} reshape(f32[64,384]{1,0:T(8,128)S(1)} %select_maximum_fusion) | data formatting | bytes 196608 | tf_op jit(solution)/shard_map/all_to_all | solution.py:266
  43.3 12.0 %all-to-all-start.1 = ((f32[64,1,384]{2,1,0:T(1,128)}), f32[64,1,384]{2,1,0:T(1,128)S(1)}, u32[]{:S(2)}, u32[]{:S(2)}) async-start(f32[64,1,384]{2,1,0:T(1,128)} %all_to_all.12), calls=%async_computation.1 | async-start | bytes 196608 | tf_op jit(solution)/shard_map/all_to_all | solution.py:266
  55.4 0.1 multiply_add_fusion
  55.6 1.3 %copy.47 = f32[3,8,64,128]{3,1,2,0:T(8,128)} copy(f32[3,8,64,128]{3,2,1,0:T(8,128)S(1)} %bitcast.61) | data formatting | bytes 1572864
  56.9 8.7 %all-to-all-done.1 = f32[64,1,384]{2,1,0:T(1,128)S(1)} async-done(((f32[64,1,384]{2,1,0:T(1,128)}), f32[64,1,384]{2,1,0:T(1,128)S(1)}, u32[]{:S(2)}, u32[]{:S(2)}) %all-to-all-start.1) | async-done | bytes 98336 | tf_op jit(solution)/shard_map/all_to_all | solution.py:266
  65.6 0.1 copy.38
  65.7 0.6 fusion.43
  66.3 0.7 %copy.39 = f32[1,1,64,2,128]{4,3,2,1,0:T(2,128)} copy(f32[1,1,64,2,128]{2,4,3,1,0:T(8,128)S(1)} %bitcast.72) | data formatting | bytes 131072
  (70 shorter events, 1.3 us)
Async XLA Ops:
  1.4 7.3 %collective-permute-start.1 = (f32[6,1,128]{2,0,1:T(8,128)S(1)}, f32[6,1,128]{2,0,1:T(8,128)S(1)}, u32[]{:S(2)}, u32[]{:S(2)}) collective-permute-start(f32[6,1,128]{2,0,1:T(8,128)S(1)} %slice.177), channel_id=1, source_target_pairs={{0,1},{1,2},{2,3},{3,4},{4,5},{5,6},{6,7},{7,8},{8,9},{9,10},{10,1... | collective-permute-start | bytes 9224 | tf_op jit(solution)/shard_map/ppermute | solution.py:222
  3.5 5.1 %collective-permute-start = (f32[6,1,128]{2,0,1:T(8,128)S(1)}, f32[6,1,128]{2,0,1:T(8,128)S(1)}, u32[]{:S(2)}, u32[]{:S(2)}) collective-permute-start(f32[6,1,128]{2,0,1:T(8,128)S(1)} %slice.176), channel_id=1, source_target_pairs={{1,0},{2,1},{3,2},{4,3},{5,4},{6,5},{7,6},{8,7},{9,8},{10,9},{11,1... | collective-permute-start | bytes 9224 | tf_op jit(solution)/shard_map/ppermute | solution.py:225
  9.4 11.4 %copy-start = (f32[20,8192]{1,0:T(8,128)S(1)}, f32[20,8192]{1,0:T(8,128)}, u32[]{:S(2)}) copy-start(f32[20,8192]{1,0:T(8,128)} %param.13) | copy-start | bytes 1966084
  13.8 8.0 %copy-start.1 = (f32[20,8192]{1,0:T(8,128)S(1)}, f32[20,8192]{1,0:T(8,128)}, u32[]{:S(2)}) copy-start(f32[20,8192]{1,0:T(8,128)} %param.14) | copy-start | bytes 1966084
  15.5 25.9 %copy-start.4 = (s32[8192]{0:T(1024)S(1)}, s32[8192]{0:T(1024)}, u32[]{:S(2)}) copy-start(s32[8192]{0:T(1024)} %param.12) | copy-start | bytes 98308
  15.5 12.5 %all-to-all-start = ((f32[4,80,512]{2,1,0:T(8,128)}), f32[4,80,512]{2,1,0:T(8,128)S(1)}, u32[]{:S(2)}, u32[]{:S(2)}) async-start(f32[4,80,512]{2,1,0:T(8,128)} %maximum_maximum_fusion), calls=%async_computation | async-start | bytes 1310720 | tf_op jit(solution)/shard_map/all_to_all | solution.py:182
  25.9 29.4 %copy-start.2 = (f32[20,64,128]{2,1,0:T(8,128)S(1)}, f32[20,64,128]{2,1,0:T(8,128)}, u32[]{:S(2)}) copy-start(f32[20,64,128]{2,1,0:T(8,128)} %get-tuple-element.8) | copy-start | bytes 1966084
  25.9 29.4 %copy-start.3 = (f32[20,64,128]{2,1,0:T(8,128)S(1)}, f32[20,64,128]{2,1,0:T(8,128)}, u32[]{:S(2)}) copy-start(f32[20,64,128]{2,1,0:T(8,128)} %get-tuple-element.9) | copy-start | bytes 1966084
  28.5 8.6 %collective-permute-start.3 = (f32[104,512]{1,0:T(8,128)S(1)}, f32[104,512]{1,0:T(8,128)S(1)}, u32[]{:S(2)}, u32[]{:S(2)}) collective-permute-start(f32[104,512]{1,0:T(8,128)S(1)} %pad_maximum_fusion.2), channel_id=1, source_target_pairs={{0,4},{4,8},{8,12},{12,16},{16,20},{20,24},{24,28},{28,32},{32,36}... | collective-permute-start | bytes 638984 | tf_op jit(solution)/shard_map/ppermute | solution.py:195
  34.3 5.3 %collective-permute-start.2 = (f32[104,512]{1,0:T(8,128)S(1)}, f32[104,512]{1,0:T(8,128)S(1)}, u32[]{:S(2)}, u32[]{:S(2)}) collective-permute-start(f32[104,512]{1,0:T(8,128)S(1)} %pad_maximum_fusion.1), channel_id=1, source_target_pairs={{0,252},{4,0},{8,4},{12,8},{16,12},{20,16},{24,20},{28,24},{32,28}... | collective-permute-start | bytes 638984 | tf_op jit(solution)/shard_map/ppermute | solution.py:193
  43.3 22.2 %all-to-all-start.1 = ((f32[64,1,384]{2,1,0:T(1,128)}), f32[64,1,384]{2,1,0:T(1,128)S(1)}, u32[]{:S(2)}, u32[]{:S(2)}) async-start(f32[64,1,384]{2,1,0:T(1,128)} %all_to_all.12), calls=%async_computation.1 | async-start | bytes 196608 | tf_op jit(solution)/shard_map/all_to_all | solution.py:266

commit v13 on v12

--- a/solution.py
+++ b/solution.py
@@ -226,10 +226,19 @@
     extended = jnp.concatenate([before, atm_fields, after], axis=1)
     grad_x = x_gradient(atm_fields)
     grad_y = (extended[:, 2:, :] - extended[:, :-2, :]) * 0.5
-    stacked = jnp.concatenate([atm_fields, grad_x, grad_y], axis=2).astype(jnp.bfloat16)
-    picked = stacked[:, pair_atm, :]
+    plain = jnp.concatenate([atm_fields, grad_x], axis=2).astype(jnp.bfloat16)
     weights = pair_weight.reshape(pair_count, 3 * row_width, LBLK)
-    partial_value = jnp.einsum("fpk,pkl->pfl", picked, weights, preferred_element_type=jnp.float32)
+    partial_value = jnp.einsum(
+        "fpk,pkl->pfl",
+        plain[:, pair_atm, :],
+        weights[:, : 2 * row_width, :],
+        preferred_element_type=jnp.float32,
+    ) + jnp.einsum(
+        "fpk,pkl->pfl",
+        grad_y.astype(jnp.bfloat16)[:, pair_atm, :],
+        weights[:, 2 * row_width :, :],
+        preferred_element_type=jnp.float32,
+    )
     owned_sums = route_partials(partial_value, pair_land, tile_count, sub_count, tile_index)
     forcing = owned_sums.reshape(field_count, LB_DEV * LBLK)
     land_forcing = forcing.astype(jnp.bfloat16)

time: 67.4 us -> 69 us (1.024)
  waiting for transfers between devices: 14.2 us -> 12.9 us
  starting transfers between devices: 28.6 us -> 29.8 us
  matrix products: 6.16 us -> 7.27 us
    ppermute x1, starting transfers between devices: 1.83 us -> 3.1 us  [route_partials(): lax.ppermute(messages[0], 'tile', [(i, (i - 1) % tile_count) for i in dev...]
    all_to_all x1, starting transfers between devices: 4.86 us -> 3.61 us  [route_partials(): lax.all_to_all(chunks, 'sub', split_axis=0, concat_axis=0, tiled=True)]
    all_to_all x1, starting transfers between devices: 12 us -> 13.2 us  [on_device(): lax.all_to_all(packed, 'tile', split_axis=0, concat_axis=0, tiled=True)]
    ppermute x1, waiting for transfers between devices: 2.56 us -> 1.39 us  [route_partials(): lax.ppermute(messages[0], 'tile', [(i, (i - 1) % tile_count) for i in dev...]
    dot_general x1 -> x2, matrix products: 4.42 us -> 5.53 us  [the longest x1 3.34 us: on_device(): jnp.einsum('fpk,pkl->pfl', plain[:, pair_atm, :], weights[:, :2 * row_wid...]
  transfers between devices with their start and end apart: 6 -> 6, of which waited for: 4 -> 4; matrix products, arithmetic and copies ran while one was open for 10% -> 16% of each run, Pallas kernels for 5% -> 5%
where the time goes in v13:
time: 69 us; the launch traced here: 68.6 us
  starting transfers between devices  29.8 us (43%)
  waiting for transfers between devices  12.9 us (19%)
  local copies, waits for them, and re-layouts  10.3 us (15%)
  matrix products  7.27 us (11%)
  other arithmetic  4.01 us (6%)
  Pallas kernels  3.14 us (5%)
  between operations  1.11 us (2%)
    all_to_all x1, starting transfers between devices, on_device(): lax.all_to_all(packed, 'tile', split_axis=0, concat_axis=0, tiled=True)  13.2 us
    all_to_all x1, waiting for transfers between devices, on_device(): lax.all_to_all(packed, 'tile', split_axis=0, concat_axis=0, tiled=True)  8.66 us
    ppermute x1, starting transfers between devices, route_partials(): lax.ppermute(messages[2], 'tile', [(i, (i + 1) % tile_count) for i in dev...  5.8 us
    unnamed x21, local copies, waits for them, and re-layouts  3.92 us
    all_to_all x1, starting transfers between devices, route_partials(): lax.all_to_all(chunks, 'sub', split_axis=0, concat_axis=0, tiled=True)  3.61 us
    dot_general x1, matrix products, on_device(): jnp.einsum('fpk,pkl->pfl', plain[:, pair_atm, :], weights[:, :2 * row_wid...  3.34 us
    pallas_call x1, Pallas kernels, soil_response(): pl.pallas_call(response_kernel, grid=(grid,), in_specs=[stack, stack], ou...  3.14 us
    ppermute x1, starting transfers between devices, route_partials(): lax.ppermute(messages[0], 'tile', [(i, (i - 1) % tile_count) for i in dev...  3.1 us
  transfers between devices with their start and end apart: 6, of which 4 were waited for; matrix products, arithmetic and copies ran while one was open for 16% of the time, Pallas kernels for 5%

profile of v13, /device:TPU:1, one launch (start us, length us, event | category | flops | bytes accessed | tf_op | source)
XLA Modules:
  0.0 68.6 jit_solution(1016900659702038682)
XLA Ops:
  0.6 0.7 %copy.36 = f32[6,8,128]{2,0,1:T(8,128)S(1)} copy(f32[6,8,128]{2,1,0:T(8,128)} %param.8) | data formatting | bytes 49152 | tf_op args[0]
  1.4 2.1 %collective-permute-start.1 = (f32[6,1,128]{2,0,1:T(8,128)S(1)}, f32[6,1,128]{2,0,1:T(8,128)S(1)}, u32[]{:S(2)}, u32[]{:S(2)}) collective-permute-start(f32[6,1,128]{2,0,1:T(8,128)S(1)} %slice.188), channel_id=1, source_target_pairs={{0,1},{1,2},{2,3},{3,4},{4,5},{5,6},{6,7},{7,8},{8,9},{9,10},{10,1... | collective-permute-start | bytes 9224 | tf_op jit(solution)/shard_map/ppermute | solution.py:222
  3.5 1.9 %collective-permute-start = (f32[6,1,128]{2,0,1:T(8,128)S(1)}, f32[6,1,128]{2,0,1:T(8,128)S(1)}, u32[]{:S(2)}, u32[]{:S(2)}) collective-permute-start(f32[6,1,128]{2,0,1:T(8,128)S(1)} %slice.187), channel_id=1, source_target_pairs={{1,0},{2,1},{3,2},{4,3},{5,4},{6,5},{7,6},{8,7},{9,8},{10,9},{11,1... | collective-permute-start | bytes 9224 | tf_op jit(solution)/shard_map/ppermute | solution.py:225
  5.5 0.8 %pad_add_fusion = s32[104]{0:T(128)S(1)} fusion(s32[64]{0:T(128)} %param.15, s32[20]{0:T(128)} %param.10, s32[20]{0:T(128)} %param.9), kind=kLoop, calls=%fused_computation.110 | loop fusion | flops 208 | bytes 832 | tf_op jit(solution)/shard_map/concatenate | solution.py:215
  6.3 0.1 compare_select_fusion.3
  6.5 0.2 select_reduce_fusion.3
  6.7 0.1 select_reduce_fusion.2
  6.9 0.1 fusion.29
  7.0 0.8 %gather_fusion.3 = s32[48]{0:T(128)S(1)} fusion(s32[20]{0:T(128)S(1)} %get-tuple-element.30, s32[1024]{0:T(1024)S(1)} %pad_clamp_fusion), kind=kCustom, calls=%fused_computation.3 | custom fusion | bytes 576 | tf_op jit(solution)/shard_map/gather | solution.py:172
  8.0 0.1 reduce_window_sum.23
  8.1 0.1 pad_maximum_fusion.5
  8.2 0.6 gather_fusion
  8.7 3.3 %fusion = f32[20,6,512]{2,1,0:T(8,128)S(1)} fusion(bf16[20,384,512]{2,1,0:T(8,128)(2,1)} %bitcast.62, bf16[20,6,256]{2,1,0:T(8,128)(2,1)S(1)} %gather_fusion), kind=kOutput, calls=%fused_computation.4 | convolution fusion | flops 31457280 | bytes 5550080 | tf_op jit(solution)/shard_map/fpk,pkl->pfl/dot_general | solution.py:231
  12.1 0.2 select_reduce_fusion.1
  12.3 0.1 ge.11
  12.5 0.1 broadcast_in_dim.67
  12.7 0.6 gather_fusion.1
  13.3 2.2 %fusion.4 = f32[20,6,512]{2,1,0:T(8,128)S(1)} fusion(f32[20,6,512]{2,1,0:T(8,128)S(1)} %fusion, bf16[20,384,512]{2,1,0:T(8,128)(2,1)} %bitcast.63, bf16[20,6,128]{2,1,0:T(8,128)(2,1)S(1)} %gather_fusion.1), kind=kOutput, calls=%fused_computation.8 | convolution fusion | flops 15790080 | bytes 3143680 | tf_op jit(solution)/shard_map/fpk,pkl->pfl/dot_general | solution.py:236
  15.5 0.6 gather_fusion.2
  16.1 0.1 gather.17
  16.2 0.1 broadcast_select_fusion
  16.3 0.9 %maximum_maximum_fusion = f32[4,80,512]{2,1,0:T(8,128)} fusion(f32[1,8,512]{2,1,0:T(8,128)S(1)} %stack_reshape.15, f32[1,8,512]{2,1,0:T(8,128)S(1)} %stack_reshape.14, f32[1,8,512]{2,1,0:T(8,128)S(1)} %stack_reshape.13, f32[1,8,512]{2,1,0:T(8,128)S(1)} %stack_reshape.12, f32[4,72,512]{2,1,0:T(8,128)S(1)} %broadcast_select_fusion), kind=kLoop, calls=%fused_computation.10 | loop fusion | flops 655360 | bytes 1310720 | tf_op jit(solution)/shard_map/concatenate | solution.py:175
  17.2 3.6 %all-to-all-start = ((f32[4,80,512]{2,1,0:T(8,128)}), f32[4,80,512]{2,1,0:T(8,128)S(1)}, u32[]{:S(2)}, u32[]{:S(2)}) async-start(f32[4,80,512]{2,1,0:T(8,128)} %maximum_maximum_fusion), calls=%async_computation | async-start | bytes 1310720 | tf_op jit(solution)/shard_map/all_to_all | solution.py:182
  20.9 0.1 select_reduce_fusion
  21.0 0.1 convert_element_type.55
  21.2 0.1 copy.42
  21.3 0.9 %slice.205.cond_ref = f32[20,64,128]{2,1,0:T(8,128)} slice(f32[24,64,128]{2,1,0:T(8,128)S(1)} %bitcast.65), slice={[0:20], [0:64], [0:128]} | slice | bytes 1310720 | tf_op jit(solution)/shard_map/reshape | solution.py:248
  22.2 0.1 copy.43
  22.4 0.9 %slice.206.moist_ref = f32[20,64,128]{2,1,0:T(8,128)} slice(f32[24,64,128]{2,1,0:T(8,128)S(1)} %bitcast.66), slice={[0:20], [0:64], [0:128]} | slice | bytes 1310720 | tf_op jit(solution)/shard_map/reshape | solution.py:248
  23.2 3.1 %shard_map.111 = (f32[20,64,128]{2,1,0:T(8,128)}, f32[20,64,128]{2,1,0:T(8,128)}, f32[64,128]{1,0:T(8,128)}, f32[64,128]{1,0:T(8,128)}) custom-call(f32[20,64,128]{2,1,0:T(8,128)} %slice.205.cond_ref, f32[20,64,128]{2,1,0:T(8,128)} %slice.206.moist_ref), custom_call_target="tpu_custom_call" | custom-call | tf_op jit(solution)/shard_map/pallas_call | solution.py:128
  26.4 2.0 %all-to-all-done = f32[4,80,512]{2,1,0:T(8,128)S(1)} async-done(((f32[4,80,512]{2,1,0:T(8,128)}), f32[4,80,512]{2,1,0:T(8,128)S(1)}, u32[]{:S(2)}, u32[]{:S(2)}) %all-to-all-start) | async-done | bytes 655392 | tf_op jit(solution)/shard_map/all_to_all | solution.py:182
  28.5 0.1 reshape.153
  28.6 0.1 reshape.150
  28.7 0.1 reshape.146
  28.9 5.8 %collective-permute-start.3 = (f32[104,512]{1,0:T(8,128)S(1)}, f32[104,512]{1,0:T(8,128)S(1)}, u32[]{:S(2)}, u32[]{:S(2)}) collective-permute-start(f32[104,512]{1,0:T(8,128)S(1)} %pad_maximum_fusion.2), channel_id=1, source_target_pairs={{0,4},{4,8},{8,12},{12,16},{16,20},{20,24},{24,28},{28,32},{32,36}... | collective-permute-start | bytes 638984 | tf_op jit(solution)/shard_map/ppermute | solution.py:195
  34.7 3.1 %collective-permute-start.2 = (f32[104,512]{1,0:T(8,128)S(1)}, f32[104,512]{1,0:T(8,128)S(1)}, u32[]{:S(2)}, u32[]{:S(2)}) collective-permute-start(f32[104,512]{1,0:T(8,128)S(1)} %pad_maximum_fusion.1), channel_id=1, source_target_pairs={{0,252},{4,0},{8,4},{12,8},{16,12},{20,16},{24,20},{28,24},{32,28}... | collective-permute-start | bytes 638984 | tf_op jit(solution)/shard_map/ppermute | solution.py:193
  37.8 0.8 %collective-permute-done.3 = f32[104,512]{1,0:T(8,128)S(1)} collective-permute-done((f32[104,512]{1,0:T(8,128)S(1)}, f32[104,512]{1,0:T(8,128)S(1)}, u32[]{:S(2)}, u32[]{:S(2)}) %collective-permute-start.3) | collective-permute-done | bytes 213024 | tf_op jit(solution)/shard_map/ppermute | solution.py:195
  38.7 1.4 %collective-permute-done.2 = f32[104,512]{1,0:T(8,128)S(1)} collective-permute-done((f32[104,512]{1,0:T(8,128)S(1)}, f32[104,512]{1,0:T(8,128)S(1)}, u32[]{:S(2)}, u32[]{:S(2)}) %collective-permute-start.2) | collective-permute-done | bytes 213024 | tf_op jit(solution)/shard_map/ppermute | solution.py:193
  40.3 0.6 convolution_bitcast_fusion
  41.1 0.7 %copy.41 = bf16[1,6,16,512]{3,1,2,0:T(8,128)(2,1)} copy(bf16[1,6,16,512]{3,2,1,0:T(8,128)(2,1)S(1)} %convert_bitcast_fusion) | data formatting | bytes 196608
  41.9 1.1 %fusion.31 = f32[128,128]{1,0:T(8,128)S(1)} fusion(f32[64,128]{1,0:T(8,128)} %get-tuple-element.10, f32[64,128]{1,0:T(8,128)S(1)} %fusion.13, f32[64,128]{1,0:T(8,128)} %get-tuple-element.11, f32[8192]{0:T(1024)S(1)} %bitcast.79, s32[8192]{0:T(1024)S(1)} %copy-done.4, f32[8192]{0:T(1024)S(1)} %bitcast.77, s32[64]{0:T(128)S(1)} %get-tuple-element.38), kind=kOutput, calls=%fused_computation.56 | convolution fusion | flops 12713984 | bytes 262400 | tf_op jit(solution)/shard_map/dot_general | solution.py:266
  43.0 0.7 %all_to_all.12 = f32[64,1,384]{2,1,0:T(1,128)} reshape(f32[64,384]{1,0:T(8,128)S(1)} %select_maximum_fusion) | data formatting | bytes 196608 | tf_op jit(solution)/shard_map/all_to_all | solution.py:275
  43.7 13.2 %all-to-all-start.1 = ((f32[64,1,384]{2,1,0:T(1,128)}), f32[64,1,384]{2,1,0:T(1,128)S(1)}, u32[]{:S(2)}, u32[]{:S(2)}) async-start(f32[64,1,384]{2,1,0:T(1,128)} %all_to_all.12), calls=%async_computation.1 | async-start | bytes 196608 | tf_op jit(solution)/shard_map/all_to_all | solution.py:275
  57.1 1.3 %copy.48 = f32[3,8,64,128]{3,1,2,0:T(8,128)} copy(f32[3,8,64,128]{3,2,1,0:T(8,128)S(1)} %bitcast.64) | data formatting | bytes 1572864
  58.5 8.7 %all-to-all-done.1 = f32[64,1,384]{2,1,0:T(1,128)S(1)} async-done(((f32[64,1,384]{2,1,0:T(1,128)}), f32[64,1,384]{2,1,0:T(1,128)S(1)}, u32[]{:S(2)}, u32[]{:S(2)}) %all-to-all-start.1) | async-done | bytes 98336 | tf_op jit(solution)/shard_map/all_to_all | solution.py:275
  67.1 0.1 copy.39
  67.3 0.6 fusion.50
  67.9 0.7 %copy.40 = f32[1,1,64,2,128]{4,3,2,1,0:T(2,128)} copy(f32[1,1,64,2,128]{2,4,3,1,0:T(8,128)S(1)} %bitcast.75) | data formatting | bytes 131072
  (72 shorter events, 1.5 us)
Async XLA Ops:
  1.4 11.3 %collective-permute-start.1 = (f32[6,1,128]{2,0,1:T(8,128)S(1)}, f32[6,1,128]{2,0,1:T(8,128)S(1)}, u32[]{:S(2)}, u32[]{:S(2)}) collective-permute-start(f32[6,1,128]{2,0,1:T(8,128)S(1)} %slice.188), channel_id=1, source_target_pairs={{0,1},{1,2},{2,3},{3,4},{4,5},{5,6},{6,7},{7,8},{8,9},{9,10},{10,1... | collective-permute-start | bytes 9224 | tf_op jit(solution)/shard_map/ppermute | solution.py:222
  3.5 9.2 %collective-permute-start = (f32[6,1,128]{2,0,1:T(8,128)S(1)}, f32[6,1,128]{2,0,1:T(8,128)S(1)}, u32[]{:S(2)}, u32[]{:S(2)}) collective-permute-start(f32[6,1,128]{2,0,1:T(8,128)S(1)} %slice.187), channel_id=1, source_target_pairs={{1,0},{2,1},{3,2},{4,3},{5,4},{6,5},{7,6},{8,7},{9,8},{10,9},{11,1... | collective-permute-start | bytes 9224 | tf_op jit(solution)/shard_map/ppermute | solution.py:225
  8.7 12.4 %copy-start = (f32[20,8192]{1,0:T(8,128)S(1)}, f32[20,8192]{1,0:T(8,128)}, u32[]{:S(2)}) copy-start(f32[20,8192]{1,0:T(8,128)} %param.13) | copy-start | bytes 1966084
  12.1 10.1 %copy-start.1 = (f32[20,8192]{1,0:T(8,128)S(1)}, f32[20,8192]{1,0:T(8,128)}, u32[]{:S(2)}) copy-start(f32[20,8192]{1,0:T(8,128)} %param.14) | copy-start | bytes 1966084
  17.2 24.6 %copy-start.4 = (s32[8192]{0:T(1024)S(1)}, s32[8192]{0:T(1024)}, u32[]{:S(2)}) copy-start(s32[8192]{0:T(1024)} %param.12) | copy-start | bytes 98308
  17.2 11.2 %all-to-all-start = ((f32[4,80,512]{2,1,0:T(8,128)}), f32[4,80,512]{2,1,0:T(8,128)S(1)}, u32[]{:S(2)}, u32[]{:S(2)}) async-start(f32[4,80,512]{2,1,0:T(8,128)} %maximum_maximum_fusion), calls=%async_computation | async-start | bytes 1310720 | tf_op jit(solution)/shard_map/all_to_all | solution.py:182
  26.4 30.6 %copy-start.2 = (f32[20,64,128]{2,1,0:T(8,128)S(1)}, f32[20,64,128]{2,1,0:T(8,128)}, u32[]{:S(2)}) copy-start(f32[20,64,128]{2,1,0:T(8,128)} %get-tuple-element.8) | copy-start | bytes 1966084
  26.4 30.6 %copy-start.3 = (f32[20,64,128]{2,1,0:T(8,128)S(1)}, f32[20,64,128]{2,1,0:T(8,128)}, u32[]{:S(2)}) copy-start(f32[20,64,128]{2,1,0:T(8,128)} %get-tuple-element.9) | copy-start | bytes 1966084
  28.9 9.8 %collective-permute-start.3 = (f32[104,512]{1,0:T(8,128)S(1)}, f32[104,512]{1,0:T(8,128)S(1)}, u32[]{:S(2)}, u32[]{:S(2)}) collective-permute-start(f32[104,512]{1,0:T(8,128)S(1)} %pad_maximum_fusion.2), channel_id=1, source_target_pairs={{0,4},{4,8},{8,12},{12,16},{16,20},{20,24},{24,28},{28,32},{32,36}... | collective-permute-start | bytes 638984 | tf_op jit(solution)/shard_map/ppermute | solution.py:195
  34.7 5.3 %collective-permute-start.2 = (f32[104,512]{1,0:T(8,128)S(1)}, f32[104,512]{1,0:T(8,128)S(1)}, u32[]{:S(2)}, u32[]{:S(2)}) collective-permute-start(f32[104,512]{1,0:T(8,128)S(1)} %pad_maximum_fusion.1), channel_id=1, source_target_pairs={{0,252},{4,0},{8,4},{12,8},{16,12},{20,16},{24,20},{28,24},{32,28}... | collective-permute-start | bytes 638984 | tf_op jit(solution)/shard_map/ppermute | solution.py:193
  43.7 23.4 %all-to-all-start.1 = ((f32[64,1,384]{2,1,0:T(1,128)}), f32[64,1,384]{2,1,0:T(1,128)S(1)}, u32[]{:S(2)}, u32[]{:S(2)}) async-start(f32[64,1,384]{2,1,0:T(1,128)} %all_to_all.12), calls=%async_computation.1 | async-start | bytes 196608 | tf_op jit(solution)/shard_map/all_to_all | solution.py:275

commit v14 on v12

--- a/solution.py
+++ b/solution.py
@@ -168,7 +168,10 @@
     source = jnp.sum(jnp.where(placing, jnp.arange(pair_count, dtype=jnp.int32)[None, :] + 1, 0), axis=1) - 1
     filled = source >= 0
     picked = jnp.maximum(source, 0)
-    rows = jnp.where(filled[:, None, None], partial_value[picked], 0.0)
+    choose = (source[:, None] == jnp.arange(pair_count, dtype=jnp.int32)[None, :]).astype(jnp.float32)
+    rows = jnp.dot(
+        choose, partial_value.reshape(pair_count, field_count * width), precision=lax.Precision.HIGHEST
+    ).reshape(source.shape[0], field_count, width)
     ids = jnp.where(filled, pair_land[picked] % LB_DEV, -1).astype(jnp.float32)
     chunk_rows = 3 * CAP_P * field_count
     ids = ids.reshape(sub_count, 3 * CAP_P)

time: 67.4 us -> 67.1 us (level)
    gather x2 -> x0, local copies, waits for them, and re-layouts: 0.71 us -> none  [route_partials(): rows = jnp.where(filled[:, None, None], partial_value[picked], 0.0)]
    unnamed x21 -> x23, local copies, waits for them, and re-layouts: 3.92 us -> 4.14 us
where the time goes in v14:
time: 67.1 us; the launch traced here: 66.7 us
  starting transfers between devices  28.3 us (42%)
  waiting for transfers between devices  14.5 us (22%)
  local copies, waits for them, and re-layouts  9.25 us (14%)
  matrix products  6.6 us (10%)
  other arithmetic  3.8 us (6%)
  Pallas kernels  3.1 us (5%)
  between operations  1.09 us (2%)
    all_to_all x1, starting transfers between devices, on_device(): lax.all_to_all(packed, 'tile', split_axis=0, concat_axis=0, tiled=True)  11.8 us
    all_to_all x1, waiting for transfers between devices, on_device(): lax.all_to_all(packed, 'tile', split_axis=0, concat_axis=0, tiled=True)  8.66 us
    ppermute x1, starting transfers between devices, route_partials(): lax.ppermute(messages[2], 'tile', [(i, (i + 1) % tile_count) for i in dev...  5.8 us
    all_to_all x1, starting transfers between devices, route_partials(): lax.all_to_all(chunks, 'sub', split_axis=0, concat_axis=0, tiled=True)  5.13 us
    dot_general x1, matrix products, on_device(): jnp.einsum('fpk,pkl->pfl', picked, weights, preferred_element_type=jnp.fl...  4.42 us
    unnamed x23, local copies, waits for them, and re-layouts  4.14 us
    pallas_call x1, Pallas kernels, soil_response(): pl.pallas_call(response_kernel, grid=(grid,), in_specs=[stack, stack], ou...  3.1 us
    ppermute x1, waiting for transfers between devices, route_partials(): lax.ppermute(messages[0], 'tile', [(i, (i - 1) % tile_count) for i in dev...  2.56 us
  transfers between devices with their start and end apart: 6, of which 4 were waited for; matrix products, arithmetic and copies ran while one was open for 10% of the time, Pallas kernels for 5%

profile of v14, /device:TPU:1, one launch (start us, length us, event | category | flops | bytes accessed | tf_op | source)
XLA Modules:
  0.0 66.7 jit_solution(11711504224896484113)
XLA Ops:
  0.6 0.7 %copy.38 = f32[6,8,128]{2,0,1:T(8,128)S(1)} copy(f32[6,8,128]{2,1,0:T(8,128)} %param.8) | data formatting | bytes 49152 | tf_op args[0]
  1.4 2.1 %collective-permute-start.1 = (f32[6,1,128]{2,0,1:T(8,128)S(1)}, f32[6,1,128]{2,0,1:T(8,128)S(1)}, u32[]{:S(2)}, u32[]{:S(2)}) collective-permute-start(f32[6,1,128]{2,0,1:T(8,128)S(1)} %slice.175), channel_id=1, source_target_pairs={{0,1},{1,2},{2,3},{3,4},{4,5},{5,6},{6,7},{7,8},{8,9},{9,10},{10,1... | collective-permute-start | bytes 9224 | tf_op jit(solution)/shard_map/ppermute | solution.py:225
  3.5 1.9 %collective-permute-start = (f32[6,1,128]{2,0,1:T(8,128)S(1)}, f32[6,1,128]{2,0,1:T(8,128)S(1)}, u32[]{:S(2)}, u32[]{:S(2)}) collective-permute-start(f32[6,1,128]{2,0,1:T(8,128)S(1)} %slice.174), channel_id=1, source_target_pairs={{1,0},{2,1},{3,2},{4,3},{5,4},{6,5},{7,6},{8,7},{9,8},{10,9},{11,1... | collective-permute-start | bytes 9224 | tf_op jit(solution)/shard_map/ppermute | solution.py:228
  5.5 0.1 fusion.21
  5.5 0.1 fusion.19
  5.6 0.8 %pad_add_fusion = s32[104]{0:T(128)S(1)} fusion(s32[64]{0:T(128)} %param.15, s32[20]{0:T(128)} %param.10, s32[20]{0:T(128)} %param.9), kind=kLoop, calls=%fused_computation.104 | loop fusion | flops 208 | bytes 832 | tf_op jit(solution)/shard_map/concatenate | solution.py:218
  6.5 0.1 compare_select_fusion.3
  6.7 0.2 select_reduce_fusion.3
  6.9 0.1 select_reduce_fusion.2
  7.0 0.8 %gather_fusion.1 = s32[48]{0:T(128)S(1)} fusion(s32[20]{0:T(128)S(1)} %get-tuple-element.32, s32[1024]{0:T(1024)S(1)} %pad_clamp_fusion), kind=kCustom, calls=%fused_computation.1 | custom fusion | bytes 576 | tf_op jit(solution)/shard_map/gather | solution.py:175
  7.9 0.1 reduce_window_sum.23
  8.0 0.2 select_reduce_fusion.1
  8.4 0.1 concatenate.35
  8.5 0.6 gather_fusion
  9.1 4.4 %fusion.1 = f32[20,6,512]{2,1,0:T(8,128)S(1)} fusion(bf16[20,384,512]{2,1,0:T(8,128)(2,1)} %bitcast.64, bf16[20,6,384]{2,1,0:T(8,128)(2,1)S(1)} %gather_fusion), kind=kOutput, calls=%fused_computation.9 | convolution fusion | flops 47185920 | bytes 8202240 | tf_op jit(solution)/shard_map/fpk,pkl->pfl/dot_general | solution.py:235
  13.6 0.2 copy.43
  13.8 0.4 fusion.35
  14.2 0.1 reshape_reshape.3
  14.3 0.9 %maximum_maximum_fusion = f32[4,80,512]{2,1,0:T(8,128)} fusion(f32[1,8,512]{2,1,0:T(8,128)S(1)} %stack_reshape.15, f32[1,8,512]{2,1,0:T(8,128)S(1)} %stack_reshape.14, f32[1,8,512]{2,1,0:T(8,128)S(1)} %stack_reshape.13, f32[1,8,512]{2,1,0:T(8,128)S(1)} %stack_reshape.12, f32[4,72,512]{2,1,0:T(8,128)S(1)} %reshape_reshape.3), kind=kLoop, calls=%fused_computation.3 | loop fusion | flops 655360 | bytes 1310720 | tf_op jit(solution)/shard_map/concatenate | solution.py:178
  15.2 5.1 %all-to-all-start = ((f32[4,80,512]{2,1,0:T(8,128)}), f32[4,80,512]{2,1,0:T(8,128)S(1)}, u32[]{:S(2)}, u32[]{:S(2)}) async-start(f32[4,80,512]{2,1,0:T(8,128)} %maximum_maximum_fusion), calls=%async_computation | async-start | bytes 1310720 | tf_op jit(solution)/shard_map/all_to_all | solution.py:185
  20.4 0.1 select_reduce_fusion
  20.6 0.1 convert_element_type.52
  20.7 0.1 copy.45
  20.8 0.9 %slice.191.cond_ref = f32[20,64,128]{2,1,0:T(8,128)} slice(f32[24,64,128]{2,1,0:T(8,128)S(1)} %bitcast.66), slice={[0:20], [0:64], [0:128]} | slice | bytes 1310720 | tf_op jit(solution)/shard_map/reshape | solution.py:242
  21.8 0.1 copy.46
  21.9 0.9 %slice.192.moist_ref = f32[20,64,128]{2,1,0:T(8,128)} slice(f32[24,64,128]{2,1,0:T(8,128)S(1)} %bitcast.67), slice={[0:20], [0:64], [0:128]} | slice | bytes 1310720 | tf_op jit(solution)/shard_map/reshape | solution.py:242
  22.8 3.1 %shard_map.111 = (f32[20,64,128]{2,1,0:T(8,128)}, f32[20,64,128]{2,1,0:T(8,128)}, f32[64,128]{1,0:T(8,128)}, f32[64,128]{1,0:T(8,128)}) custom-call(f32[20,64,128]{2,1,0:T(8,128)} %slice.191.cond_ref, f32[20,64,128]{2,1,0:T(8,128)} %slice.192.moist_ref), custom_call_target="tpu_custom_call" | custom-call | tf_op jit(solution)/shard_map/pallas_call | solution.py:128
  25.9 2.1 %all-to-all-done = f32[4,80,512]{2,1,0:T(8,128)S(1)} async-done(((f32[4,80,512]{2,1,0:T(8,128)}), f32[4,80,512]{2,1,0:T(8,128)S(1)}, u32[]{:S(2)}, u32[]{:S(2)}) %all-to-all-start) | async-done | bytes 655392 | tf_op jit(solution)/shard_map/all_to_all | solution.py:185
  28.1 0.1 reshape.144
  28.2 0.1 reshape.141
  28.3 0.1 reshape.137
  28.5 5.8 %collective-permute-start.3 = (f32[104,512]{1,0:T(8,128)S(1)}, f32[104,512]{1,0:T(8,128)S(1)}, u32[]{:S(2)}, u32[]{:S(2)}) collective-permute-start(f32[104,512]{1,0:T(8,128)S(1)} %pad_maximum_fusion.2), channel_id=1, source_target_pairs={{0,4},{4,8},{8,12},{12,16},{16,20},{20,24},{24,28},{28,32},{32,36}... | collective-permute-start | bytes 638984 | tf_op jit(solution)/shard_map/ppermute | solution.py:198
  34.3 1.6 %collective-permute-start.2 = (f32[104,512]{1,0:T(8,128)S(1)}, f32[104,512]{1,0:T(8,128)S(1)}, u32[]{:S(2)}, u32[]{:S(2)}) collective-permute-start(f32[104,512]{1,0:T(8,128)S(1)} %pad_maximum_fusion.1), channel_id=1, source_target_pairs={{0,252},{4,0},{8,4},{12,8},{16,12},{20,16},{24,20},{28,24},{32,28}... | collective-permute-start | bytes 638984 | tf_op jit(solution)/shard_map/ppermute | solution.py:196
  35.8 1.2 %collective-permute-done.3 = f32[104,512]{1,0:T(8,128)S(1)} collective-permute-done((f32[104,512]{1,0:T(8,128)S(1)}, f32[104,512]{1,0:T(8,128)S(1)}, u32[]{:S(2)}, u32[]{:S(2)}) %collective-permute-start.3) | collective-permute-done | bytes 213024 | tf_op jit(solution)/shard_map/ppermute | solution.py:198
  37.1 2.6 %collective-permute-done.2 = f32[104,512]{1,0:T(8,128)S(1)} collective-permute-done((f32[104,512]{1,0:T(8,128)S(1)}, f32[104,512]{1,0:T(8,128)S(1)}, u32[]{:S(2)}, u32[]{:S(2)}) %collective-permute-start.2) | collective-permute-done | bytes 213024 | tf_op jit(solution)/shard_map/ppermute | solution.py:196
  39.7 0.1 reshape.143
  39.8 0.1 pad_maximum_fusion.5
  39.9 0.6 convolution_bitcast_fusion
  40.7 0.7 %copy.44 = bf16[1,6,16,512]{3,1,2,0:T(8,128)(2,1)} copy(bf16[1,6,16,512]{3,2,1,0:T(8,128)(2,1)S(1)} %convert_bitcast_fusion) | data formatting | bytes 196608
  41.4 1.1 %fusion.24 = f32[128,128]{1,0:T(8,128)S(1)} fusion(f32[64,128]{1,0:T(8,128)} %get-tuple-element.10, f32[64,128]{1,0:T(8,128)S(1)} %fusion.6, f32[64,128]{1,0:T(8,128)} %get-tuple-element.11, f32[8192]{0:T(1024)S(1)} %bitcast.82, s32[8192]{0:T(1024)S(1)} %copy-done.4, f32[8192]{0:T(1024)S(1)} %bitcast.80, s32[64]{0:T(128)S(1)} %get-tuple-element.40), kind=kOutput, calls=%fused_computation.47 | convolution fusion | flops 12713984 | bytes 262400 | tf_op jit(solution)/shard_map/dot_general | solution.py:260
  42.6 0.7 %all_to_all.12 = f32[64,1,384]{2,1,0:T(1,128)} reshape(f32[64,384]{1,0:T(8,128)S(1)} %select_maximum_fusion) | data formatting | bytes 196608 | tf_op jit(solution)/shard_map/all_to_all | solution.py:269
  43.3 11.8 %all-to-all-start.1 = ((f32[64,1,384]{2,1,0:T(1,128)}), f32[64,1,384]{2,1,0:T(1,128)S(1)}, u32[]{:S(2)}, u32[]{:S(2)}) async-start(f32[64,1,384]{2,1,0:T(1,128)} %all_to_all.12), calls=%async_computation.1 | async-start | bytes 196608 | tf_op jit(solution)/shard_map/all_to_all | solution.py:269
  55.1 0.1 multiply_add_fusion
  55.2 1.3 %copy.51 = f32[3,8,64,128]{3,1,2,0:T(8,128)} copy(f32[3,8,64,128]{3,2,1,0:T(8,128)S(1)} %bitcast.65) | data formatting | bytes 1572864
  56.6 8.7 %all-to-all-done.1 = f32[64,1,384]{2,1,0:T(1,128)S(1)} async-done(((f32[64,1,384]{2,1,0:T(1,128)}), f32[64,1,384]{2,1,0:T(1,128)S(1)}, u32[]{:S(2)}, u32[]{:S(2)}) %all-to-all-start.1) | async-done | bytes 98336 | tf_op jit(solution)/shard_map/all_to_all | solution.py:269
  65.2 0.1 copy.41
  65.4 0.6 fusion.45
  66.0 0.7 %copy.42 = f32[1,1,64,2,128]{4,3,2,1,0:T(2,128)} copy(f32[1,1,64,2,128]{2,4,3,1,0:T(8,128)S(1)} %bitcast.78) | data formatting | bytes 131072
  (67 shorter events, 1.1 us)
Async XLA Ops:
  1.4 7.0 %collective-permute-start.1 = (f32[6,1,128]{2,0,1:T(8,128)S(1)}, f32[6,1,128]{2,0,1:T(8,128)S(1)}, u32[]{:S(2)}, u32[]{:S(2)}) collective-permute-start(f32[6,1,128]{2,0,1:T(8,128)S(1)} %slice.175), channel_id=1, source_target_pairs={{0,1},{1,2},{2,3},{3,4},{4,5},{5,6},{6,7},{7,8},{8,9},{9,10},{10,1... | collective-permute-start | bytes 9224 | tf_op jit(solution)/shard_map/ppermute | solution.py:225
  3.5 4.9 %collective-permute-start = (f32[6,1,128]{2,0,1:T(8,128)S(1)}, f32[6,1,128]{2,0,1:T(8,128)S(1)}, u32[]{:S(2)}, u32[]{:S(2)}) collective-permute-start(f32[6,1,128]{2,0,1:T(8,128)S(1)} %slice.174), channel_id=1, source_target_pairs={{1,0},{2,1},{3,2},{4,3},{5,4},{6,5},{7,6},{8,7},{9,8},{10,9},{11,1... | collective-permute-start | bytes 9224 | tf_op jit(solution)/shard_map/ppermute | solution.py:228
  9.1 11.6 %copy-start = (f32[20,8192]{1,0:T(8,128)S(1)}, f32[20,8192]{1,0:T(8,128)}, u32[]{:S(2)}) copy-start(f32[20,8192]{1,0:T(8,128)} %param.13) | copy-start | bytes 1966084
  13.5 8.2 %copy-start.1 = (f32[20,8192]{1,0:T(8,128)S(1)}, f32[20,8192]{1,0:T(8,128)}, u32[]{:S(2)}) copy-start(f32[20,8192]{1,0:T(8,128)} %param.14) | copy-start | bytes 1966084
  15.2 26.2 %copy-start.4 = (s32[8192]{0:T(1024)S(1)}, s32[8192]{0:T(1024)}, u32[]{:S(2)}) copy-start(s32[8192]{0:T(1024)} %param.12) | copy-start | bytes 98308
  15.2 12.8 %all-to-all-start = ((f32[4,80,512]{2,1,0:T(8,128)}), f32[4,80,512]{2,1,0:T(8,128)S(1)}, u32[]{:S(2)}, u32[]{:S(2)}) async-start(f32[4,80,512]{2,1,0:T(8,128)} %maximum_maximum_fusion), calls=%async_computation | async-start | bytes 1310720 | tf_op jit(solution)/shard_map/all_to_all | solution.py:185
  25.9 29.2 %copy-start.2 = (f32[20,64,128]{2,1,0:T(8,128)S(1)}, f32[20,64,128]{2,1,0:T(8,128)}, u32[]{:S(2)}) copy-start(f32[20,64,128]{2,1,0:T(8,128)} %get-tuple-element.8) | copy-start | bytes 1966084
  25.9 29.2 %copy-start.3 = (f32[20,64,128]{2,1,0:T(8,128)S(1)}, f32[20,64,128]{2,1,0:T(8,128)}, u32[]{:S(2)}) copy-start(f32[20,64,128]{2,1,0:T(8,128)} %get-tuple-element.9) | copy-start | bytes 1966084
  28.5 8.6 %collective-permute-start.3 = (f32[104,512]{1,0:T(8,128)S(1)}, f32[104,512]{1,0:T(8,128)S(1)}, u32[]{:S(2)}, u32[]{:S(2)}) collective-permute-start(f32[104,512]{1,0:T(8,128)S(1)} %pad_maximum_fusion.2), channel_id=1, source_target_pairs={{0,4},{4,8},{8,12},{12,16},{16,20},{20,24},{24,28},{28,32},{32,36}... | collective-permute-start | bytes 638984 | tf_op jit(solution)/shard_map/ppermute | solution.py:198
  34.3 5.3 %collective-permute-start.2 = (f32[104,512]{1,0:T(8,128)S(1)}, f32[104,512]{1,0:T(8,128)S(1)}, u32[]{:S(2)}, u32[]{:S(2)}) collective-permute-start(f32[104,512]{1,0:T(8,128)S(1)} %pad_maximum_fusion.1), channel_id=1, source_target_pairs={{0,252},{4,0},{8,4},{12,8},{16,12},{20,16},{24,20},{28,24},{32,28}... | collective-permute-start | bytes 638984 | tf_op jit(solution)/shard_map/ppermute | solution.py:196
  43.3 21.9 %all-to-all-start.1 = ((f32[64,1,384]{2,1,0:T(1,128)}), f32[64,1,384]{2,1,0:T(1,128)S(1)}, u32[]{:S(2)}, u32[]{:S(2)}) async-start(f32[64,1,384]{2,1,0:T(1,128)} %all_to_all.12), calls=%async_computation.1 | async-start | bytes 196608 | tf_op jit(solution)/shard_map/all_to_all | solution.py:269
